TPU v7x, 256 devices: a whole 4x4x8 slice. The times are simulated.
256 devices in a mesh: rad: 8 (over y, z_lo), az: 32 (over x, z_hi, core).
Axes of the slice: x: 4, y: 4, z: 8 (z_hi: 4, z_lo: 2; z = z_hi * 2 + z_lo), core: 2. Of those that a mesh axis runs over, the one named last changes fastest.
Arguments:
- dust_density: float32 [512, 512, 128], P('rad', 'az'), may hold values from 0.05 to 1
- dust_velocity: float32 [512, 512, 2, 128], P('rad', 'az'), may hold values from -6 to 6
- gas_density: float32 [1024, 2048], P('rad', 'az'), may hold values from 0.5 to 2
- gas_velocity: float32 [1024, 2, 2048], P('rad', None, 'az'), may hold values from -6 to 6
- kernel: float32 [128, 128], replicated, may hold values from 0.0005 to 0.005
- grain_param: float32 [128], replicated, may hold values from 0.1 to 10
- cycle_shifts: int32 [512], P('rad'), may hold values from 0 to 511
- fragment_bins: int32 [128, 128], replicated, may hold values from 0 to 127
- gas_map: int32 [512], P('rad'), may hold values from 0 to 1023, as said below
Outputs:
- dust_density_out: float32 [512, 512, 128], P('rad', 'az')
- dust_velocity_out: float32 [512, 512, 2, 128], P('rad', 'az')
- gas_velocity_out: float32 [1024, 2, 2048], P('rad', None, 'az')
Inputs may be any that keep to these rules, and one draw needn't show every extreme that they name: gas_map never decreases along the dust cycles; the first dust cycle maps to gas cycle 0 and the last to gas cycle 1024 - 1. `gas_map`: the dust cycles of index i of rad map into gas cycles of index i - 1 or i of rad, and each index after the first has a dust cycle in the gas cycles of index i - 1.
All inputs are finite; a program needn't handle non-finite values.
Results may differ from a plain program's by a relative error of at most 0.000064.
Values sent between devices are 32-bit elements; how exact they have to be, the bound alone decides.
No kernel may reach another device: no remote copies, remote signals or barrier semaphores. Data moves between devices by JAX's collectives and lax.ppermute only.
A program may use at most 64 MiB of HBM per device.

v0:
```python
import math

import jax
import jax.numpy as jnp
from jax import lax
from jax.sharding import PartitionSpec as P


def from_behind(block, axis, distance):
    devices = range(lax.axis_size(axis))
    route = [((i - distance) % len(devices), i) for i in devices]
    return lax.ppermute(block, axis, route)


def shifted(block, axis, distance):
    devices = range(lax.axis_size(axis))
    route = [(i - distance, i) for i in devices if i - distance in devices]
    return lax.ppermute(block, axis, route)


def body(
    dust_density,
    dust_velocity,
    gas_density,
    gas_velocity,
    kernel,
    grain_param,
    cycle_shifts,
    fragment_bins,
    gas_map,
):
    cycles, cells, bins = dust_density.shape
    gas_cycles = gas_density.shape[0]
    state = jnp.concatenate([dust_density[:, :, None, :], dust_velocity], axis=2)
    az_count = lax.axis_size("az")
    quotient = cycle_shifts // cells
    remain = cycle_shifts % cells
    for level in range(az_count.bit_length() - 1):
        moved = from_behind(state, "az", 1 << level)
        taken = quotient // (1 << level) % 2 == 1
        state = jnp.where(taken[:, None, None, None], moved, state)
    before = from_behind(state, "az", 1)
    joined = jnp.concatenate([before, state], axis=1)
    position = cells + jnp.arange(cells, dtype=jnp.int32)[None, :] - remain[:, None]
    state = jnp.take_along_axis(joined, position[:, :, None, None], axis=1)
    moved_density = state[:, :, 0, :]
    moved_velocity = state[:, :, 1:, :]
    onehot = (
        fragment_bins.reshape(-1)[:, None] == jnp.arange(bins, dtype=jnp.int32)[None, :]
    ).astype(jnp.float32)
    table = kernel.reshape(-1)[:, None] * onehot
    total_cells = cycles * cells
    block = math.gcd(total_cells, 64)

    def coag_block(dens):
        pairs = (dens[:, :, None] * dens[:, None, :]).reshape(dens.shape[0], -1)
        gain = jnp.dot(pairs, table, precision=lax.Precision.HIGHEST)
        loss = dens * jnp.dot(dens, kernel.T, precision=lax.Precision.HIGHEST)
        return dens + gain - loss

    coag_density = lax.map(
        coag_block, moved_density.reshape(total_cells // block, block, bins)
    ).reshape(cycles, cells, bins)
    coarse_density = gas_density.reshape(gas_cycles, cells, 4).mean(-1)
    coarse_velocity = (
        gas_velocity.reshape(gas_cycles, 2, cells, 4).mean(-1).reshape(gas_cycles, 2 * cells)
    )
    prev_density, prev_velocity = shifted((coarse_density, coarse_velocity), "rad", 1)
    near_density = jnp.concatenate([prev_density, coarse_density], axis=0)
    near_velocity = jnp.concatenate([prev_velocity, coarse_velocity], axis=0)
    first_row = (lax.axis_index("rad") - 1) * gas_cycles
    near_rows = first_row + jnp.arange(2 * gas_cycles, dtype=jnp.int32)
    select = (gas_map[:, None] == near_rows[None, :]).astype(jnp.float32)
    rho_dust = jnp.dot(select, near_density, precision=lax.Precision.HIGHEST)
    u_flat = jnp.dot(select, near_velocity, precision=lax.Precision.HIGHEST)
    u_dust = jnp.transpose(u_flat.reshape(cycles, 2, cells), (0, 2, 1))
    frac = 1.0 - jnp.exp(-rho_dust[:, :, None] / grain_param[None, None, :])
    velocity_out = moved_velocity + (u_dust[:, :, :, None] - moved_velocity) * frac[:, :, None, :]
    momentum = jnp.sum(coag_density[:, :, None, :] * (velocity_out - moved_velocity), axis=3) / bins
    spread = jnp.repeat(jnp.transpose(momentum, (0, 2, 1)), 4, axis=2).reshape(cycles, 8 * cells)
    near_kick = jnp.dot(select.T, spread, precision=lax.Precision.HIGHEST)
    from_next = shifted(near_kick[:gas_cycles], "rad", -1)
    kick = (near_kick[gas_cycles:] + from_next).reshape(gas_cycles, 2, 4 * cells)
    gas_out = gas_velocity - kick / gas_density[:, None, :]
    return (coag_density, velocity_out, gas_out)


def solution(mesh):
    placed = (
        P("rad", "az", None),
        P("rad", "az", None, None),
        P("rad", "az"),
        P("rad", None, "az"),
        P(),
        P(),
        P("rad"),
        P(),
        P("rad"),
    )
    return jax.shard_map(
        body,
        mesh=mesh,
        in_specs=placed,
        out_specs=(P("rad", "az", None), P("rad", "az", None, None), P("rad", None, "az")),
        check_vma=False,
    )
```

profile of v0, /device:TPU:8, one launch (start us, length us, event | category | flops | bytes accessed | tf_op | source)
XLA Modules:
  0.0 710.8 jit_solution(9347872942406076190)
XLA Ops:
  3.7 31.5 %collective-permute-done = f32[64,16,3,128]{3,1,2,0:T(8,128)S(1)} collective-permute-done((f32[64,16,3,128]{3,1,2,0:T(8,128)S(1)}, f32[64,16,3,128]{3,1,2,0:T(8,128)S(1)}, u32[]{:S(2)}, u32[]{:S(2)}) %collective-permute-start) | collective-permute-done | bytes 1572896 | tf_op jit(solution)/shard_map/ppermute | solution.py:12
  37.1 65.3 %collective-permute-done.1 = f32[64,16,3,128]{3,1,2,0:T(8,128)S(1)} collective-permute-done((f32[64,16,3,128]{3,1,2,0:T(8,128)S(1)}, f32[64,16,3,128]{3,1,2,0:T(8,128)S(1)}, u32[]{:S(2)}, u32[]{:S(2)}) %collective-permute-start.1) | collective-permute-done | bytes 1572896 | tf_op jit(solution)/shard_map/ppermute | solution.py:12
  103.7 19.0 %collective-permute-start.2 = (f32[64,16,3,128]{3,1,2,0:T(8,128)S(1)}, f32[64,16,3,128]{3,1,2,0:T(8,128)S(1)}, u32[]{:S(2)}, u32[]{:S(2)}) collective-permute-start(f32[64,16,3,128]{3,1,2,0:T(8,128)S(1)} %copy.26), channel_id=1, source_target_pairs={{28,0},{29,1},{30,2},{31,3},{0,4},{1,5},{2,6},{3,7},{4,8},{5,9},{6... | collective-permute-start | bytes 4718600 | tf_op jit(solution)/shard_map/ppermute | solution.py:12
  122.7 66.4 %collective-permute-done.2 = f32[64,16,3,128]{3,1,2,0:T(8,128)S(1)} collective-permute-done((f32[64,16,3,128]{3,1,2,0:T(8,128)S(1)}, f32[64,16,3,128]{3,1,2,0:T(8,128)S(1)}, u32[]{:S(2)}, u32[]{:S(2)}) %collective-permute-start.2) | collective-permute-done | bytes 1572896 | tf_op jit(solution)/shard_map/ppermute | solution.py:12
  190.5 37.0 %collective-permute-done.3 = f32[64,16,3,128]{3,1,2,0:T(8,128)S(1)} collective-permute-done((f32[64,16,3,128]{3,1,2,0:T(8,128)S(1)}, f32[64,16,3,128]{3,1,2,0:T(8,128)S(1)}, u32[]{:S(2)}, u32[]{:S(2)}) %collective-permute-start.3) | collective-permute-done | bytes 1572896 | tf_op jit(solution)/shard_map/ppermute | solution.py:12
  229.9 3.3 collective-permute-start.6
  233.3 3.7 collective-permute-start.7
  237.0 29.5 %collective-permute-done.4 = f32[64,16,3,128]{3,1,2,0:T(8,128)} collective-permute-done((f32[64,16,3,128]{3,1,2,0:T(8,128)}, f32[64,16,3,128]{3,1,2,0:T(8,128)}, u32[]{:S(2)}, u32[]{:S(2)}) %collective-permute-start.4) | collective-permute-done | bytes 1572896 | tf_op jit(solution)/shard_map/ppermute | solution.py:12
  266.5 2.5 copy_select_fusion
  273.1 34.1 %collective-permute-done.5 = f32[64,16,3,128]{3,1,2,0:T(8,128)} collective-permute-done((f32[64,16,3,128]{3,1,2,0:T(8,128)}, f32[64,16,3,128]{3,1,2,0:T(8,128)}, u32[]{:S(2)}, u32[]{:S(2)}) %collective-permute-start.5) | collective-permute-done | bytes 1572896 | tf_op jit(solution)/shard_map/ppermute | solution.py:12
  309.5 3.5 pad_maximum_fusion
  313.0 6.8 gather_fusion
  323.7 370.8 %while.11 = (s32[]{:T(128)}, f32[16,64,128]{2,1,0:T(8,128)}, f32[16,64,128]{2,1,0:T(8,128)}, f32[128,128]{1,0:T(8,128)S(1)}, s32[16384]{0:T(1024)S(1)}, /*index=5*/f32[16384]{0:T(1024)S(1)}, s32[]{:T(128)}) while((s32[]{:T(128)}, f32[16,64,128]{2,1,0:T(8,128)}, f32[16,64,128]{2,1,0:T(8,128)}, f32[128,128]{1,0:T(8,128)S(1)}, ...), condition=%wide.region_1.2_spmd.clone, body=%wide.region_0.1_spmd.clone.sunk | while | flops 1628463104 | bytes 8880721 | solution.py:61
  325.8 20.4 %fusion.66 = f32[64,128]{1,0:T(8,128)S(1)} fusion(f32[64,128]{1,0:T(8,128)S(1)} %dynamic-slice_bitcast_fusion.2, f32[16384]{0:T(1024)S(1)} %get-tuple-element.123, s32[16384]{0:T(1024)S(1)} %get-tuple-element.122, f32[8,8,128,128]{3,2,1,0:T(8,128)S(1)} %bitcast.45), kind=kOutput, calls=%fused_computation.15.clone.1 | convolution fusion | flops 1614815232 | bytes 4390912 | tf_op jit(solution)/shard_map/while/body/eval_jaxpr/dot_general | solution.py:57
  348.9 20.4 %fusion.66 = f32[64,128]{1,0:T(8,128)S(1)} fusion(f32[64,128]{1,0:T(8,128)S(1)} %dynamic-slice_bitcast_fusion.2, f32[16384]{0:T(1024)S(1)} %get-tuple-element.123, s32[16384]{0:T(1024)S(1)} %get-tuple-element.122, f32[8,8,128,128]{3,2,1,0:T(8,128)S(1)} %bitcast.45), kind=kOutput, calls=%fused_computation.15.clone.1 | convolution fusion | flops 1614815232 | bytes 4390912 | tf_op jit(solution)/shard_map/while/body/eval_jaxpr/dot_general | solution.py:57
  372.1 20.4 %fusion.66 = f32[64,128]{1,0:T(8,128)S(1)} fusion(f32[64,128]{1,0:T(8,128)S(1)} %dynamic-slice_bitcast_fusion.2, f32[16384]{0:T(1024)S(1)} %get-tuple-element.123, s32[16384]{0:T(1024)S(1)} %get-tuple-element.122, f32[8,8,128,128]{3,2,1,0:T(8,128)S(1)} %bitcast.45), kind=kOutput, calls=%fused_computation.15.clone.1 | convolution fusion | flops 1614815232 | bytes 4390912 | tf_op jit(solution)/shard_map/while/body/eval_jaxpr/dot_general | solution.py:57
  395.3 20.4 %fusion.66 = f32[64,128]{1,0:T(8,128)S(1)} fusion(f32[64,128]{1,0:T(8,128)S(1)} %dynamic-slice_bitcast_fusion.2, f32[16384]{0:T(1024)S(1)} %get-tuple-element.123, s32[16384]{0:T(1024)S(1)} %get-tuple-element.122, f32[8,8,128,128]{3,2,1,0:T(8,128)S(1)} %bitcast.45), kind=kOutput, calls=%fused_computation.15.clone.1 | convolution fusion | flops 1614815232 | bytes 4390912 | tf_op jit(solution)/shard_map/while/body/eval_jaxpr/dot_general | solution.py:57
  418.4 20.4 %fusion.66 = f32[64,128]{1,0:T(8,128)S(1)} fusion(f32[64,128]{1,0:T(8,128)S(1)} %dynamic-slice_bitcast_fusion.2, f32[16384]{0:T(1024)S(1)} %get-tuple-element.123, s32[16384]{0:T(1024)S(1)} %get-tuple-element.122, f32[8,8,128,128]{3,2,1,0:T(8,128)S(1)} %bitcast.45), kind=kOutput, calls=%fused_computation.15.clone.1 | convolution fusion | flops 1614815232 | bytes 4390912 | tf_op jit(solution)/shard_map/while/body/eval_jaxpr/dot_general | solution.py:57
  441.6 20.4 %fusion.66 = f32[64,128]{1,0:T(8,128)S(1)} fusion(f32[64,128]{1,0:T(8,128)S(1)} %dynamic-slice_bitcast_fusion.2, f32[16384]{0:T(1024)S(1)} %get-tuple-element.123, s32[16384]{0:T(1024)S(1)} %get-tuple-element.122, f32[8,8,128,128]{3,2,1,0:T(8,128)S(1)} %bitcast.45), kind=kOutput, calls=%fused_computation.15.clone.1 | convolution fusion | flops 1614815232 | bytes 4390912 | tf_op jit(solution)/shard_map/while/body/eval_jaxpr/dot_general | solution.py:57
  464.8 20.4 %fusion.66 = f32[64,128]{1,0:T(8,128)S(1)} fusion(f32[64,128]{1,0:T(8,128)S(1)} %dynamic-slice_bitcast_fusion.2, f32[16384]{0:T(1024)S(1)} %get-tuple-element.123, s32[16384]{0:T(1024)S(1)} %get-tuple-element.122, f32[8,8,128,128]{3,2,1,0:T(8,128)S(1)} %bitcast.45), kind=kOutput, calls=%fused_computation.15.clone.1 | convolution fusion | flops 1614815232 | bytes 4390912 | tf_op jit(solution)/shard_map/while/body/eval_jaxpr/dot_general | solution.py:57
  487.9 20.4 %fusion.66 = f32[64,128]{1,0:T(8,128)S(1)} fusion(f32[64,128]{1,0:T(8,128)S(1)} %dynamic-slice_bitcast_fusion.2, f32[16384]{0:T(1024)S(1)} %get-tuple-element.123, s32[16384]{0:T(1024)S(1)} %get-tuple-element.122, f32[8,8,128,128]{3,2,1,0:T(8,128)S(1)} %bitcast.45), kind=kOutput, calls=%fused_computation.15.clone.1 | convolution fusion | flops 1614815232 | bytes 4390912 | tf_op jit(solution)/shard_map/while/body/eval_jaxpr/dot_general | solution.py:57
  511.1 20.4 %fusion.66 = f32[64,128]{1,0:T(8,128)S(1)} fusion(f32[64,128]{1,0:T(8,128)S(1)} %dynamic-slice_bitcast_fusion.2, f32[16384]{0:T(1024)S(1)} %get-tuple-element.123, s32[16384]{0:T(1024)S(1)} %get-tuple-element.122, f32[8,8,128,128]{3,2,1,0:T(8,128)S(1)} %bitcast.45), kind=kOutput, calls=%fused_computation.15.clone.1 | convolution fusion | flops 1614815232 | bytes 4390912 | tf_op jit(solution)/shard_map/while/body/eval_jaxpr/dot_general | solution.py:57
  534.3 20.4 %fusion.66 = f32[64,128]{1,0:T(8,128)S(1)} fusion(f32[64,128]{1,0:T(8,128)S(1)} %dynamic-slice_bitcast_fusion.2, f32[16384]{0:T(1024)S(1)} %get-tuple-element.123, s32[16384]{0:T(1024)S(1)} %get-tuple-element.122, f32[8,8,128,128]{3,2,1,0:T(8,128)S(1)} %bitcast.45), kind=kOutput, calls=%fused_computation.15.clone.1 | convolution fusion | flops 1614815232 | bytes 4390912 | tf_op jit(solution)/shard_map/while/body/eval_jaxpr/dot_general | solution.py:57
  557.4 20.4 %fusion.66 = f32[64,128]{1,0:T(8,128)S(1)} fusion(f32[64,128]{1,0:T(8,128)S(1)} %dynamic-slice_bitcast_fusion.2, f32[16384]{0:T(1024)S(1)} %get-tuple-element.123, s32[16384]{0:T(1024)S(1)} %get-tuple-element.122, f32[8,8,128,128]{3,2,1,0:T(8,128)S(1)} %bitcast.45), kind=kOutput, calls=%fused_computation.15.clone.1 | convolution fusion | flops 1614815232 | bytes 4390912 | tf_op jit(solution)/shard_map/while/body/eval_jaxpr/dot_general | solution.py:57
  580.6 20.4 %fusion.66 = f32[64,128]{1,0:T(8,128)S(1)} fusion(f32[64,128]{1,0:T(8,128)S(1)} %dynamic-slice_bitcast_fusion.2, f32[16384]{0:T(1024)S(1)} %get-tuple-element.123, s32[16384]{0:T(1024)S(1)} %get-tuple-element.122, f32[8,8,128,128]{3,2,1,0:T(8,128)S(1)} %bitcast.45), kind=kOutput, calls=%fused_computation.15.clone.1 | convolution fusion | flops 1614815232 | bytes 4390912 | tf_op jit(solution)/shard_map/while/body/eval_jaxpr/dot_general | solution.py:57
  603.8 20.4 %fusion.66 = f32[64,128]{1,0:T(8,128)S(1)} fusion(f32[64,128]{1,0:T(8,128)S(1)} %dynamic-slice_bitcast_fusion.2, f32[16384]{0:T(1024)S(1)} %get-tuple-element.123, s32[16384]{0:T(1024)S(1)} %get-tuple-element.122, f32[8,8,128,128]{3,2,1,0:T(8,128)S(1)} %bitcast.45), kind=kOutput, calls=%fused_computation.15.clone.1 | convolution fusion | flops 1614815232 | bytes 4390912 | tf_op jit(solution)/shard_map/while/body/eval_jaxpr/dot_general | solution.py:57
  626.9 20.4 %fusion.66 = f32[64,128]{1,0:T(8,128)S(1)} fusion(f32[64,128]{1,0:T(8,128)S(1)} %dynamic-slice_bitcast_fusion.2, f32[16384]{0:T(1024)S(1)} %get-tuple-element.123, s32[16384]{0:T(1024)S(1)} %get-tuple-element.122, f32[8,8,128,128]{3,2,1,0:T(8,128)S(1)} %bitcast.45), kind=kOutput, calls=%fused_computation.15.clone.1 | convolution fusion | flops 1614815232 | bytes 4390912 | tf_op jit(solution)/shard_map/while/body/eval_jaxpr/dot_general | solution.py:57
  650.1 20.4 %fusion.66 = f32[64,128]{1,0:T(8,128)S(1)} fusion(f32[64,128]{1,0:T(8,128)S(1)} %dynamic-slice_bitcast_fusion.2, f32[16384]{0:T(1024)S(1)} %get-tuple-element.123, s32[16384]{0:T(1024)S(1)} %get-tuple-element.122, f32[8,8,128,128]{3,2,1,0:T(8,128)S(1)} %bitcast.45), kind=kOutput, calls=%fused_computation.15.clone.1 | convolution fusion | flops 1614815232 | bytes 4390912 | tf_op jit(solution)/shard_map/while/body/eval_jaxpr/dot_general | solution.py:57
  673.3 20.4 %fusion.66 = f32[64,128]{1,0:T(8,128)S(1)} fusion(f32[64,128]{1,0:T(8,128)S(1)} %dynamic-slice_bitcast_fusion.2, f32[16384]{0:T(1024)S(1)} %get-tuple-element.123, s32[16384]{0:T(1024)S(1)} %get-tuple-element.122, f32[8,8,128,128]{3,2,1,0:T(8,128)S(1)} %bitcast.45), kind=kOutput, calls=%fused_computation.15.clone.1 | convolution fusion | flops 1614815232 | bytes 4390912 | tf_op jit(solution)/shard_map/while/body/eval_jaxpr/dot_general | solution.py:57
  694.5 4.3 multiply_reduce_fusion
  699.4 8.3 %collective-permute-start.8 = (f32[128,128]{0,1:T(8,128)S(1)}, f32[128,128]{0,1:T(8,128)S(1)}, u32[]{:S(2)}, u32[]{:S(2)}) collective-permute-start(f32[128,128]{0,1:T(8,128)S(1)} %slice.21), channel_id=1, source_target_pairs={{32,0},{64,32},{96,64},{128,96},{160,128},{192,160},{224,192},{33,... | collective-permute-start | bytes 196616 | tf_op jit(solution)/shard_map/ppermute | solution.py:18
  707.7 2.3 collective-permute-done.8
  (120 shorter events, 65.8 us)
Async XLA Ops:
  2.9 0.7 copy-start.12
  3.0 32.2 %copy-start.4 = (f32[64,16,2,128]{3,2,1,0:T(2,128)S(1)}, f32[64,16,2,128]{3,2,1,0:T(2,128)}, u32[]{:S(2)}) copy-start(f32[64,16,2,128]{3,2,1,0:T(2,128)} %param.12) | copy-start | bytes 3145732
  3.0 32.2 %copy-start.5 = (f32[64,16,128]{2,1,0:T(8,128)S(1)}, f32[64,16,128]{2,1,0:T(8,128)}, u32[]{:S(2)}) copy-start(f32[64,16,128]{2,1,0:T(8,128)} %param.11) | copy-start | bytes 1572868
  3.1 32.0 %collective-permute-start = (f32[64,16,3,128]{3,1,2,0:T(8,128)S(1)}, f32[64,16,3,128]{3,1,2,0:T(8,128)S(1)}, u32[]{:S(2)}, u32[]{:S(2)}) collective-permute-start(f32[64,16,3,128]{3,1,2,0:T(8,128)S(1)} %copy.22), channel_id=1, source_target_pairs={{31,0},{0,1},{1,2},{2,3},{3,4},{4,5},{5,6},{6,7},{7,8},{8,9},{9,10... | collective-permute-start | bytes 4718600 | tf_op jit(solution)/shard_map/ppermute | solution.py:12
  37.1 65.4 %collective-permute-start.1 = (f32[64,16,3,128]{3,1,2,0:T(8,128)S(1)}, f32[64,16,3,128]{3,1,2,0:T(8,128)S(1)}, u32[]{:S(2)}, u32[]{:S(2)}) collective-permute-start(f32[64,16,3,128]{3,1,2,0:T(8,128)S(1)} %copy.24), channel_id=1, source_target_pairs={{30,0},{31,1},{0,2},{1,3},{2,4},{3,5},{4,6},{5,7},{6,8},{7,9},{8,1... | collective-permute-start | bytes 4718600 | tf_op jit(solution)/shard_map/ppermute | solution.py:12
  103.7 85.5 %collective-permute-start.2 = (f32[64,16,3,128]{3,1,2,0:T(8,128)S(1)}, f32[64,16,3,128]{3,1,2,0:T(8,128)S(1)}, u32[]{:S(2)}, u32[]{:S(2)}) collective-permute-start(f32[64,16,3,128]{3,1,2,0:T(8,128)S(1)} %copy.26), channel_id=1, source_target_pairs={{28,0},{29,1},{30,2},{31,3},{0,4},{1,5},{2,6},{3,7},{4,8},{5,9},{6... | collective-permute-start | bytes 4718600 | tf_op jit(solution)/shard_map/ppermute | solution.py:12
  190.4 37.1 %collective-permute-start.3 = (f32[64,16,3,128]{3,1,2,0:T(8,128)S(1)}, f32[64,16,3,128]{3,1,2,0:T(8,128)S(1)}, u32[]{:S(2)}, u32[]{:S(2)}) collective-permute-start(f32[64,16,3,128]{3,1,2,0:T(8,128)S(1)} %copy.28), channel_id=1, source_target_pairs={{24,0},{25,1},{26,2},{27,3},{28,4},{29,5},{30,6},{31,7},{0,8},{1,9... | collective-permute-start | bytes 4718600 | tf_op jit(solution)/shard_map/ppermute | solution.py:12
  228.5 1.3 copy-start.7
  228.5 4.7 copy-start.8
  229.9 36.7 %collective-permute-start.4 = (f32[64,16,3,128]{3,1,2,0:T(8,128)}, f32[64,16,3,128]{3,1,2,0:T(8,128)}, u32[]{:S(2)}, u32[]{:S(2)}) collective-permute-start(f32[64,16,3,128]{3,1,2,0:T(8,128)} %copy.30), channel_id=1, source_target_pairs={{16,0},{17,1},{18,2},{19,3},{20,4},{21,5},{22,6},{23,7},{24,8},{25... | collective-permute-start | bytes 4718600 | tf_op jit(solution)/shard_map/ppermute | solution.py:12
  229.9 42.6 %collective-permute-start.6 = (f32[128,32]{0,1:T(8,128)S(1)}, f32[128,32]{0,1:T(8,128)S(1)}, u32[]{:S(2)}, u32[]{:S(2)}) collective-permute-start(f32[128,32]{0,1:T(8,128)S(1)} %bitcast.58), channel_id=1, source_target_pairs={{0,32},{32,64},{64,96},{96,128},{128,160},{160,192},{192,224},{1,3... | collective-permute-start | bytes 49160 | tf_op jit(solution)/shard_map/ppermute | solution.py:18
  233.3 38.7 %collective-permute-start.7 = (f32[128,16]{0,1:T(8,128)S(1)}, f32[128,16]{0,1:T(8,128)S(1)}, u32[]{:S(2)}, u32[]{:S(2)}) collective-permute-start(f32[128,16]{0,1:T(8,128)S(1)} %broadcast_multiply_fusion.2), channel_id=1, source_target_pairs={{0,32},{32,64},{64,96},{96,128},{128,160},{160,192},{192,224},{1,3... | collective-permute-start | bytes 24584 | tf_op jit(solution)/shard_map/ppermute | solution.py:18
  269.0 1.3 copy-start
  270.4 1.6 copy-start.10
  270.4 1.9 copy-start.9
  271.7 35.5 %collective-permute-start.5 = (f32[64,16,3,128]{3,1,2,0:T(8,128)}, f32[64,16,3,128]{3,1,2,0:T(8,128)}, u32[]{:S(2)}, u32[]{:S(2)}) collective-permute-start(f32[64,16,3,128]{3,1,2,0:T(8,128)} %copy.32), channel_id=1, source_target_pairs={{31,0},{0,1},{1,2},{2,3},{3,4},{4,5},{5,6},{6,7},{7,8},{8,9},{9,10... | collective-permute-start | bytes 4718600 | tf_op jit(solution)/shard_map/ppermute | solution.py:12
  272.7 36.7 %copy-start.1 = (f32[64,16,3,128]{3,2,1,0:T(4,128)S(1)}, f32[64,16,3,128]{3,2,1,0:T(4,128)}, u32[]{:S(2)}) copy-start(f32[64,16,3,128]{3,2,1,0:T(4,128)} %copy-done) | copy-start | bytes 4718596
  319.7 4.0 copy-start.6
  319.8 3.9 copy-start.11
  321.2 1.3 copy-start.2
  323.7 370.8 %copy-start.3 = (f32[64,16,3,128]{3,2,1,0:T(4,128)S(1)}, f32[64,16,3,128]{3,2,1,0:T(4,128)}, u32[]{:S(2)}) copy-start(f32[64,16,3,128]{3,2,1,0:T(4,128)} %copy-done.2) | copy-start | bytes 4718596
  699.4 10.7 %collective-permute-start.8 = (f32[128,128]{0,1:T(8,128)S(1)}, f32[128,128]{0,1:T(8,128)S(1)}, u32[]{:S(2)}, u32[]{:S(2)}) collective-permute-start(f32[128,128]{0,1:T(8,128)S(1)} %slice.21), channel_id=1, source_target_pairs={{32,0},{64,32},{96,64},{128,96},{160,128},{192,160},{224,192},{33,... | collective-permute-start | bytes 196616 | tf_op jit(solution)/shard_map/ppermute | solution.py:18
where the time goes:
time: 713 us; the launch traced here: 711 us
  matrix products  341 us (48%)
  waiting for transfers between devices  266 us (37%)
  other arithmetic  38.5 us (5%)
  starting transfers between devices  34.7 us (5%)
  local copies, waits for them, and re-layouts  29.6 us (4%)
    dot_general x16, matrix products, coag_block(): gain = jnp.dot(pairs, table, precision=lax.Precision.HIGHEST)  326 us
    ppermute x6, waiting for transfers between devices, from_behind(): return lax.ppermute(block, axis, route)  264 us
    ppermute x6, starting transfers between devices, from_behind(): return lax.ppermute(block, axis, route)  19.3 us
    mul x16, other arithmetic, coag_block(): pairs = (dens[:, :, None] * dens[:, None, :]).reshape(dens.shape[0], -1)  18.3 us
    ppermute x3, starting transfers between devices, shifted(): return lax.ppermute(block, axis, route)  15.4 us
  transfers between devices with their start and end apart: 9, of which 7 were waited for; matrix products, arithmetic and copies ran while one was open for 1% of the time, Pallas kernels for 0%

commit v1 on v0

--- a/solution.py
+++ b/solution.py
@@ -4,6 +4,60 @@
 import jax.numpy as jnp
 from jax import lax
 from jax.sharding import PartitionSpec as P
+from jax.experimental import pallas as pl
+from jax.experimental.pallas import tpu as pltpu
+import functools
+
+F32 = jnp.float32
+BF16 = jnp.bfloat16
+
+
+def split(x):
+    hi = x.astype(BF16)
+    lo = (x - hi.astype(F32)).astype(BF16)
+    return hi, lo
+
+
+def dot3(a, b):
+    a_hi, a_lo = a
+    b_hi, b_lo = b
+    d = functools.partial(jnp.dot, preferred_element_type=F32)
+    return d(a_hi, b_hi) + (d(a_hi, b_lo) + d(a_lo, b_hi))
+
+
+def coag_kernel(n_ref, k_ref, f_ref, o_ref, nt_ref, gain_ref):
+    bins = k_ref.shape[0]
+    nt = n_ref[...].T
+    nt_ref[...] = nt
+    n_parts = split(nt)
+    loss = nt * dot3(split(k_ref[...]), n_parts)
+    gain_ref[...] = jnp.zeros_like(gain_ref)
+    rows = lax.broadcasted_iota(jnp.int32, (bins, bins), 0)
+
+    def step(i, carry):
+        table = jnp.where(f_ref[pl.ds(i, 1), :] == rows, k_ref[pl.ds(i, 1), :], 0.0)
+        gain_ref[...] += nt_ref[pl.ds(i, 1), :] * dot3(split(table), n_parts)
+        return carry
+
+    lax.fori_loop(0, bins, step, 0)
+    o_ref[...] = (nt + gain_ref[...] - loss).T
+
+
+def coag(dens, kernel, fragment_bins, block=512):
+    cells, bins = dens.shape
+    block = min(block, cells)
+    return pl.pallas_call(
+        coag_kernel,
+        grid=(cells // block,),
+        in_specs=[
+            pl.BlockSpec((block, bins), lambda c: (c, 0)),
+            pl.BlockSpec((bins, bins), lambda c: (0, 0)),
+            pl.BlockSpec((bins, bins), lambda c: (0, 0)),
+        ],
+        out_specs=pl.BlockSpec((block, bins), lambda c: (c, 0)),
+        out_shape=jax.ShapeDtypeStruct((cells, bins), F32),
+        scratch_shapes=[pltpu.VMEM((bins, block), F32), pltpu.VMEM((bins, block), F32)],
+    )(dens, kernel, fragment_bins)
 
 
 def from_behind(block, axis, distance):
@@ -31,7 +85,8 @@
 ):
     cycles, cells, bins = dust_density.shape
     gas_cycles = gas_density.shape[0]
-    state = jnp.concatenate([dust_density[:, :, None, :], dust_velocity], axis=2)
+    coag_local = coag(dust_density.reshape(cycles * cells, bins), kernel, fragment_bins)
+    state = jnp.concatenate([coag_local.reshape(cycles, cells, 1, bins), dust_velocity], axis=2)
     az_count = lax.axis_size("az")
     quotient = cycle_shifts // cells
     remain = cycle_shifts % cells
@@ -43,24 +98,8 @@
     joined = jnp.concatenate([before, state], axis=1)
     position = cells + jnp.arange(cells, dtype=jnp.int32)[None, :] - remain[:, None]
     state = jnp.take_along_axis(joined, position[:, :, None, None], axis=1)
-    moved_density = state[:, :, 0, :]
+    coag_density = state[:, :, 0, :]
     moved_velocity = state[:, :, 1:, :]
-    onehot = (
-        fragment_bins.reshape(-1)[:, None] == jnp.arange(bins, dtype=jnp.int32)[None, :]
-    ).astype(jnp.float32)
-    table = kernel.reshape(-1)[:, None] * onehot
-    total_cells = cycles * cells
-    block = math.gcd(total_cells, 64)
-
-    def coag_block(dens):
-        pairs = (dens[:, :, None] * dens[:, None, :]).reshape(dens.shape[0], -1)
-        gain = jnp.dot(pairs, table, precision=lax.Precision.HIGHEST)
-        loss = dens * jnp.dot(dens, kernel.T, precision=lax.Precision.HIGHEST)
-        return dens + gain - loss
-
-    coag_density = lax.map(
-        coag_block, moved_density.reshape(total_cells // block, block, bins)
-    ).reshape(cycles, cells, bins)
     coarse_density = gas_density.reshape(gas_cycles, cells, 4).mean(-1)
     coarse_velocity = (
         gas_velocity.reshape(gas_cycles, 2, cells, 4).mean(-1).reshape(gas_cycles, 2 * cells)

time: 713 us -> 405 us (0.57)
  matrix products: 341 us -> 0.67 us
  Pallas kernels: 0 us -> 67.9 us
  other arithmetic: 38.5 us -> 19 us
  local copies, waits for them, and re-layouts: 29.6 us -> 14.1 us
  starting transfers between devices: 34.7 us -> 46.9 us
  waiting for transfers between devices: 266 us -> 254 us
    dot_general x32 -> x0, matrix products: 340 us -> none  [the longest x16 326 us: coag_block(): gain = jnp.dot(pairs, table, precision=lax.Precision.HIGHEST)]
    pallas_call x0 -> x1, Pallas kernels: none -> 67.9 us  [coag(): pl.pallas_call(coag_kernel, grid=(cells // block,), in_specs=[pl.BlockSpe...]
    mul x16 -> x0, other arithmetic: 18.3 us -> none  [coag_block(): pairs = (dens[:, :, None] * dens[:, None, :]).reshape(dens.shape[0], -1)]
    ppermute x6, starting transfers between devices: 19.3 us -> 35 us  [from_behind(): return lax.ppermute(block, axis, route)]
    squeeze x16 -> x0, local copies, waits for them, and re-layouts: 12.3 us -> none  [body(): lax.map(coag_block, moved_density.reshape(total_cells // block, block, bi...]
    ppermute x6, waiting for transfers between devices: 264 us -> 252 us  [from_behind(): return lax.ppermute(block, axis, route)]
where the time goes in v1:
time: 405 us; the launch traced here: 403 us
  waiting for transfers between devices  254 us (63%)
  Pallas kernels  67.9 us (17%)
  starting transfers between devices  46.9 us (12%)
  other arithmetic  19 us (5%)
  local copies, waits for them, and re-layouts  14.1 us (3%)
    ppermute x6, waiting for transfers between devices, from_behind(): return lax.ppermute(block, axis, route)  252 us
    pallas_call x1, Pallas kernels, coag(): pl.pallas_call(coag_kernel, grid=(cells // block,), in_specs=[pl.BlockSpe...  67.9 us
    ppermute x6, starting transfers between devices, from_behind(): return lax.ppermute(block, axis, route)  35 us
    ppermute x3, starting transfers between devices, shifted(): return lax.ppermute(block, axis, route)  11.9 us
  transfers between devices with their start and end apart: 9, of which 7 were waited for; matrix products, arithmetic and copies ran while one was open for 1% of the time, Pallas kernels for 0%

profile of v1, /device:TPU:8, one launch (start us, length us, event | category | flops | bytes accessed | tf_op | source)
XLA Modules:
  0.0 403.4 jit_solution(11962371551348263603)
XLA Ops:
  0.6 67.9 %shard_map.112 = f32[1024,128]{1,0:T(8,128)} custom-call(f32[1024,128]{1,0:T(8,128)} %bitcast.24, f32[128,128]{1,0:T(8,128)} %k_ref.1, s32[128,128]{1,0:T(8,128)} %f_ref.1), custom_call_target="tpu_custom_call" | custom-call | tf_op jit(solution)/shard_map/pallas_call | solution.py:49
  68.5 2.3 pad_maximum_fusion.1
  71.1 0.4 copy-done.9
  71.5 30.9 %collective-permute-done = f32[64,16,3,128]{3,1,2,0:T(8,128)S(1)} collective-permute-done((f32[64,16,3,128]{3,1,2,0:T(8,128)S(1)}, f32[64,16,3,128]{3,1,2,0:T(8,128)S(1)}, u32[]{:S(2)}, u32[]{:S(2)}) %collective-permute-start) | collective-permute-done | bytes 1572896 | tf_op jit(solution)/shard_map/ppermute | solution.py:66
  102.4 1.8 copy_select_fusion.4
  104.3 0.4 collective-permute-start.1
  104.7 52.1 %collective-permute-done.1 = f32[64,16,3,128]{3,1,2,0:T(8,128)S(1)} collective-permute-done((f32[64,16,3,128]{3,1,2,0:T(8,128)S(1)}, f32[64,16,3,128]{3,1,2,0:T(8,128)S(1)}, u32[]{:S(2)}, u32[]{:S(2)}) %collective-permute-start.1) | collective-permute-done | bytes 1572896 | tf_op jit(solution)/shard_map/ppermute | solution.py:66
  156.8 1.1 copy_select_fusion.3
  158.0 32.5 %collective-permute-start.2 = (f32[64,16,3,128]{3,1,2,0:T(8,128)S(1)}, f32[64,16,3,128]{3,1,2,0:T(8,128)S(1)}, u32[]{:S(2)}, u32[]{:S(2)}) collective-permute-start(f32[64,16,3,128]{3,1,2,0:T(8,128)S(1)} %copy.30), channel_id=1, source_target_pairs={{28,0},{29,1},{30,2},{31,3},{0,4},{1,5},{2,6},{3,7},{4,8},{5,9},{6... | collective-permute-start | bytes 4718600 | tf_op jit(solution)/shard_map/ppermute | solution.py:66
  190.5 65.4 %collective-permute-done.2 = f32[64,16,3,128]{3,1,2,0:T(8,128)S(1)} collective-permute-done((f32[64,16,3,128]{3,1,2,0:T(8,128)S(1)}, f32[64,16,3,128]{3,1,2,0:T(8,128)S(1)}, u32[]{:S(2)}, u32[]{:S(2)}) %collective-permute-start.2) | collective-permute-done | bytes 1572896 | tf_op jit(solution)/shard_map/ppermute | solution.py:66
  255.8 1.1 copy_select_fusion.2
  257.1 1.0 collective-permute-start.3
  258.0 36.4 %collective-permute-done.3 = f32[64,16,3,128]{3,1,2,0:T(8,128)S(1)} collective-permute-done((f32[64,16,3,128]{3,1,2,0:T(8,128)S(1)}, f32[64,16,3,128]{3,1,2,0:T(8,128)S(1)}, u32[]{:S(2)}, u32[]{:S(2)}) %collective-permute-start.3) | collective-permute-done | bytes 1572896 | tf_op jit(solution)/shard_map/ppermute | solution.py:66
  294.5 1.1 copy_select_fusion.1
  295.6 1.3 copy.34
  296.9 1.1 collective-permute-start.4
  298.0 3.8 collective-permute-start.6
  301.9 3.5 collective-permute-start.7
  305.3 27.6 %collective-permute-done.4 = f32[64,16,3,128]{3,1,2,0:T(8,128)} collective-permute-done((f32[64,16,3,128]{3,1,2,0:T(8,128)}, f32[64,16,3,128]{3,1,2,0:T(8,128)}, u32[]{:S(2)}, u32[]{:S(2)}) %collective-permute-start.4) | collective-permute-done | bytes 1572896 | tf_op jit(solution)/shard_map/ppermute | solution.py:66
  332.9 2.5 copy_select_fusion
  335.4 1.4 copy.36
  338.1 0.3 copy.38
  338.4 39.7 %collective-permute-done.5 = f32[64,16,3,128]{3,1,2,0:T(8,128)} collective-permute-done((f32[64,16,3,128]{3,1,2,0:T(8,128)}, f32[64,16,3,128]{3,1,2,0:T(8,128)}, u32[]{:S(2)}, u32[]{:S(2)}) %collective-permute-start.5) | collective-permute-done | bytes 1572896 | tf_op jit(solution)/shard_map/ppermute | solution.py:66
  378.1 2.3 copy.37
  380.4 3.5 pad_maximum_fusion
  383.9 6.8 %gather_fusion = f32[1024,3,128]{2,1,0:T(4,128)S(1)} fusion(f32[64,32,3,128]{3,2,1,0:T(4,128)} %pad_maximum_fusion, s32[1024]{0:T(1024)S(1)} %reshape.139), kind=kCustom, calls=%fused_computation | custom fusion | bytes 3153920 | tf_op jit(solution)/shard_map/jit(take_along_axis)/gather | solution.py:100
  390.6 1.4 broadcast_select_fusion
  392.1 0.4 slice.18
  392.4 3.2 multiply_reduce_fusion
  396.2 4.7 %collective-permute-start.8 = (f32[128,128]{0,1:T(8,128)S(1)}, f32[128,128]{0,1:T(8,128)S(1)}, u32[]{:S(2)}, u32[]{:S(2)}) collective-permute-start(f32[128,128]{0,1:T(8,128)S(1)} %slice.21), channel_id=1, source_target_pairs={{32,0},{64,32},{96,64},{128,96},{160,128},{192,160},{224,192},{33,... | collective-permute-start | bytes 196616 | tf_op jit(solution)/shard_map/ppermute | solution.py:72
  400.9 1.9 collective-permute-done.8
  402.8 0.6 divide_subtract_fusion
  (49 shorter events, 2.5 us)
Async XLA Ops:
  70.8 0.7 copy-start.9
  70.8 31.6 %copy-start.2 = (f32[1024,128]{1,0:T(8,128)S(1)}, f32[1024,128]{1,0:T(8,128)}, u32[]{:S(2)}) copy-start(f32[1024,128]{1,0:T(8,128)} %shard_map.112) | copy-start | bytes 1572868
  70.8 31.6 %copy-start.3 = (f32[64,16,2,128]{3,2,1,0:T(2,128)S(1)}, f32[64,16,2,128]{3,2,1,0:T(2,128)}, u32[]{:S(2)}) copy-start(f32[64,16,2,128]{3,2,1,0:T(2,128)} %param.10) | copy-start | bytes 3145732
  71.0 31.4 %collective-permute-start = (f32[64,16,3,128]{3,1,2,0:T(8,128)S(1)}, f32[64,16,3,128]{3,1,2,0:T(8,128)S(1)}, u32[]{:S(2)}, u32[]{:S(2)}) collective-permute-start(f32[64,16,3,128]{3,1,2,0:T(8,128)S(1)} %copy.26), channel_id=1, source_target_pairs={{31,0},{0,1},{1,2},{2,3},{3,4},{4,5},{5,6},{6,7},{7,8},{8,9},{9,10... | collective-permute-start | bytes 4718600 | tf_op jit(solution)/shard_map/ppermute | solution.py:66
  104.3 52.5 %collective-permute-start.1 = (f32[64,16,3,128]{3,1,2,0:T(8,128)S(1)}, f32[64,16,3,128]{3,1,2,0:T(8,128)S(1)}, u32[]{:S(2)}, u32[]{:S(2)}) collective-permute-start(f32[64,16,3,128]{3,1,2,0:T(8,128)S(1)} %copy.28), channel_id=1, source_target_pairs={{30,0},{31,1},{0,2},{1,3},{2,4},{3,5},{4,6},{5,7},{6,8},{7,9},{8,1... | collective-permute-start | bytes 4718600 | tf_op jit(solution)/shard_map/ppermute | solution.py:66
  158.0 97.9 %collective-permute-start.2 = (f32[64,16,3,128]{3,1,2,0:T(8,128)S(1)}, f32[64,16,3,128]{3,1,2,0:T(8,128)S(1)}, u32[]{:S(2)}, u32[]{:S(2)}) collective-permute-start(f32[64,16,3,128]{3,1,2,0:T(8,128)S(1)} %copy.30), channel_id=1, source_target_pairs={{28,0},{29,1},{30,2},{31,3},{0,4},{1,5},{2,6},{3,7},{4,8},{5,9},{6... | collective-permute-start | bytes 4718600 | tf_op jit(solution)/shard_map/ppermute | solution.py:66
  257.1 37.4 %collective-permute-start.3 = (f32[64,16,3,128]{3,1,2,0:T(8,128)S(1)}, f32[64,16,3,128]{3,1,2,0:T(8,128)S(1)}, u32[]{:S(2)}, u32[]{:S(2)}) collective-permute-start(f32[64,16,3,128]{3,1,2,0:T(8,128)S(1)} %copy.32), channel_id=1, source_target_pairs={{24,0},{25,1},{26,2},{27,3},{28,4},{29,5},{30,6},{31,7},{0,8},{1,9... | collective-permute-start | bytes 4718600 | tf_op jit(solution)/shard_map/ppermute | solution.py:66
  295.6 2.4 copy-start.5
  295.6 6.3 %copy-start.6 = (f32[128,64]{0,1:T(8,128)S(1)}, f32[128,64]{0,1:T(8,128)}, u32[]{:S(2)}) copy-start(f32[128,64]{0,1:T(8,128)} %param.11) | copy-start | bytes 98308
  296.9 36.0 %collective-permute-start.4 = (f32[64,16,3,128]{3,1,2,0:T(8,128)}, f32[64,16,3,128]{3,1,2,0:T(8,128)}, u32[]{:S(2)}, u32[]{:S(2)}) collective-permute-start(f32[64,16,3,128]{3,1,2,0:T(8,128)} %copy.34), channel_id=1, source_target_pairs={{16,0},{17,1},{18,2},{19,3},{20,4},{21,5},{22,6},{23,7},{24,8},{25... | collective-permute-start | bytes 4718600 | tf_op jit(solution)/shard_map/ppermute | solution.py:66
  298.0 39.8 %collective-permute-start.6 = (f32[128,32]{0,1:T(8,128)S(1)}, f32[128,32]{0,1:T(8,128)S(1)}, u32[]{:S(2)}, u32[]{:S(2)}) collective-permute-start(f32[128,32]{0,1:T(8,128)S(1)} %bitcast.30), channel_id=1, source_target_pairs={{0,32},{32,64},{64,96},{96,128},{128,160},{160,192},{192,224},{1,3... | collective-permute-start | bytes 49160 | tf_op jit(solution)/shard_map/ppermute | solution.py:72
  301.9 35.4 %collective-permute-start.7 = (f32[128,16]{0,1:T(8,128)S(1)}, f32[128,16]{0,1:T(8,128)S(1)}, u32[]{:S(2)}, u32[]{:S(2)}) collective-permute-start(f32[128,16]{0,1:T(8,128)S(1)} %broadcast_multiply_fusion.1), channel_id=1, source_target_pairs={{0,32},{32,64},{64,96},{96,128},{128,160},{160,192},{192,224},{1,3... | collective-permute-start | bytes 24584 | tf_op jit(solution)/shard_map/ppermute | solution.py:72
  335.4 1.8 copy-start
  335.4 1.9 copy-start.8
  335.4 2.2 copy-start.7
  336.9 41.2 %collective-permute-start.5 = (f32[64,16,3,128]{3,1,2,0:T(8,128)}, f32[64,16,3,128]{3,1,2,0:T(8,128)}, u32[]{:S(2)}, u32[]{:S(2)}) collective-permute-start(f32[64,16,3,128]{3,1,2,0:T(8,128)} %copy.36), channel_id=1, source_target_pairs={{31,0},{0,1},{1,2},{2,3},{3,4},{4,5},{5,6},{6,7},{7,8},{8,9},{9,10... | collective-permute-start | bytes 4718600 | tf_op jit(solution)/shard_map/ppermute | solution.py:66
  338.0 42.3 %copy-start.1 = (f32[64,16,3,128]{3,2,1,0:T(4,128)S(1)}, f32[64,16,3,128]{3,2,1,0:T(4,128)}, u32[]{:S(2)}) copy-start(f32[64,16,3,128]{3,2,1,0:T(4,128)} %copy-done) | copy-start | bytes 4718596
  392.4 3.2 copy-start.4
  396.2 6.5 %collective-permute-start.8 = (f32[128,128]{0,1:T(8,128)S(1)}, f32[128,128]{0,1:T(8,128)S(1)}, u32[]{:S(2)}, u32[]{:S(2)}) collective-permute-start(f32[128,128]{0,1:T(8,128)S(1)} %slice.21), channel_id=1, source_target_pairs={{32,0},{64,32},{96,64},{128,96},{160,128},{192,160},{224,192},{33,... | collective-permute-start | bytes 196616 | tf_op jit(solution)/shard_map/ppermute | solution.py:72

commit v2 on v1

--- a/solution.py
+++ b/solution.py
@@ -88,16 +88,15 @@
     coag_local = coag(dust_density.reshape(cycles * cells, bins), kernel, fragment_bins)
     state = jnp.concatenate([coag_local.reshape(cycles, cells, 1, bins), dust_velocity], axis=2)
     az_count = lax.axis_size("az")
-    quotient = cycle_shifts // cells
-    remain = cycle_shifts % cells
-    for level in range(az_count.bit_length() - 1):
-        moved = from_behind(state, "az", 1 << level)
-        taken = quotient // (1 << level) % 2 == 1
-        state = jnp.where(taken[:, None, None, None], moved, state)
-    before = from_behind(state, "az", 1)
-    joined = jnp.concatenate([before, state], axis=1)
-    position = cells + jnp.arange(cells, dtype=jnp.int32)[None, :] - remain[:, None]
-    state = jnp.take_along_axis(joined, position[:, :, None, None], axis=1)
+    whole = cells * az_count
+    own = cycles // az_count
+    rings = lax.all_to_all(state, "az", 0, 1, tiled=True)
+    turns = lax.dynamic_slice(cycle_shifts, (lax.axis_index("az") * own,), (own,))
+    doubled = jnp.concatenate([rings, rings], axis=1)
+    rings = jnp.stack(
+        [lax.dynamic_slice_in_dim(doubled[c], whole - turns[c], whole, 0) for c in range(own)]
+    )
+    state = lax.all_to_all(rings, "az", 1, 0, tiled=True)
     coag_density = state[:, :, 0, :]
     moved_velocity = state[:, :, 1:, :]
     coarse_density = gas_density.reshape(gas_cycles, cells, 4).mean(-1)

time: 405 us -> 183 us (0.45)
  waiting for transfers between devices: 254 us -> 74.2 us
  starting transfers between devices: 46.9 us -> 24.2 us
  other arithmetic: 19 us -> 4.53 us
  local copies, waits for them, and re-layouts: 14.1 us -> 6.86 us
    ppermute x6 -> x0, waiting for transfers between devices: 252 us -> none  [from_behind(): return lax.ppermute(block, axis, route)]
    all_to_all x0 -> x2, waiting for transfers between devices: none -> 44.6 us  [the longest x1 38.4 us: body(): rings = lax.all_to_all(state, 'az', 0, 1, tiled=True)]
    ppermute x6 -> x0, starting transfers between devices: 35 us -> none  [from_behind(): return lax.ppermute(block, axis, route)]
    ppermute x3, waiting for transfers between devices: 1.89 us -> 29.6 us  [shifted(): return lax.ppermute(block, axis, route)]
    all_to_all x0 -> x2, starting transfers between devices: none -> 15.6 us  [the longest x1 11.5 us: body(): rings = lax.all_to_all(state, 'az', 0, 1, tiled=True)]
    select_n x7 -> x0, other arithmetic: 8.87 us -> none  [the longest x5 7.46 us: body(): state = jnp.where(taken[:, None, None, None], moved, state)]
    gather x2 -> x0, local copies, waits for them, and re-layouts: 6.85 us -> none  [body(): state = jnp.take_along_axis(joined, position[:, :, None, None], axis=1)]
  transfers between devices with their start and end apart: 9 -> 5, of which waited for: 7 -> 4; matrix products, arithmetic and copies ran while one was open for 1% -> 2% of each run, Pallas kernels for 0% -> 0%
where the time goes in v2:
time: 183 us; the launch traced here: 182 us
  waiting for transfers between devices  74.2 us (41%)
  Pallas kernels  67.9 us (37%)
  starting transfers between devices  24.2 us (13%)
  local copies, waits for them, and re-layouts  6.86 us (4%)
  other arithmetic  4.53 us (2%)
  between operations  3.49 us (2%)
    pallas_call x1, Pallas kernels, coag(): pl.pallas_call(coag_kernel, grid=(cells // block,), in_specs=[pl.BlockSpe...  67.9 us
    all_to_all x1, waiting for transfers between devices, body(): rings = lax.all_to_all(state, 'az', 0, 1, tiled=True)  38.4 us
    ppermute x3, waiting for transfers between devices, shifted(): return lax.ppermute(block, axis, route)  29.6 us
    all_to_all x1, starting transfers between devices, body(): rings = lax.all_to_all(state, 'az', 0, 1, tiled=True)  11.5 us
    ppermute x3, starting transfers between devices, shifted(): return lax.ppermute(block, axis, route)  8.64 us
    all_to_all x1, waiting for transfers between devices, body(): state = lax.all_to_all(rings, 'az', 1, 0, tiled=True)  6.27 us
    all_to_all x1, starting transfers between devices, body(): state = lax.all_to_all(rings, 'az', 1, 0, tiled=True)  4.11 us
  transfers between devices with their start and end apart: 5, of which 4 were waited for; matrix products, arithmetic and copies ran while one was open for 2% of the time, Pallas kernels for 0%

profile of v2, /device:TPU:8, one launch (start us, length us, event | category | flops | bytes accessed | tf_op | source)
XLA Modules:
  0.0 181.9 jit_solution(11715757069118360389)
XLA Ops:
  0.6 1.3 copy.37
  1.9 67.9 %shard_map.112 = f32[1024,128]{1,0:T(8,128)} custom-call(f32[1024,128]{1,0:T(8,128)} %bitcast.36, f32[128,128]{1,0:T(8,128)} %k_ref.1, s32[128,128]{1,0:T(8,128)} %f_ref.1), custom_call_target="tpu_custom_call" | custom-call | tf_op jit(solution)/shard_map/pallas_call | solution.py:49
  69.8 2.3 %pad_maximum_fusion = f32[64,16,3,128]{3,1,2,0:T(8,128)} fusion(f32[64,16,2,128]{3,1,2,0:T(8,128)S(1)} %copy.37, f32[64,16,1,128]{3,1,2,0:T(8,128)} %bitcast.35), kind=kLoop, calls=%fused_computation.4 | loop fusion | flops 393216 | bytes 3145728 | tf_op jit(solution)/shard_map/concatenate | solution.py:89
  72.1 11.5 %all-to-all-start = ((f32[64,16,3,128]{3,1,2,0:T(8,128)}), f32[64,16,3,128]{3,1,2,0:T(8,128)S(1)}, u32[]{:S(2)}, u32[]{:S(2)}) async-start(f32[64,16,3,128]{3,1,2,0:T(8,128)} %pad_maximum_fusion), calls=%async_computation | async-start | bytes 3145728 | tf_op jit(solution)/shard_map/all_to_all | solution.py:93
  83.6 0.1 dynamic_slice.9
  83.7 0.6 fusion.21
  86.9 38.4 %all-to-all-done = f32[64,16,3,128]{3,1,2,0:T(8,128)S(1)} async-done(((f32[64,16,3,128]{3,1,2,0:T(8,128)}), f32[64,16,3,128]{3,1,2,0:T(8,128)S(1)}, u32[]{:S(2)}, u32[]{:S(2)}) %all-to-all-start) | async-done | bytes 1572896 | tf_op jit(solution)/shard_map/all_to_all | solution.py:93
  125.2 0.1 copy.38
  125.4 0.2 pad_slice_fusion.1
  125.6 0.4 fusion
  126.0 0.1 pad_maximum_fusion.1
  126.1 2.4 %copy.39 = f32[2,512,3,128]{3,0,2,1:T(2,128)} copy(f32[2,512,3,128]{3,1,2,0:T(8,128)S(1)} %pad_maximum_fusion.1) | data formatting | bytes 3145728 | tf_op jit(solution)/shard_map/stack | solution.py:96
  128.4 4.1 %all-to-all-start.1 = ((f32[2,512,3,128]{3,0,2,1:T(2,128)}), f32[2,512,3,128]{3,0,2,1:T(2,128)S(1)}, u32[]{:S(2)}, u32[]{:S(2)}) async-start(f32[2,512,3,128]{3,0,2,1:T(2,128)} %copy.39), calls=%async_computation.1 | async-start | bytes 3145728 | tf_op jit(solution)/shard_map/all_to_all | solution.py:99
  132.6 2.0 %collective-permute-start.1 = (f32[128,16]{0,1:T(8,128)S(1)}, f32[128,16]{0,1:T(8,128)S(1)}, u32[]{:S(2)}, u32[]{:S(2)}) collective-permute-start(f32[128,16]{0,1:T(8,128)S(1)} %broadcast_multiply_fusion.1), channel_id=1, source_target_pairs={{0,32},{32,64},{64,96},{96,128},{128,160},{160,192},{192,224},{1,3... | collective-permute-start | bytes 24584 | tf_op jit(solution)/shard_map/ppermute | solution.py:72
  134.7 4.8 %collective-permute-start = (f32[128,32]{0,1:T(8,128)S(1)}, f32[128,32]{0,1:T(8,128)S(1)}, u32[]{:S(2)}, u32[]{:S(2)}) collective-permute-start(f32[128,32]{0,1:T(8,128)S(1)} %bitcast.42), channel_id=1, source_target_pairs={{0,32},{32,64},{64,96},{96,128},{128,160},{160,192},{192,224},{1,3... | collective-permute-start | bytes 49160 | tf_op jit(solution)/shard_map/ppermute | solution.py:72
  139.4 26.9 %collective-permute-done.1 = f32[128,16]{0,1:T(8,128)S(1)} collective-permute-done((f32[128,16]{0,1:T(8,128)S(1)}, f32[128,16]{0,1:T(8,128)S(1)}, u32[]{:S(2)}, u32[]{:S(2)}) %collective-permute-start.1) | collective-permute-done | bytes 8224 | tf_op jit(solution)/shard_map/ppermute | solution.py:72
  166.3 0.2 convolution_negate_fusion
  166.5 0.1 copy.43
  166.6 0.0 copy-done.3
  166.6 0.2 fusion.1
  166.9 0.2 fusion.5
  167.1 0.1 copy.42
  167.2 6.3 %all-to-all-done.1 = f32[2,512,3,128]{3,0,2,1:T(2,128)S(1)} async-done(((f32[2,512,3,128]{3,0,2,1:T(2,128)}), f32[2,512,3,128]{3,0,2,1:T(2,128)S(1)}, u32[]{:S(2)}, u32[]{:S(2)}) %all-to-all-start.1) | async-done | bytes 1572896 | tf_op jit(solution)/shard_map/all_to_all | solution.py:99
  173.5 0.1 copy.40
  173.6 0.2 copy.41
  173.8 0.8 multiply_reduce_fusion
  174.7 0.1 copy.44
  174.8 0.3 fusion.2
  175.1 1.9 %collective-permute-start.2 = (f32[128,128]{0,1:T(8,128)S(1)}, f32[128,128]{0,1:T(8,128)S(1)}, u32[]{:S(2)}, u32[]{:S(2)}) collective-permute-start(f32[128,128]{0,1:T(8,128)S(1)} %slice.37), channel_id=1, source_target_pairs={{32,0},{64,32},{96,64},{128,96},{160,128},{192,160},{224,192},{33,... | collective-permute-start | bytes 196616 | tf_op jit(solution)/shard_map/ppermute | solution.py:72
  177.0 1.5 copy.45
  178.5 2.7 %collective-permute-done.2 = f32[128,128]{0,1:T(8,128)S(1)} collective-permute-done((f32[128,128]{0,1:T(8,128)S(1)}, f32[128,128]{0,1:T(8,128)S(1)}, u32[]{:S(2)}, u32[]{:S(2)}) %collective-permute-start.2) | collective-permute-done | bytes 65568 | tf_op jit(solution)/shard_map/ppermute | solution.py:72
  181.2 0.6 divide_subtract_fusion
  (22 shorter events, 0.2 us)
Async XLA Ops:
  72.1 11.5 %copy-start.5 = (s32[64]{0:T(128)S(1)}, s32[64]{0:T(128)}, u32[]{:S(2)}) copy-start(s32[64]{0:T(128)} %param.15) | copy-start | bytes 772
  72.1 53.1 %all-to-all-start = ((f32[64,16,3,128]{3,1,2,0:T(8,128)}), f32[64,16,3,128]{3,1,2,0:T(8,128)S(1)}, u32[]{:S(2)}, u32[]{:S(2)}) async-start(f32[64,16,3,128]{3,1,2,0:T(8,128)} %pad_maximum_fusion), calls=%async_computation | async-start | bytes 3145728 | tf_op jit(solution)/shard_map/all_to_all | solution.py:93
  128.4 4.1 %copy-start.2 = (f32[128,64]{0,1:T(8,128)S(1)}, f32[128,64]{0,1:T(8,128)}, u32[]{:S(2)}) copy-start(f32[128,64]{0,1:T(8,128)} %param.11) | copy-start | bytes 98308
  128.4 6.2 %copy-start.1 = (f32[128,2,64]{0,2,1:T(8,128)S(1)}, f32[128,2,64]{0,2,1:T(8,128)}, u32[]{:S(2)}) copy-start(f32[128,2,64]{0,2,1:T(8,128)} %param.12) | copy-start | bytes 196612
  128.4 37.9 %copy-start.4 = (s32[64]{0:T(128)S(1)}, s32[64]{0:T(128)}, u32[]{:S(2)}) copy-start(s32[64]{0:T(128)} %param.17) | copy-start | bytes 772
  128.4 38.2 %copy-start.3 = (f32[128]{0:T(128)S(1)}, f32[128]{0:T(128)}, u32[]{:S(2)}) copy-start(f32[128]{0:T(128)} %param.14) | copy-start | bytes 1540
  128.4 45.0 %all-to-all-start.1 = ((f32[2,512,3,128]{3,0,2,1:T(2,128)}), f32[2,512,3,128]{3,0,2,1:T(2,128)S(1)}, u32[]{:S(2)}, u32[]{:S(2)}) async-start(f32[2,512,3,128]{3,0,2,1:T(2,128)} %copy.39), calls=%async_computation.1 | async-start | bytes 3145728 | tf_op jit(solution)/shard_map/all_to_all | solution.py:99
  132.6 33.7 %collective-permute-start.1 = (f32[128,16]{0,1:T(8,128)S(1)}, f32[128,16]{0,1:T(8,128)S(1)}, u32[]{:S(2)}, u32[]{:S(2)}) collective-permute-start(f32[128,16]{0,1:T(8,128)S(1)} %broadcast_multiply_fusion.1), channel_id=1, source_target_pairs={{0,32},{32,64},{64,96},{96,128},{128,160},{160,192},{192,224},{1,3... | collective-permute-start | bytes 24584 | tf_op jit(solution)/shard_map/ppermute | solution.py:72
  134.7 32.2 %collective-permute-start = (f32[128,32]{0,1:T(8,128)S(1)}, f32[128,32]{0,1:T(8,128)S(1)}, u32[]{:S(2)}, u32[]{:S(2)}) collective-permute-start(f32[128,32]{0,1:T(8,128)S(1)} %bitcast.42), channel_id=1, source_target_pairs={{0,32},{32,64},{64,96},{96,128},{128,160},{160,192},{192,224},{1,3... | collective-permute-start | bytes 49160 | tf_op jit(solution)/shard_map/ppermute | solution.py:72
  173.8 0.8 copy-start
  175.1 6.2 %collective-permute-start.2 = (f32[128,128]{0,1:T(8,128)S(1)}, f32[128,128]{0,1:T(8,128)S(1)}, u32[]{:S(2)}, u32[]{:S(2)}) collective-permute-start(f32[128,128]{0,1:T(8,128)S(1)} %slice.37), channel_id=1, source_target_pairs={{32,0},{64,32},{96,64},{128,96},{160,128},{192,160},{224,192},{33,... | collective-permute-start | bytes 196616 | tf_op jit(solution)/shard_map/ppermute | solution.py:72

commit v3 on v2

--- a/solution.py
+++ b/solution.py
@@ -57,6 +57,9 @@
         out_specs=pl.BlockSpec((block, bins), lambda c: (c, 0)),
         out_shape=jax.ShapeDtypeStruct((cells, bins), F32),
         scratch_shapes=[pltpu.VMEM((bins, block), F32), pltpu.VMEM((bins, block), F32)],
+        cost_estimate=pl.CostEstimate(
+            flops=6 * cells * bins**3, transcendentals=0, bytes_accessed=8 * cells * bins
+        ),
     )(dens, kernel, fragment_bins)
 
 
@@ -85,13 +88,15 @@
 ):
     cycles, cells, bins = dust_density.shape
     gas_cycles = gas_density.shape[0]
-    coag_local = coag(dust_density.reshape(cycles * cells, bins), kernel, fragment_bins)
-    state = jnp.concatenate([coag_local.reshape(cycles, cells, 1, bins), dust_velocity], axis=2)
     az_count = lax.axis_size("az")
     whole = cells * az_count
     own = cycles // az_count
-    rings = lax.all_to_all(state, "az", 0, 1, tiled=True)
     turns = lax.dynamic_slice(cycle_shifts, (lax.axis_index("az") * own,), (own,))
+    ring_velocity = lax.all_to_all(dust_velocity, "az", 0, 1, tiled=True)
+    coag_local = coag(dust_density.reshape(cycles * cells, bins), kernel, fragment_bins)
+    coag_local, ring_velocity = lax.optimization_barrier((coag_local, ring_velocity))
+    ring_density = lax.all_to_all(coag_local.reshape(cycles, cells, 1, bins), "az", 0, 1, tiled=True)
+    rings = jnp.concatenate([ring_density, ring_velocity], axis=2)
     doubled = jnp.concatenate([rings, rings], axis=1)
     rings = jnp.stack(
         [lax.dynamic_slice_in_dim(doubled[c], whole - turns[c], whole, 0) for c in range(own)]

time: 183 us -> 169 us (0.923)
  waiting for transfers between devices: 74.2 us -> 52.3 us
  starting transfers between devices: 24.2 us -> 34 us
  other arithmetic: 4.53 us -> 2.08 us
    all_to_all x1 -> x2, waiting for transfers between devices: 38.4 us -> 15.8 us  [the longest x1 15.8 us: body(): lax.all_to_all(coag_local.reshape(cycles, cells, 1, bins), 'az', 0, 1, ti...]
    all_to_all x1 -> x2, starting transfers between devices: 11.5 us -> 21.1 us  [the longest x1 11.3 us: body(): ring_velocity = lax.all_to_all(dust_velocity, 'az', 0, 1, tiled=True)]
    concatenate x1 -> x0, other arithmetic: 2.3 us -> none  [body(): jnp.concatenate([coag_local.reshape(cycles, cells, 1, bins), dust_velocit...]
  transfers between devices with their start and end apart: 5 -> 6, of which waited for: 4 -> 4; matrix products, arithmetic and copies ran while one was open for 2% -> 2% of each run, Pallas kernels for 0% -> 40%
where the time goes in v3:
time: 169 us; the launch traced here: 168 us
  Pallas kernels  67.9 us (40%)
  waiting for transfers between devices  52.3 us (31%)
  starting transfers between devices  34 us (20%)
  local copies, waits for them, and re-layouts  7.95 us (5%)
  between operations  3.51 us (2%)
  other arithmetic  2.08 us (1%)
    pallas_call x1, Pallas kernels, coag(): pl.pallas_call(coag_kernel, grid=(cells // block,), in_specs=[pl.BlockSpe...  67.9 us
    ppermute x3, waiting for transfers between devices, shifted(): return lax.ppermute(block, axis, route)  28.4 us
    all_to_all x1, waiting for transfers between devices, body(): lax.all_to_all(coag_local.reshape(cycles, cells, 1, bins), 'az', 0, 1, ti...  15.8 us
    all_to_all x1, starting transfers between devices, body(): ring_velocity = lax.all_to_all(dust_velocity, 'az', 0, 1, tiled=True)  11.3 us
    all_to_all x1, starting transfers between devices, body(): lax.all_to_all(coag_local.reshape(cycles, cells, 1, bins), 'az', 0, 1, ti...  9.78 us
    ppermute x3, starting transfers between devices, shifted(): return lax.ppermute(block, axis, route)  8.78 us
    all_to_all x1, waiting for transfers between devices, body(): state = lax.all_to_all(rings, 'az', 1, 0, tiled=True)  8.05 us
    all_to_all x1, starting transfers between devices, body(): state = lax.all_to_all(rings, 'az', 1, 0, tiled=True)  4.11 us
  transfers between devices with their start and end apart: 6, of which 4 were waited for; matrix products, arithmetic and copies ran while one was open for 2% of the time, Pallas kernels for 40%

profile of v3, /device:TPU:8, one launch (start us, length us, event | category | flops | bytes accessed | tf_op | source)
XLA Modules:
  0.0 168.4 jit_solution(3959166356522095410)
XLA Ops:
  0.6 2.3 %copy.38 = f32[64,16,2,128]{3,1,2,0:T(8,128)} copy(f32[64,16,2,128]{3,2,1,0:T(2,128)} %param.10) | data formatting | bytes 2097152 | tf_op args[1]
  2.9 11.3 %all-to-all-start = ((f32[64,16,2,128]{3,1,2,0:T(8,128)}), f32[64,16,2,128]{3,1,2,0:T(8,128)S(1)}, u32[]{:S(2)}, u32[]{:S(2)}) async-start(f32[64,16,2,128]{3,1,2,0:T(8,128)} %copy.38), calls=%async_computation | async-start | bytes 2097152 | tf_op jit(solution)/shard_map/all_to_all | solution.py:95
  14.2 67.9 %shard_map.112 = f32[1024,128]{1,0:T(8,128)} custom-call(f32[1024,128]{1,0:T(8,128)} %bitcast.49, f32[128,128]{1,0:T(8,128)} %k_ref.1, s32[128,128]{1,0:T(8,128)} %f_ref.1), custom_call_target="tpu_custom_call" | custom-call | flops 12884901888 | bytes 1048576 | tf_op jit(solution)/shard_map/pallas_call | solution.py:49
  82.1 0.1 copy.39
  82.2 9.8 %all-to-all-start.1 = ((f32[64,16,1,128]{3,1,2,0:T(8,128)}), f32[64,16,1,128]{3,1,2,0:T(8,128)S(1)}, u32[]{:S(2)}, u32[]{:S(2)}) async-start(f32[64,16,1,128]{3,1,2,0:T(8,128)} %bitcast.5), calls=%async_computation.1 | async-start | bytes 1048576 | tf_op jit(solution)/shard_map/all_to_all | solution.py:98
  92.0 0.1 dynamic_slice.9
  92.1 0.6 fusion.21
  95.3 15.8 %all-to-all-done.1 = f32[64,16,1,128]{3,1,2,0:T(8,128)S(1)} async-done(((f32[64,16,1,128]{3,1,2,0:T(8,128)}), f32[64,16,1,128]{3,1,2,0:T(8,128)S(1)}, u32[]{:S(2)}, u32[]{:S(2)}) %all-to-all-start.1) | async-done | bytes 524320 | tf_op jit(solution)/shard_map/all_to_all | solution.py:98
  111.1 0.2 maximum_maximum_fusion
  111.3 0.2 fusion.20
  111.6 0.1 constant_dynamic-slice_fusion
  111.7 0.1 pad_maximum_fusion
  111.8 2.4 %copy.43 = f32[2,512,3,128]{3,0,2,1:T(2,128)} copy(f32[2,512,3,128]{3,1,2,0:T(8,128)S(1)} %pad_maximum_fusion) | data formatting | bytes 3145728 | tf_op jit(solution)/shard_map/stack | solution.py:101
  114.2 4.1 %all-to-all-start.2 = ((f32[2,512,3,128]{3,0,2,1:T(2,128)}), f32[2,512,3,128]{3,0,2,1:T(2,128)S(1)}, u32[]{:S(2)}, u32[]{:S(2)}) async-start(f32[2,512,3,128]{3,0,2,1:T(2,128)} %copy.43), calls=%async_computation.2 | async-start | bytes 3145728 | tf_op jit(solution)/shard_map/all_to_all | solution.py:104
  118.4 2.9 %collective-permute-start.1 = (f32[128,16]{0,1:T(8,128)S(1)}, f32[128,16]{0,1:T(8,128)S(1)}, u32[]{:S(2)}, u32[]{:S(2)}) collective-permute-start(f32[128,16]{0,1:T(8,128)S(1)} %broadcast_multiply_fusion.1), channel_id=1, source_target_pairs={{0,32},{32,64},{64,96},{96,128},{128,160},{160,192},{192,224},{1,3... | collective-permute-start | bytes 24584 | tf_op jit(solution)/shard_map/ppermute | solution.py:75
  121.3 4.0 %collective-permute-start = (f32[128,32]{0,1:T(8,128)S(1)}, f32[128,32]{0,1:T(8,128)S(1)}, u32[]{:S(2)}, u32[]{:S(2)}) collective-permute-start(f32[128,32]{0,1:T(8,128)S(1)} %bitcast.47), channel_id=1, source_target_pairs={{0,32},{32,64},{64,96},{96,128},{128,160},{160,192},{192,224},{1,3... | collective-permute-start | bytes 49160 | tf_op jit(solution)/shard_map/ppermute | solution.py:75
  125.3 25.7 %collective-permute-done.1 = f32[128,16]{0,1:T(8,128)S(1)} collective-permute-done((f32[128,16]{0,1:T(8,128)S(1)}, f32[128,16]{0,1:T(8,128)S(1)}, u32[]{:S(2)}, u32[]{:S(2)}) %collective-permute-start.1) | collective-permute-done | bytes 8224 | tf_op jit(solution)/shard_map/ppermute | solution.py:75
  151.0 0.2 convolution_negate_fusion
  151.2 0.1 copy.47
  151.4 0.2 fusion
  151.6 0.2 fusion.4
  151.8 0.1 copy.46
  151.9 8.1 %all-to-all-done.2 = f32[2,512,3,128]{3,0,2,1:T(2,128)S(1)} async-done(((f32[2,512,3,128]{3,0,2,1:T(2,128)}), f32[2,512,3,128]{3,0,2,1:T(2,128)S(1)}, u32[]{:S(2)}, u32[]{:S(2)}) %all-to-all-start.2) | async-done | bytes 1572896 | tf_op jit(solution)/shard_map/all_to_all | solution.py:104
  160.0 0.1 copy.44
  160.1 0.2 copy.45
  160.4 0.8 multiply_reduce_fusion
  161.2 0.1 copy.48
  161.3 0.3 fusion.1
  161.6 1.9 %collective-permute-start.2 = (f32[128,128]{0,1:T(8,128)S(1)}, f32[128,128]{0,1:T(8,128)S(1)}, u32[]{:S(2)}, u32[]{:S(2)}) collective-permute-start(f32[128,128]{0,1:T(8,128)S(1)} %slice.37), channel_id=1, source_target_pairs={{32,0},{64,32},{96,64},{128,96},{160,128},{192,160},{224,192},{33,... | collective-permute-start | bytes 196616 | tf_op jit(solution)/shard_map/ppermute | solution.py:75
  163.5 1.5 copy.49
  165.0 2.7 %collective-permute-done.2 = f32[128,128]{0,1:T(8,128)S(1)} collective-permute-done((f32[128,128]{0,1:T(8,128)S(1)}, f32[128,128]{0,1:T(8,128)S(1)}, u32[]{:S(2)}, u32[]{:S(2)}) %collective-permute-start.2) | collective-permute-done | bytes 65568 | tf_op jit(solution)/shard_map/ppermute | solution.py:75
  167.8 0.6 divide_subtract_fusion
  (25 shorter events, 0.3 us)
Async XLA Ops:
  2.9 79.2 %all-to-all-start = ((f32[64,16,2,128]{3,1,2,0:T(8,128)}), f32[64,16,2,128]{3,1,2,0:T(8,128)S(1)}, u32[]{:S(2)}, u32[]{:S(2)}) async-start(f32[64,16,2,128]{3,1,2,0:T(8,128)} %copy.38), calls=%async_computation | async-start | bytes 2097152 | tf_op jit(solution)/shard_map/all_to_all | solution.py:95
  82.1 9.9 %copy-start.5 = (s32[64]{0:T(128)S(1)}, s32[64]{0:T(128)}, u32[]{:S(2)}) copy-start(s32[64]{0:T(128)} %param.15) | copy-start | bytes 772
  82.2 28.9 %all-to-all-start.1 = ((f32[64,16,1,128]{3,1,2,0:T(8,128)}), f32[64,16,1,128]{3,1,2,0:T(8,128)S(1)}, u32[]{:S(2)}, u32[]{:S(2)}) async-start(f32[64,16,1,128]{3,1,2,0:T(8,128)} %bitcast.5), calls=%async_computation.1 | async-start | bytes 1048576 | tf_op jit(solution)/shard_map/all_to_all | solution.py:98
  114.2 4.1 %copy-start.2 = (f32[128,64]{0,1:T(8,128)S(1)}, f32[128,64]{0,1:T(8,128)}, u32[]{:S(2)}) copy-start(f32[128,64]{0,1:T(8,128)} %param.11) | copy-start | bytes 98308
  114.2 7.0 %copy-start.1 = (f32[128,2,64]{0,2,1:T(8,128)S(1)}, f32[128,2,64]{0,2,1:T(8,128)}, u32[]{:S(2)}) copy-start(f32[128,2,64]{0,2,1:T(8,128)} %param.12) | copy-start | bytes 196612
  114.2 36.9 %copy-start.4 = (s32[64]{0:T(128)S(1)}, s32[64]{0:T(128)}, u32[]{:S(2)}) copy-start(s32[64]{0:T(128)} %param.17) | copy-start | bytes 772
  114.2 37.2 %copy-start.3 = (f32[128]{0:T(128)S(1)}, f32[128]{0:T(128)}, u32[]{:S(2)}) copy-start(f32[128]{0:T(128)} %param.14) | copy-start | bytes 1540
  114.2 45.8 %all-to-all-start.2 = ((f32[2,512,3,128]{3,0,2,1:T(2,128)}), f32[2,512,3,128]{3,0,2,1:T(2,128)S(1)}, u32[]{:S(2)}, u32[]{:S(2)}) async-start(f32[2,512,3,128]{3,0,2,1:T(2,128)} %copy.43), calls=%async_computation.2 | async-start | bytes 3145728 | tf_op jit(solution)/shard_map/all_to_all | solution.py:104
  118.4 32.7 %collective-permute-start.1 = (f32[128,16]{0,1:T(8,128)S(1)}, f32[128,16]{0,1:T(8,128)S(1)}, u32[]{:S(2)}, u32[]{:S(2)}) collective-permute-start(f32[128,16]{0,1:T(8,128)S(1)} %broadcast_multiply_fusion.1), channel_id=1, source_target_pairs={{0,32},{32,64},{64,96},{96,128},{128,160},{160,192},{192,224},{1,3... | collective-permute-start | bytes 24584 | tf_op jit(solution)/shard_map/ppermute | solution.py:75
  121.3 30.3 %collective-permute-start = (f32[128,32]{0,1:T(8,128)S(1)}, f32[128,32]{0,1:T(8,128)S(1)}, u32[]{:S(2)}, u32[]{:S(2)}) collective-permute-start(f32[128,32]{0,1:T(8,128)S(1)} %bitcast.47), channel_id=1, source_target_pairs={{0,32},{32,64},{64,96},{96,128},{128,160},{160,192},{192,224},{1,3... | collective-permute-start | bytes 49160 | tf_op jit(solution)/shard_map/ppermute | solution.py:75
  160.3 0.8 copy-start
  161.6 6.2 %collective-permute-start.2 = (f32[128,128]{0,1:T(8,128)S(1)}, f32[128,128]{0,1:T(8,128)S(1)}, u32[]{:S(2)}, u32[]{:S(2)}) collective-permute-start(f32[128,128]{0,1:T(8,128)S(1)} %slice.37), channel_id=1, source_target_pairs={{32,0},{64,32},{96,64},{128,96},{160,128},{192,160},{224,192},{33,... | collective-permute-start | bytes 196616 | tf_op jit(solution)/shard_map/ppermute | solution.py:75

commit v4 on v3

--- a/solution.py
+++ b/solution.py
@@ -18,45 +18,53 @@
     return hi, lo
 
 
-def dot3(a, b):
-    a_hi, a_lo = a
-    b_hi, b_lo = b
-    d = functools.partial(jnp.dot, preferred_element_type=F32)
-    return d(a_hi, b_hi) + (d(a_hi, b_lo) + d(a_lo, b_hi))
-
-
-def coag_kernel(n_ref, k_ref, f_ref, o_ref, nt_ref, gain_ref):
+def coag_kernel(n_ref, k_ref, f_ref, o_ref, nt_ref, gain_ref, rhs_ref, *, group):
     bins = k_ref.shape[0]
     nt = n_ref[...].T
     nt_ref[...] = nt
-    n_parts = split(nt)
-    loss = nt * dot3(split(k_ref[...]), n_parts)
+    n_hi, n_lo = split(nt)
+    rhs_ref[...] = jnp.concatenate([n_hi, n_lo, n_hi], axis=0)
+
+    def three_pass(table):
+        t_hi, t_lo = split(table)
+        lhs = jnp.concatenate([t_hi, t_hi, t_lo], axis=1)
+        return jnp.dot(lhs, rhs_ref[...], preferred_element_type=F32)
+
+    loss = nt * three_pass(k_ref[...])
     gain_ref[...] = jnp.zeros_like(gain_ref)
     rows = lax.broadcasted_iota(jnp.int32, (bins, bins), 0)
 
-    def step(i, carry):
-        table = jnp.where(f_ref[pl.ds(i, 1), :] == rows, k_ref[pl.ds(i, 1), :], 0.0)
-        gain_ref[...] += nt_ref[pl.ds(i, 1), :] * dot3(split(table), n_parts)
+    def step(s, carry):
+        first = s * group
+        tables = [
+            jnp.where(f_ref[pl.ds(first + g, 1), :] == rows, k_ref[pl.ds(first + g, 1), :], 0.0)
+            for g in range(group)
+        ]
+        q = three_pass(jnp.concatenate(tables, axis=0))
+        acc = gain_ref[...]
+        for g in range(group):
+            acc = acc + nt_ref[pl.ds(first + g, 1), :] * q[g * bins : (g + 1) * bins]
+        gain_ref[...] = acc
         return carry
 
-    lax.fori_loop(0, bins, step, 0)
+    lax.fori_loop(0, bins // group, step, 0)
     o_ref[...] = (nt + gain_ref[...] - loss).T
 
 
-def coag(dens, kernel, fragment_bins, block=512):
+def coag(dens, kernel, fragment_bins, group=16):
     cells, bins = dens.shape
-    block = min(block, cells)
+    full = lambda shape: pl.BlockSpec(shape, lambda c: (0, 0))
     return pl.pallas_call(
-        coag_kernel,
-        grid=(cells // block,),
-        in_specs=[
-            pl.BlockSpec((block, bins), lambda c: (c, 0)),
-            pl.BlockSpec((bins, bins), lambda c: (0, 0)),
-            pl.BlockSpec((bins, bins), lambda c: (0, 0)),
+        functools.partial(coag_kernel, group=group),
+        grid=(1,),
+        in_specs=[full((cells, bins)), full((bins, bins)), full((bins, bins))],
+        out_specs=full((cells, bins)),
+        out_shape=jax.ShapeDtypeStruct((cells, bins), F32),
+        scratch_shapes=[
+            pltpu.VMEM((bins, cells), F32),
+            pltpu.VMEM((bins, cells), F32),
+            pltpu.VMEM((3 * bins, cells), BF16),
         ],
-        out_specs=pl.BlockSpec((block, bins), lambda c: (c, 0)),
-        out_shape=jax.ShapeDtypeStruct((cells, bins), F32),
-        scratch_shapes=[pltpu.VMEM((bins, block), F32), pltpu.VMEM((bins, block), F32)],
         cost_estimate=pl.CostEstimate(
             flops=6 * cells * bins**3, transcendentals=0, bytes_accessed=8 * cells * bins
         ),

time: 169 us -> 125 us (0.74)
  Pallas kernels: 67.9 us -> 21.4 us
  waiting for transfers between devices: 52.3 us -> 60 us
  starting transfers between devices: 34 us -> 28.7 us
    pallas_call x1, Pallas kernels: 67.9 us -> 21.4 us  [coag(): pl.pallas_call(functools.partial(coag_kernel, group=group), grid=(1,), in...]
    all_to_all x1, waiting for transfers between devices: 0.01 us -> 9 us  [body(): ring_velocity = lax.all_to_all(dust_velocity, 'az', 0, 1, tiled=True)]
    all_to_all x1, starting transfers between devices: 9.78 us -> 3.91 us  [body(): lax.all_to_all(coag_local.reshape(cycles, cells, 1, bins), 'az', 0, 1, ti...]
    all_to_all x1, waiting for transfers between devices: 8.05 us -> 6.2 us  [body(): state = lax.all_to_all(rings, 'az', 1, 0, tiled=True)]
  transfers between devices with their start and end apart: 6 -> 6, of which waited for: 4 -> 5; matrix products, arithmetic and copies ran while one was open for 2% -> 2% of each run, Pallas kernels for 40% -> 17%
where the time goes in v4:
time: 125 us; the launch traced here: 124 us
  waiting for transfers between devices  60 us (48%)
  starting transfers between devices  28.7 us (23%)
  Pallas kernels  21.4 us (17%)
  local copies, waits for them, and re-layouts  7.96 us (6%)
  between operations  3.5 us (3%)
  other arithmetic  2.08 us (2%)
    ppermute x3, waiting for transfers between devices, shifted(): return lax.ppermute(block, axis, route)  29.5 us
    pallas_call x1, Pallas kernels, coag(): pl.pallas_call(functools.partial(coag_kernel, group=group), grid=(1,), in...  21.4 us
    all_to_all x1, waiting for transfers between devices, body(): lax.all_to_all(coag_local.reshape(cycles, cells, 1, bins), 'az', 0, 1, ti...  15.3 us
    all_to_all x1, starting transfers between devices, body(): ring_velocity = lax.all_to_all(dust_velocity, 'az', 0, 1, tiled=True)  11.3 us
    all_to_all x1, waiting for transfers between devices, body(): ring_velocity = lax.all_to_all(dust_velocity, 'az', 0, 1, tiled=True)  9 us
    ppermute x3, starting transfers between devices, shifted(): return lax.ppermute(block, axis, route)  8.78 us
    all_to_all x1, waiting for transfers between devices, body(): state = lax.all_to_all(rings, 'az', 1, 0, tiled=True)  6.2 us
    all_to_all x1, starting transfers between devices, body(): state = lax.all_to_all(rings, 'az', 1, 0, tiled=True)  4.66 us
  transfers between devices with their start and end apart: 6, of which 5 were waited for; matrix products, arithmetic and copies ran while one was open for 2% of the time, Pallas kernels for 17%

profile of v4, /device:TPU:8, one launch (start us, length us, event | category | flops | bytes accessed | tf_op | source)
XLA Modules:
  0.0 124.3 jit_solution(14761535443092291483)
XLA Ops:
  0.6 2.3 %copy.38 = f32[64,16,2,128]{3,1,2,0:T(8,128)} copy(f32[64,16,2,128]{3,2,1,0:T(2,128)} %param.10) | data formatting | bytes 2097152 | tf_op args[1]
  2.9 11.3 %all-to-all-start = ((f32[64,16,2,128]{3,1,2,0:T(8,128)}), f32[64,16,2,128]{3,1,2,0:T(8,128)S(1)}, u32[]{:S(2)}, u32[]{:S(2)}) async-start(f32[64,16,2,128]{3,1,2,0:T(8,128)} %copy.38), calls=%async_computation | async-start | bytes 2097152 | tf_op jit(solution)/shard_map/all_to_all | solution.py:103
  14.2 21.4 %shard_map.112 = f32[1024,128]{1,0:T(8,128)} custom-call(f32[1024,128]{1,0:T(8,128)} %bitcast.49, f32[128,128]{1,0:T(8,128)} %k_ref.1, s32[128,128]{1,0:T(8,128)} %f_ref.1), custom_call_target="tpu_custom_call" | custom-call | flops 12884901888 | bytes 1048576 | tf_op jit(solution)/shard_map/pallas_call | solution.py:57
  35.6 9.0 %all-to-all-done = f32[64,16,2,128]{3,1,2,0:T(8,128)S(1)} async-done(((f32[64,16,2,128]{3,1,2,0:T(8,128)}), f32[64,16,2,128]{3,1,2,0:T(8,128)S(1)}, u32[]{:S(2)}, u32[]{:S(2)}) %all-to-all-start) | async-done | bytes 1048608 | tf_op jit(solution)/shard_map/all_to_all | solution.py:103
  44.6 0.1 copy.39
  44.7 3.9 %all-to-all-start.1 = ((f32[64,16,1,128]{3,1,2,0:T(8,128)}), f32[64,16,1,128]{3,1,2,0:T(8,128)S(1)}, u32[]{:S(2)}, u32[]{:S(2)}) async-start(f32[64,16,1,128]{3,1,2,0:T(8,128)} %bitcast.5), calls=%async_computation.1 | async-start | bytes 1048576 | tf_op jit(solution)/shard_map/all_to_all | solution.py:106
  48.6 0.1 dynamic_slice.9
  48.7 0.6 fusion.21
  51.9 15.3 %all-to-all-done.1 = f32[64,16,1,128]{3,1,2,0:T(8,128)S(1)} async-done(((f32[64,16,1,128]{3,1,2,0:T(8,128)}), f32[64,16,1,128]{3,1,2,0:T(8,128)S(1)}, u32[]{:S(2)}, u32[]{:S(2)}) %all-to-all-start.1) | async-done | bytes 524320 | tf_op jit(solution)/shard_map/all_to_all | solution.py:106
  67.3 0.2 maximum_maximum_fusion
  67.5 0.2 fusion.20
  67.7 0.1 constant_dynamic-slice_fusion
  67.8 0.1 pad_maximum_fusion
  67.9 2.4 %copy.43 = f32[2,512,3,128]{3,0,2,1:T(2,128)} copy(f32[2,512,3,128]{3,1,2,0:T(8,128)S(1)} %pad_maximum_fusion) | data formatting | bytes 3145728 | tf_op jit(solution)/shard_map/stack | solution.py:109
  70.3 4.7 %all-to-all-start.2 = ((f32[2,512,3,128]{3,0,2,1:T(2,128)}), f32[2,512,3,128]{3,0,2,1:T(2,128)S(1)}, u32[]{:S(2)}, u32[]{:S(2)}) async-start(f32[2,512,3,128]{3,0,2,1:T(2,128)} %copy.43), calls=%async_computation.2 | async-start | bytes 3145728 | tf_op jit(solution)/shard_map/all_to_all | solution.py:112
  75.0 2.0 %collective-permute-start.1 = (f32[128,16]{0,1:T(8,128)S(1)}, f32[128,16]{0,1:T(8,128)S(1)}, u32[]{:S(2)}, u32[]{:S(2)}) collective-permute-start(f32[128,16]{0,1:T(8,128)S(1)} %broadcast_multiply_fusion.1), channel_id=1, source_target_pairs={{0,32},{32,64},{64,96},{96,128},{128,160},{160,192},{192,224},{1,3... | collective-permute-start | bytes 24584 | tf_op jit(solution)/shard_map/ppermute | solution.py:83
  77.1 4.9 %collective-permute-start = (f32[128,32]{0,1:T(8,128)S(1)}, f32[128,32]{0,1:T(8,128)S(1)}, u32[]{:S(2)}, u32[]{:S(2)}) collective-permute-start(f32[128,32]{0,1:T(8,128)S(1)} %bitcast.47), channel_id=1, source_target_pairs={{0,32},{32,64},{64,96},{96,128},{128,160},{160,192},{192,224},{1,3... | collective-permute-start | bytes 49160 | tf_op jit(solution)/shard_map/ppermute | solution.py:83
  82.0 26.8 %collective-permute-done.1 = f32[128,16]{0,1:T(8,128)S(1)} collective-permute-done((f32[128,16]{0,1:T(8,128)S(1)}, f32[128,16]{0,1:T(8,128)S(1)}, u32[]{:S(2)}, u32[]{:S(2)}) %collective-permute-start.1) | collective-permute-done | bytes 8224 | tf_op jit(solution)/shard_map/ppermute | solution.py:83
  108.8 0.2 convolution_negate_fusion
  109.0 0.1 copy.47
  109.1 0.2 fusion
  109.3 0.2 fusion.4
  109.5 0.1 copy.46
  109.7 6.2 %all-to-all-done.2 = f32[2,512,3,128]{3,0,2,1:T(2,128)S(1)} async-done(((f32[2,512,3,128]{3,0,2,1:T(2,128)}), f32[2,512,3,128]{3,0,2,1:T(2,128)S(1)}, u32[]{:S(2)}, u32[]{:S(2)}) %all-to-all-start.2) | async-done | bytes 1572896 | tf_op jit(solution)/shard_map/all_to_all | solution.py:112
  115.9 0.1 copy.44
  116.0 0.2 copy.45
  116.2 0.8 multiply_reduce_fusion
  117.2 0.3 fusion.1
  117.5 1.9 %collective-permute-start.2 = (f32[128,128]{0,1:T(8,128)S(1)}, f32[128,128]{0,1:T(8,128)S(1)}, u32[]{:S(2)}, u32[]{:S(2)}) collective-permute-start(f32[128,128]{0,1:T(8,128)S(1)} %slice.37), channel_id=1, source_target_pairs={{32,0},{64,32},{96,64},{128,96},{160,128},{192,160},{224,192},{33,... | collective-permute-start | bytes 196616 | tf_op jit(solution)/shard_map/ppermute | solution.py:83
  119.4 1.5 %copy.49 = f32[64,16,2,128]{3,2,1,0:T(2,128)} copy(f32[64,16,2,128]{3,1,2,0:T(8,128)S(1)} %get-tuple-element.17) | data formatting | bytes 2097152
  120.9 2.7 %collective-permute-done.2 = f32[128,128]{0,1:T(8,128)S(1)} collective-permute-done((f32[128,128]{0,1:T(8,128)S(1)}, f32[128,128]{0,1:T(8,128)S(1)}, u32[]{:S(2)}, u32[]{:S(2)}) %collective-permute-start.2) | collective-permute-done | bytes 65568 | tf_op jit(solution)/shard_map/ppermute | solution.py:83
  123.6 0.6 divide_subtract_fusion
  (25 shorter events, 0.3 us)
Async XLA Ops:
  2.9 41.7 %all-to-all-start = ((f32[64,16,2,128]{3,1,2,0:T(8,128)}), f32[64,16,2,128]{3,1,2,0:T(8,128)S(1)}, u32[]{:S(2)}, u32[]{:S(2)}) async-start(f32[64,16,2,128]{3,1,2,0:T(8,128)} %copy.38), calls=%async_computation | async-start | bytes 2097152 | tf_op jit(solution)/shard_map/all_to_all | solution.py:103
  44.6 4.0 %copy-start.5 = (s32[64]{0:T(128)S(1)}, s32[64]{0:T(128)}, u32[]{:S(2)}) copy-start(s32[64]{0:T(128)} %param.15) | copy-start | bytes 772
  44.7 22.5 %all-to-all-start.1 = ((f32[64,16,1,128]{3,1,2,0:T(8,128)}), f32[64,16,1,128]{3,1,2,0:T(8,128)S(1)}, u32[]{:S(2)}, u32[]{:S(2)}) async-start(f32[64,16,1,128]{3,1,2,0:T(8,128)} %bitcast.5), calls=%async_computation.1 | async-start | bytes 1048576 | tf_op jit(solution)/shard_map/all_to_all | solution.py:106
  70.3 4.7 %copy-start.2 = (f32[128,64]{0,1:T(8,128)S(1)}, f32[128,64]{0,1:T(8,128)}, u32[]{:S(2)}) copy-start(f32[128,64]{0,1:T(8,128)} %param.11) | copy-start | bytes 98308
  70.3 6.7 %copy-start.1 = (f32[128,2,64]{0,2,1:T(8,128)S(1)}, f32[128,2,64]{0,2,1:T(8,128)}, u32[]{:S(2)}) copy-start(f32[128,2,64]{0,2,1:T(8,128)} %param.12) | copy-start | bytes 196612
  70.3 38.5 %copy-start.4 = (s32[64]{0:T(128)S(1)}, s32[64]{0:T(128)}, u32[]{:S(2)}) copy-start(s32[64]{0:T(128)} %param.17) | copy-start | bytes 772
  70.3 38.8 %copy-start.3 = (f32[128]{0:T(128)S(1)}, f32[128]{0:T(128)}, u32[]{:S(2)}) copy-start(f32[128]{0:T(128)} %param.14) | copy-start | bytes 1540
  70.3 45.5 %all-to-all-start.2 = ((f32[2,512,3,128]{3,0,2,1:T(2,128)}), f32[2,512,3,128]{3,0,2,1:T(2,128)S(1)}, u32[]{:S(2)}, u32[]{:S(2)}) async-start(f32[2,512,3,128]{3,0,2,1:T(2,128)} %copy.43), calls=%async_computation.2 | async-start | bytes 3145728 | tf_op jit(solution)/shard_map/all_to_all | solution.py:112
  75.0 33.7 %collective-permute-start.1 = (f32[128,16]{0,1:T(8,128)S(1)}, f32[128,16]{0,1:T(8,128)S(1)}, u32[]{:S(2)}, u32[]{:S(2)}) collective-permute-start(f32[128,16]{0,1:T(8,128)S(1)} %broadcast_multiply_fusion.1), channel_id=1, source_target_pairs={{0,32},{32,64},{64,96},{96,128},{128,160},{160,192},{192,224},{1,3... | collective-permute-start | bytes 24584 | tf_op jit(solution)/shard_map/ppermute | solution.py:83
  77.1 32.2 %collective-permute-start = (f32[128,32]{0,1:T(8,128)S(1)}, f32[128,32]{0,1:T(8,128)S(1)}, u32[]{:S(2)}, u32[]{:S(2)}) collective-permute-start(f32[128,32]{0,1:T(8,128)S(1)} %bitcast.47), channel_id=1, source_target_pairs={{0,32},{32,64},{64,96},{96,128},{128,160},{160,192},{192,224},{1,3... | collective-permute-start | bytes 49160 | tf_op jit(solution)/shard_map/ppermute | solution.py:83
  116.2 0.8 copy-start
  117.5 6.2 %collective-permute-start.2 = (f32[128,128]{0,1:T(8,128)S(1)}, f32[128,128]{0,1:T(8,128)S(1)}, u32[]{:S(2)}, u32[]{:S(2)}) collective-permute-start(f32[128,128]{0,1:T(8,128)S(1)} %slice.37), channel_id=1, source_target_pairs={{32,0},{64,32},{96,64},{128,96},{160,128},{192,160},{224,192},{33,... | collective-permute-start | bytes 196616 | tf_op jit(solution)/shard_map/ppermute | solution.py:83

commit v5 on v4

--- a/solution.py
+++ b/solution.py
@@ -100,18 +100,16 @@
     whole = cells * az_count
     own = cycles // az_count
     turns = lax.dynamic_slice(cycle_shifts, (lax.axis_index("az") * own,), (own,))
-    ring_velocity = lax.all_to_all(dust_velocity, "az", 0, 1, tiled=True)
-    coag_local = coag(dust_density.reshape(cycles * cells, bins), kernel, fragment_bins)
-    coag_local, ring_velocity = lax.optimization_barrier((coag_local, ring_velocity))
-    ring_density = lax.all_to_all(coag_local.reshape(cycles, cells, 1, bins), "az", 0, 1, tiled=True)
-    rings = jnp.concatenate([ring_density, ring_velocity], axis=2)
+    state = jnp.concatenate([dust_density[:, :, None, :], dust_velocity], axis=2)
+    rings = lax.all_to_all(state, "az", 0, 1, tiled=True)
     doubled = jnp.concatenate([rings, rings], axis=1)
     rings = jnp.stack(
         [lax.dynamic_slice_in_dim(doubled[c], whole - turns[c], whole, 0) for c in range(own)]
     )
-    state = lax.all_to_all(rings, "az", 1, 0, tiled=True)
-    coag_density = state[:, :, 0, :]
-    moved_velocity = state[:, :, 1:, :]
+    moved_velocity = lax.all_to_all(rings[:, :, 1:, :], "az", 1, 0, tiled=True)
+    ring_coag = coag(rings[:, :, 0, :].reshape(own * whole, bins), kernel, fragment_bins)
+    ring_coag, moved_velocity = lax.optimization_barrier((ring_coag, moved_velocity))
+    coag_density = lax.all_to_all(ring_coag.reshape(own, whole, bins), "az", 1, 0, tiled=True)
     coarse_density = gas_density.reshape(gas_cycles, cells, 4).mean(-1)
     coarse_velocity = (
         gas_velocity.reshape(gas_cycles, 2, cells, 4).mean(-1).reshape(gas_cycles, 2 * cells)

time: 125 us -> 139 us (1.11)
  other arithmetic: 2.08 us -> 12.9 us
  starting transfers between devices: 28.7 us -> 32.7 us
  waiting for transfers between devices: 60 us -> 57.7 us
    ppermute x3, waiting for transfers between devices: 29.5 us -> 12.4 us  [shifted(): return lax.ppermute(block, axis, route)]
    all_to_all x3, waiting for transfers between devices: 30.5 us -> 45.4 us  [the longest x1 38.1 us: body(): rings = lax.all_to_all(state, 'az', 0, 1, tiled=True)]
    concatenate x1, other arithmetic: 0.2 us -> 5.13 us  [body(): doubled = jnp.concatenate([rings, rings], axis=1)]
    ppermute x3, starting transfers between devices: 8.78 us -> 11.6 us  [shifted(): return lax.ppermute(block, axis, route)]
    unnamed x14 -> x17, local copies, waits for them, and re-layouts: 3.81 us -> 1.4 us
    another operation x1 -> x0, local copies, waits for them, and re-layouts: 2.37 us -> none  [body(): jnp.stack([lax.dynamic_slice_in_dim(doubled[c], whole - turns[c], whole,...]
    reduce_sum x1, other arithmetic: 0.8 us -> 3.1 us  [body(): jnp.sum(coag_density[:, :, None, :] * (velocity_out - moved_velocity), ax...]
    slice x1, local copies, waits for them, and re-layouts: 0.2 us -> 2.19 us  [body(): doubled[c]]
  transfers between devices with their start and end apart: 6 -> 6, of which waited for: 5 -> 5; matrix products, arithmetic and copies ran while one was open for 2% -> 4% of each run, Pallas kernels for 17% -> 16%
where the time goes in v5:
time: 139 us; the launch traced here: 137 us
  waiting for transfers between devices  57.7 us (42%)
  starting transfers between devices  32.7 us (24%)
  Pallas kernels  21.4 us (15%)
  other arithmetic  12.9 us (9%)
  local copies, waits for them, and re-layouts  8.4 us (6%)
  between operations  3.51 us (3%)
    all_to_all x1, waiting for transfers between devices, body(): rings = lax.all_to_all(state, 'az', 0, 1, tiled=True)  38.1 us
    pallas_call x1, Pallas kernels, coag(): pl.pallas_call(functools.partial(coag_kernel, group=group), grid=(1,), in...  21.4 us
    ppermute x3, waiting for transfers between devices, shifted(): return lax.ppermute(block, axis, route)  12.4 us
    ppermute x3, starting transfers between devices, shifted(): return lax.ppermute(block, axis, route)  11.6 us
    all_to_all x1, starting transfers between devices, body(): rings = lax.all_to_all(state, 'az', 0, 1, tiled=True)  11.4 us
    all_to_all x1, starting transfers between devices, body(): lax.all_to_all(ring_coag.reshape(own, whole, bins), 'az', 1, 0, tiled=True)  5.57 us
    concatenate x1, other arithmetic, body(): doubled = jnp.concatenate([rings, rings], axis=1)  5.13 us
    all_to_all x1, waiting for transfers between devices, body(): moved_velocity = lax.all_to_all(rings[:, :, 1:, :], 'az', 1, 0, tiled=True)  4.66 us
  transfers between devices with their start and end apart: 6, of which 5 were waited for; matrix products, arithmetic and copies ran while one was open for 4% of the time, Pallas kernels for 16%

profile of v5, /device:TPU:8, one launch (start us, length us, event | category | flops | bytes accessed | tf_op | source)
XLA Modules:
  0.0 137.2 jit_solution(571020147807829764)
XLA Ops:
  0.6 1.4 copy.23
  2.0 1.3 pad_maximum_fusion
  3.3 11.4 %all-to-all-start = ((f32[64,16,3,128]{3,1,2,0:T(8,128)}), f32[64,16,3,128]{3,1,2,0:T(8,128)S(1)}, u32[]{:S(2)}, u32[]{:S(2)}) async-start(f32[64,16,3,128]{3,1,2,0:T(8,128)} %pad_maximum_fusion), calls=%async_computation | async-start | bytes 3145728 | tf_op jit(solution)/shard_map/all_to_all | solution.py:104
  14.8 0.6 fusion.21
  18.0 38.1 %all-to-all-done = f32[64,16,3,128]{3,1,2,0:T(8,128)S(1)} async-done(((f32[64,16,3,128]{3,1,2,0:T(8,128)}), f32[64,16,3,128]{3,1,2,0:T(8,128)S(1)}, u32[]{:S(2)}, u32[]{:S(2)}) %all-to-all-start) | async-done | bytes 1572896 | tf_op jit(solution)/shard_map/all_to_all | solution.py:104
  56.1 0.8 copy.24
  57.0 2.2 %pad_slice_fusion.1 = (f32[1,1024,3,128]{3,0,2,1:T(1,128)S(1)}, f32[1,1024,3,128]{3,0,2,1:T(1,128)S(1)}) fusion(f32[2,512,3,128]{3,0,2,1:T(2,128)S(1)} %bitcast.30), kind=kLoop, calls=%fused_computation.1 | loop fusion | bytes 4718592 | tf_op jit(solution)/shard_map/slice | solution.py:107
  59.1 5.1 %fusion = (f32[1,512,3,128]{3,0,2,1:T(1,128)S(1)}, f32[1,512,3,128]{3,0,2,1:T(1,128)S(1)}) fusion(s32[]{:T(128)S(6)} %select_n.11, f32[2,512,3,128]{3,0,2,1:T(2,128)S(1)} %bitcast.31, f32[1,1024,3,128]{3,0,2,1:T(1,128)S(1)} %get-tuple-element.10, s32[]{:T(128)S(6)} %select_n.10, f32[1,1024,3,128]{3,0,2,1:T(1,128)S(1)} %get-tuple-element.9), kind=kLoop, calls=%fused_computation.9 | loop fusion | flops 393216 | bytes 4718600 | tf_op jit(solution)/shard_map/concatenate | solution.py:105
  64.3 1.9 %pad_maximum_fusion.1 = f32[2,512,2,128]{3,0,2,1:T(2,128)} fusion(f32[1,512,3,128]{3,0,2,1:T(1,128)S(1)} %get-tuple-element.13, f32[1,512,3,128]{3,0,2,1:T(1,128)S(1)} %get-tuple-element.14), kind=kLoop, calls=%fused_computation.6 | loop fusion | flops 262144 | bytes 2621440 | tf_op jit(solution)/shard_map/stack | solution.py:106
  66.2 4.1 %all-to-all-start.1 = ((f32[2,512,2,128]{3,0,2,1:T(2,128)}), f32[2,512,2,128]{3,0,2,1:T(2,128)S(1)}, u32[]{:S(2)}, u32[]{:S(2)}) async-start(f32[2,512,2,128]{3,0,2,1:T(2,128)} %pad_maximum_fusion.1), calls=%async_computation.1 | async-start | bytes 2097152 | tf_op jit(solution)/shard_map/all_to_all | solution.py:109
  70.4 2.8 %collective-permute-start = (f32[128,32]{0,1:T(8,128)S(1)}, f32[128,32]{0,1:T(8,128)S(1)}, u32[]{:S(2)}, u32[]{:S(2)}) collective-permute-start(f32[128,32]{0,1:T(8,128)S(1)} %bitcast.46), channel_id=1, source_target_pairs={{0,32},{32,64},{64,96},{96,128},{128,160},{160,192},{192,224},{1,3... | collective-permute-start | bytes 49160 | tf_op jit(solution)/shard_map/ppermute | solution.py:83
  73.2 0.5 pad_maximum_fusion.2
  73.7 0.8 copy.25
  74.5 21.4 %shard_map.112 = f32[1024,128]{1,0:T(8,128)} custom-call(f32[1024,128]{1,0:T(8,128)} %bitcast.39, f32[128,128]{1,0:T(8,128)} %k_ref.1, s32[128,128]{1,0:T(8,128)} %f_ref.1), custom_call_target="tpu_custom_call" | custom-call | flops 12884901888 | bytes 1048576 | tf_op jit(solution)/shard_map/pallas_call | solution.py:57
  95.9 4.7 %all-to-all-done.1 = f32[2,512,2,128]{3,0,2,1:T(2,128)S(1)} async-done(((f32[2,512,2,128]{3,0,2,1:T(2,128)}), f32[2,512,2,128]{3,0,2,1:T(2,128)S(1)}, u32[]{:S(2)}, u32[]{:S(2)}) %all-to-all-start.1) | async-done | bytes 1048608 | tf_op jit(solution)/shard_map/all_to_all | solution.py:109
  100.5 0.6 copy.26
  101.1 1.2 copy.27
  102.3 5.6 %all-to-all-start.2 = ((f32[2,512,128]{2,0,1:T(2,128)}), f32[2,512,128]{2,0,1:T(2,128)S(1)}, u32[]{:S(2)}, u32[]{:S(2)}) async-start(f32[2,512,128]{2,0,1:T(2,128)} %copy.27), calls=%async_computation.2 | async-start | bytes 1048576 | tf_op jit(solution)/shard_map/all_to_all | solution.py:112
  107.9 4.1 %collective-permute-start.1 = (f32[128,16]{0,1:T(8,128)S(1)}, f32[128,16]{0,1:T(8,128)S(1)}, u32[]{:S(2)}, u32[]{:S(2)}) collective-permute-start(f32[128,16]{0,1:T(8,128)S(1)} %broadcast_multiply_fusion.1), channel_id=1, source_target_pairs={{0,32},{32,64},{64,96},{96,128},{128,160},{160,192},{192,224},{1,3... | collective-permute-start | bytes 24584 | tf_op jit(solution)/shard_map/ppermute | solution.py:83
  112.1 9.8 %collective-permute-done.1 = f32[128,16]{0,1:T(8,128)S(1)} collective-permute-done((f32[128,16]{0,1:T(8,128)S(1)}, f32[128,16]{0,1:T(8,128)S(1)}, u32[]{:S(2)}, u32[]{:S(2)}) %collective-permute-start.1) | collective-permute-done | bytes 8224 | tf_op jit(solution)/shard_map/ppermute | solution.py:83
  121.9 0.2 convolution_negate_fusion
  122.1 0.1 copy.30
  122.2 0.2 fusion.1
  122.4 0.2 fusion.5
  122.7 0.3 copy.29
  123.0 2.6 %all-to-all-done.2 = f32[2,512,128]{2,0,1:T(2,128)S(1)} async-done(((f32[2,512,128]{2,0,1:T(2,128)}), f32[2,512,128]{2,0,1:T(2,128)S(1)}, u32[]{:S(2)}, u32[]{:S(2)}) %all-to-all-start.2) | async-done | bytes 524320 | tf_op jit(solution)/shard_map/all_to_all | solution.py:112
  125.6 3.1 %multiply_reduce_fusion = (f32[64,16,2]{2,1,0:T(8,128)S(1)}, f32[64,16,2,128]{3,2,1,0:T(2,128)}) fusion(f32[64,16,2,128]{3,2,1,0:T(2,128)S(1)} %bitcast.34, f32[64,16,128]{2,1,0:T(8,128)S(1)} %bitcast.36, f32[64,16,128]{2,1,0:T(8,128)S(1)} %fusion.1, f32[64,16,2]{2,1,0:T(8,128)S(1)} %copy.29), kind=kLoop, calls=%fused_computation.7 | loop fusion | flops 1570816 | bytes 3162112 | tf_op jit(solution)/shard_map/reduce_sum | solution.py:128
  128.8 0.3 copy.31
  129.1 0.3 fusion.2
  129.3 4.7 %collective-permute-start.2 = (f32[128,128]{0,1:T(8,128)S(1)}, f32[128,128]{0,1:T(8,128)S(1)}, u32[]{:S(2)}, u32[]{:S(2)}) collective-permute-start(f32[128,128]{0,1:T(8,128)S(1)} %slice.35), channel_id=1, source_target_pairs={{32,0},{64,32},{96,64},{128,96},{160,128},{192,160},{224,192},{33,... | collective-permute-start | bytes 196616 | tf_op jit(solution)/shard_map/ppermute | solution.py:83
  134.0 2.5 %collective-permute-done.2 = f32[128,128]{0,1:T(8,128)S(1)} collective-permute-done((f32[128,128]{0,1:T(8,128)S(1)}, f32[128,128]{0,1:T(8,128)S(1)}, u32[]{:S(2)}, u32[]{:S(2)}) %collective-permute-start.2) | collective-permute-done | bytes 65568 | tf_op jit(solution)/shard_map/ppermute | solution.py:83
  136.6 0.6 divide_subtract_fusion
  (28 shorter events, 0.3 us)
Async XLA Ops:
  0.6 1.4 copy-start.2
  3.3 11.5 %copy-start.7 = (s32[64]{0:T(128)S(1)}, s32[64]{0:T(128)}, u32[]{:S(2)}) copy-start(s32[64]{0:T(128)} %param.15) | copy-start | bytes 772
  3.3 52.9 %all-to-all-start = ((f32[64,16,3,128]{3,1,2,0:T(8,128)}), f32[64,16,3,128]{3,1,2,0:T(8,128)S(1)}, u32[]{:S(2)}, u32[]{:S(2)}) async-start(f32[64,16,3,128]{3,1,2,0:T(8,128)} %pad_maximum_fusion), calls=%async_computation | async-start | bytes 3145728 | tf_op jit(solution)/shard_map/all_to_all | solution.py:104
  66.2 4.1 %copy-start.3 = (f32[128,2,64]{0,2,1:T(8,128)S(1)}, f32[128,2,64]{0,2,1:T(8,128)}, u32[]{:S(2)}) copy-start(f32[128,2,64]{0,2,1:T(8,128)} %param.12) | copy-start | bytes 196612
  66.2 6.9 %copy-start.4 = (f32[128,64]{0,1:T(8,128)S(1)}, f32[128,64]{0,1:T(8,128)}, u32[]{:S(2)}) copy-start(f32[128,64]{0,1:T(8,128)} %param.11) | copy-start | bytes 98308
  66.2 34.3 %all-to-all-start.1 = ((f32[2,512,2,128]{3,0,2,1:T(2,128)}), f32[2,512,2,128]{3,0,2,1:T(2,128)S(1)}, u32[]{:S(2)}, u32[]{:S(2)}) async-start(f32[2,512,2,128]{3,0,2,1:T(2,128)} %pad_maximum_fusion.1), calls=%async_computation.1 | async-start | bytes 2097152 | tf_op jit(solution)/shard_map/all_to_all | solution.py:109
  70.4 52.1 %collective-permute-start = (f32[128,32]{0,1:T(8,128)S(1)}, f32[128,32]{0,1:T(8,128)S(1)}, u32[]{:S(2)}, u32[]{:S(2)}) collective-permute-start(f32[128,32]{0,1:T(8,128)S(1)} %bitcast.46), channel_id=1, source_target_pairs={{0,32},{32,64},{64,96},{96,128},{128,160},{160,192},{192,224},{1,3... | collective-permute-start | bytes 49160 | tf_op jit(solution)/shard_map/ppermute | solution.py:83
  95.9 5.3 %copy-start.1 = (f32[1024,128]{1,0:T(8,128)S(1)}, f32[1024,128]{1,0:T(8,128)}, u32[]{:S(2)}) copy-start(f32[1024,128]{1,0:T(8,128)} %shard_map.112) | copy-start | bytes 1572868
  101.1 20.8 %copy-start.6 = (s32[64]{0:T(128)S(1)}, s32[64]{0:T(128)}, u32[]{:S(2)}) copy-start(s32[64]{0:T(128)} %param.17) | copy-start | bytes 772
  101.1 21.1 %copy-start.5 = (f32[128]{0:T(128)S(1)}, f32[128]{0:T(128)}, u32[]{:S(2)}) copy-start(f32[128]{0:T(128)} %param.14) | copy-start | bytes 1540
  102.3 23.2 %all-to-all-start.2 = ((f32[2,512,128]{2,0,1:T(2,128)}), f32[2,512,128]{2,0,1:T(2,128)S(1)}, u32[]{:S(2)}, u32[]{:S(2)}) async-start(f32[2,512,128]{2,0,1:T(2,128)} %copy.27), calls=%async_computation.2 | async-start | bytes 1048576 | tf_op jit(solution)/shard_map/all_to_all | solution.py:112
  107.9 14.0 %collective-permute-start.1 = (f32[128,16]{0,1:T(8,128)S(1)}, f32[128,16]{0,1:T(8,128)S(1)}, u32[]{:S(2)}, u32[]{:S(2)}) collective-permute-start(f32[128,16]{0,1:T(8,128)S(1)} %broadcast_multiply_fusion.1), channel_id=1, source_target_pairs={{0,32},{32,64},{64,96},{96,128},{128,160},{160,192},{192,224},{1,3... | collective-permute-start | bytes 24584 | tf_op jit(solution)/shard_map/ppermute | solution.py:83
  125.6 3.1 %copy-start = (f32[32,2,16,128]{3,2,1,0:T(8,128)}, f32[32,2,16,128]{3,2,1,0:T(8,128)S(1)}, u32[]{:S(2)}) copy-start(f32[32,2,16,128]{3,2,1,0:T(8,128)S(1)} %copy.28) | copy-start | bytes 1572868
  129.3 7.2 %collective-permute-start.2 = (f32[128,128]{0,1:T(8,128)S(1)}, f32[128,128]{0,1:T(8,128)S(1)}, u32[]{:S(2)}, u32[]{:S(2)}) collective-permute-start(f32[128,128]{0,1:T(8,128)S(1)} %slice.35), channel_id=1, source_target_pairs={{32,0},{64,32},{96,64},{128,96},{160,128},{192,160},{224,192},{33,... | collective-permute-start | bytes 196616 | tf_op jit(solution)/shard_map/ppermute | solution.py:83

commit v6 on v4

--- a/solution.py
+++ b/solution.py
@@ -102,7 +102,14 @@
     turns = lax.dynamic_slice(cycle_shifts, (lax.axis_index("az") * own,), (own,))
     ring_velocity = lax.all_to_all(dust_velocity, "az", 0, 1, tiled=True)
     coag_local = coag(dust_density.reshape(cycles * cells, bins), kernel, fragment_bins)
-    coag_local, ring_velocity = lax.optimization_barrier((coag_local, ring_velocity))
+    coarse_density = gas_density.reshape(gas_cycles, cells, 4).mean(-1)
+    coarse_velocity = (
+        gas_velocity.reshape(gas_cycles, 2, cells, 4).mean(-1).reshape(gas_cycles, 2 * cells)
+    )
+    prev_density, prev_velocity = shifted((coarse_density, coarse_velocity), "rad", 1)
+    coag_local, ring_velocity, prev_density, prev_velocity = lax.optimization_barrier(
+        (coag_local, ring_velocity, prev_density, prev_velocity)
+    )
     ring_density = lax.all_to_all(coag_local.reshape(cycles, cells, 1, bins), "az", 0, 1, tiled=True)
     rings = jnp.concatenate([ring_density, ring_velocity], axis=2)
     doubled = jnp.concatenate([rings, rings], axis=1)
@@ -112,11 +119,6 @@
     state = lax.all_to_all(rings, "az", 1, 0, tiled=True)
     coag_density = state[:, :, 0, :]
     moved_velocity = state[:, :, 1:, :]
-    coarse_density = gas_density.reshape(gas_cycles, cells, 4).mean(-1)
-    coarse_velocity = (
-        gas_velocity.reshape(gas_cycles, 2, cells, 4).mean(-1).reshape(gas_cycles, 2 * cells)
-    )
-    prev_density, prev_velocity = shifted((coarse_density, coarse_velocity), "rad", 1)
     near_density = jnp.concatenate([prev_density, coarse_density], axis=0)
     near_velocity = jnp.concatenate([prev_velocity, coarse_velocity], axis=0)
     first_row = (lax.axis_index("rad") - 1) * gas_cycles

time: 125 us -> 129 us (1.032)
  starting transfers between devices: 28.7 us -> 32.1 us
    all_to_all x1, waiting for transfers between devices: 6.2 us -> 40.2 us  [body(): state = lax.all_to_all(rings, 'az', 1, 0, tiled=True)]
    ppermute x3, waiting for transfers between devices: 29.5 us -> 2.73 us  [shifted(): return lax.ppermute(block, axis, route)]
    all_to_all x1, waiting for transfers between devices: 9 us -> 2 us  [body(): ring_velocity = lax.all_to_all(dust_velocity, 'az', 0, 1, tiled=True)]
    all_to_all x1, starting transfers between devices: 3.91 us -> 7.8 us  [body(): lax.all_to_all(coag_local.reshape(cycles, cells, 1, bins), 'az', 0, 1, ti...]
  transfers between devices with their start and end apart: 6 -> 6, of which waited for: 5 -> 4; matrix products, arithmetic and copies ran while one was open for 2% -> 2% of each run, Pallas kernels for 17% -> 17%
where the time goes in v6:
time: 129 us; the launch traced here: 128 us
  waiting for transfers between devices  60.7 us (47%)
  starting transfers between devices  32.1 us (25%)
  Pallas kernels  21.4 us (17%)
  local copies, waits for them, and re-layouts  7.96 us (6%)
  between operations  3.52 us (3%)
  other arithmetic  2.08 us (2%)
    all_to_all x1, waiting for transfers between devices, body(): state = lax.all_to_all(rings, 'az', 1, 0, tiled=True)  40.2 us
    pallas_call x1, Pallas kernels, coag(): pl.pallas_call(functools.partial(coag_kernel, group=group), grid=(1,), in...  21.4 us
    all_to_all x1, waiting for transfers between devices, body(): lax.all_to_all(coag_local.reshape(cycles, cells, 1, bins), 'az', 0, 1, ti...  15.8 us
    all_to_all x1, starting transfers between devices, body(): ring_velocity = lax.all_to_all(dust_velocity, 'az', 0, 1, tiled=True)  11.4 us
    ppermute x3, starting transfers between devices, shifted(): return lax.ppermute(block, axis, route)  8.78 us
    all_to_all x1, starting transfers between devices, body(): lax.all_to_all(coag_local.reshape(cycles, cells, 1, bins), 'az', 0, 1, ti...  7.8 us
    all_to_all x1, starting transfers between devices, body(): state = lax.all_to_all(rings, 'az', 1, 0, tiled=True)  4.1 us
    unnamed x14, local copies, waits for them, and re-layouts  3.8 us
  transfers between devices with their start and end apart: 6, of which 4 were waited for; matrix products, arithmetic and copies ran while one was open for 2% of the time, Pallas kernels for 17%

profile of v6, /device:TPU:8, one launch (start us, length us, event | category | flops | bytes accessed | tf_op | source)
XLA Modules:
  0.0 128.4 jit_solution(9642894942648064316)
XLA Ops:
  0.6 2.3 %copy.38 = f32[64,16,2,128]{3,1,2,0:T(8,128)} copy(f32[64,16,2,128]{3,2,1,0:T(2,128)} %param.10) | data formatting | bytes 2097152 | tf_op args[1]
  2.9 11.4 %all-to-all-start = ((f32[64,16,2,128]{3,1,2,0:T(8,128)}), f32[64,16,2,128]{3,1,2,0:T(8,128)S(1)}, u32[]{:S(2)}, u32[]{:S(2)}) async-start(f32[64,16,2,128]{3,1,2,0:T(8,128)} %copy.38), calls=%async_computation | async-start | bytes 2097152 | tf_op jit(solution)/shard_map/all_to_all | solution.py:103
  14.4 2.9 %collective-permute-start = (f32[128,16]{0,1:T(8,128)S(1)}, f32[128,16]{0,1:T(8,128)S(1)}, u32[]{:S(2)}, u32[]{:S(2)}) collective-permute-start(f32[128,16]{0,1:T(8,128)S(1)} %broadcast_multiply_fusion.1), channel_id=1, source_target_pairs={{0,32},{32,64},{64,96},{96,128},{128,160},{160,192},{192,224},{1,3... | collective-permute-start | bytes 24584 | tf_op jit(solution)/shard_map/ppermute | solution.py:83
  17.4 3.9 %collective-permute-start.1 = (f32[128,32]{0,1:T(8,128)S(1)}, f32[128,32]{0,1:T(8,128)S(1)}, u32[]{:S(2)}, u32[]{:S(2)}) collective-permute-start(f32[128,32]{0,1:T(8,128)S(1)} %bitcast.47), channel_id=1, source_target_pairs={{0,32},{32,64},{64,96},{96,128},{128,160},{160,192},{192,224},{1,3... | collective-permute-start | bytes 49160 | tf_op jit(solution)/shard_map/ppermute | solution.py:83
  21.3 21.4 %shard_map.112 = f32[1024,128]{1,0:T(8,128)} custom-call(f32[1024,128]{1,0:T(8,128)} %bitcast.49, f32[128,128]{1,0:T(8,128)} %k_ref.1, s32[128,128]{1,0:T(8,128)} %f_ref.1), custom_call_target="tpu_custom_call" | custom-call | flops 12884901888 | bytes 1048576 | tf_op jit(solution)/shard_map/pallas_call | solution.py:57
  42.7 2.0 %all-to-all-done = f32[64,16,2,128]{3,1,2,0:T(8,128)S(1)} async-done(((f32[64,16,2,128]{3,1,2,0:T(8,128)}), f32[64,16,2,128]{3,1,2,0:T(8,128)S(1)}, u32[]{:S(2)}, u32[]{:S(2)}) %all-to-all-start) | async-done | bytes 1048608 | tf_op jit(solution)/shard_map/all_to_all | solution.py:103
  44.7 0.1 copy.39
  44.8 7.8 %all-to-all-start.1 = ((f32[64,16,1,128]{3,1,2,0:T(8,128)}), f32[64,16,1,128]{3,1,2,0:T(8,128)S(1)}, u32[]{:S(2)}, u32[]{:S(2)}) async-start(f32[64,16,1,128]{3,1,2,0:T(8,128)} %bitcast.8), calls=%async_computation.1 | async-start | bytes 1048576 | tf_op jit(solution)/shard_map/all_to_all | solution.py:113
  52.7 0.1 dynamic_slice.9
  52.7 0.6 fusion.21
  55.9 15.8 %all-to-all-done.1 = f32[64,16,1,128]{3,1,2,0:T(8,128)S(1)} async-done(((f32[64,16,1,128]{3,1,2,0:T(8,128)}), f32[64,16,1,128]{3,1,2,0:T(8,128)S(1)}, u32[]{:S(2)}, u32[]{:S(2)}) %all-to-all-start.1) | async-done | bytes 524320 | tf_op jit(solution)/shard_map/all_to_all | solution.py:113
  71.8 0.2 maximum_maximum_fusion
  72.0 0.2 fusion.20
  72.2 0.2 constant_dynamic-slice_fusion
  72.3 0.1 pad_maximum_fusion
  72.5 2.4 %copy.43 = f32[2,512,3,128]{3,0,2,1:T(2,128)} copy(f32[2,512,3,128]{3,1,2,0:T(8,128)S(1)} %pad_maximum_fusion) | data formatting | bytes 3145728 | tf_op jit(solution)/shard_map/stack | solution.py:116
  74.8 4.1 %all-to-all-start.2 = ((f32[2,512,3,128]{3,0,2,1:T(2,128)}), f32[2,512,3,128]{3,0,2,1:T(2,128)S(1)}, u32[]{:S(2)}, u32[]{:S(2)}) async-start(f32[2,512,3,128]{3,0,2,1:T(2,128)} %copy.43), calls=%async_computation.2 | async-start | bytes 3145728 | tf_op jit(solution)/shard_map/all_to_all | solution.py:119
  79.0 0.2 convolution_negate_fusion
  79.2 0.1 copy.47
  79.3 0.2 fusion.4
  79.5 0.1 copy.46
  79.6 0.2 fusion
  79.8 40.2 %all-to-all-done.2 = f32[2,512,3,128]{3,0,2,1:T(2,128)S(1)} async-done(((f32[2,512,3,128]{3,0,2,1:T(2,128)}), f32[2,512,3,128]{3,0,2,1:T(2,128)S(1)}, u32[]{:S(2)}, u32[]{:S(2)}) %all-to-all-start.2) | async-done | bytes 1572896 | tf_op jit(solution)/shard_map/all_to_all | solution.py:119
  120.0 0.1 copy.44
  120.1 0.2 copy.45
  120.4 0.8 multiply_reduce_fusion
  121.2 0.1 copy.48
  121.3 0.3 fusion.1
  121.6 1.9 %collective-permute-start.2 = (f32[128,128]{0,1:T(8,128)S(1)}, f32[128,128]{0,1:T(8,128)S(1)}, u32[]{:S(2)}, u32[]{:S(2)}) collective-permute-start(f32[128,128]{0,1:T(8,128)S(1)} %slice.37), channel_id=1, source_target_pairs={{32,0},{64,32},{96,64},{128,96},{160,128},{192,160},{224,192},{33,... | collective-permute-start | bytes 196616 | tf_op jit(solution)/shard_map/ppermute | solution.py:83
  123.5 1.5 %copy.49 = f32[64,16,2,128]{3,2,1,0:T(2,128)} copy(f32[64,16,2,128]{3,1,2,0:T(8,128)S(1)} %get-tuple-element.21) | data formatting | bytes 2097152
  125.0 2.7 %collective-permute-done.2 = f32[128,128]{0,1:T(8,128)S(1)} collective-permute-done((f32[128,128]{0,1:T(8,128)S(1)}, f32[128,128]{0,1:T(8,128)S(1)}, u32[]{:S(2)}, u32[]{:S(2)}) %collective-permute-start.2) | collective-permute-done | bytes 65568 | tf_op jit(solution)/shard_map/ppermute | solution.py:83
  127.8 0.6 divide_subtract_fusion
  (25 shorter events, 0.2 us)
Async XLA Ops:
  2.9 11.5 %copy-start.2 = (f32[128,64]{0,1:T(8,128)S(1)}, f32[128,64]{0,1:T(8,128)}, u32[]{:S(2)}) copy-start(f32[128,64]{0,1:T(8,128)} %param.11) | copy-start | bytes 98308
  2.9 14.4 %copy-start.1 = (f32[128,2,64]{0,2,1:T(8,128)S(1)}, f32[128,2,64]{0,2,1:T(8,128)}, u32[]{:S(2)}) copy-start(f32[128,2,64]{0,2,1:T(8,128)} %param.12) | copy-start | bytes 196612
  2.9 41.8 %all-to-all-start = ((f32[64,16,2,128]{3,1,2,0:T(8,128)}), f32[64,16,2,128]{3,1,2,0:T(8,128)S(1)}, u32[]{:S(2)}, u32[]{:S(2)}) async-start(f32[64,16,2,128]{3,1,2,0:T(8,128)} %copy.38), calls=%async_computation | async-start | bytes 2097152 | tf_op jit(solution)/shard_map/all_to_all | solution.py:103
  14.4 30.4 %collective-permute-start = (f32[128,16]{0,1:T(8,128)S(1)}, f32[128,16]{0,1:T(8,128)S(1)}, u32[]{:S(2)}, u32[]{:S(2)}) collective-permute-start(f32[128,16]{0,1:T(8,128)S(1)} %broadcast_multiply_fusion.1), channel_id=1, source_target_pairs={{0,32},{32,64},{64,96},{96,128},{128,160},{160,192},{192,224},{1,3... | collective-permute-start | bytes 24584 | tf_op jit(solution)/shard_map/ppermute | solution.py:83
  17.4 27.4 %collective-permute-start.1 = (f32[128,32]{0,1:T(8,128)S(1)}, f32[128,32]{0,1:T(8,128)S(1)}, u32[]{:S(2)}, u32[]{:S(2)}) collective-permute-start(f32[128,32]{0,1:T(8,128)S(1)} %bitcast.47), channel_id=1, source_target_pairs={{0,32},{32,64},{64,96},{96,128},{128,160},{160,192},{192,224},{1,3... | collective-permute-start | bytes 49160 | tf_op jit(solution)/shard_map/ppermute | solution.py:83
  44.7 7.9 %copy-start.5 = (s32[64]{0:T(128)S(1)}, s32[64]{0:T(128)}, u32[]{:S(2)}) copy-start(s32[64]{0:T(128)} %param.15) | copy-start | bytes 772
  44.8 26.9 %all-to-all-start.1 = ((f32[64,16,1,128]{3,1,2,0:T(8,128)}), f32[64,16,1,128]{3,1,2,0:T(8,128)S(1)}, u32[]{:S(2)}, u32[]{:S(2)}) async-start(f32[64,16,1,128]{3,1,2,0:T(8,128)} %bitcast.8), calls=%async_computation.1 | async-start | bytes 1048576 | tf_op jit(solution)/shard_map/all_to_all | solution.py:113
  74.8 4.1 %copy-start.4 = (s32[64]{0:T(128)S(1)}, s32[64]{0:T(128)}, u32[]{:S(2)}) copy-start(s32[64]{0:T(128)} %param.17) | copy-start | bytes 772
  74.8 4.8 %copy-start.3 = (f32[128]{0:T(128)S(1)}, f32[128]{0:T(128)}, u32[]{:S(2)}) copy-start(f32[128]{0:T(128)} %param.14) | copy-start | bytes 1540
  74.8 45.2 %all-to-all-start.2 = ((f32[2,512,3,128]{3,0,2,1:T(2,128)}), f32[2,512,3,128]{3,0,2,1:T(2,128)S(1)}, u32[]{:S(2)}, u32[]{:S(2)}) async-start(f32[2,512,3,128]{3,0,2,1:T(2,128)} %copy.43), calls=%async_computation.2 | async-start | bytes 3145728 | tf_op jit(solution)/shard_map/all_to_all | solution.py:119
  120.4 0.8 copy-start
  121.6 6.2 %collective-permute-start.2 = (f32[128,128]{0,1:T(8,128)S(1)}, f32[128,128]{0,1:T(8,128)S(1)}, u32[]{:S(2)}, u32[]{:S(2)}) collective-permute-start(f32[128,128]{0,1:T(8,128)S(1)} %slice.37), channel_id=1, source_target_pairs={{32,0},{64,32},{96,64},{128,96},{160,128},{192,160},{224,192},{33,... | collective-permute-start | bytes 196616 | tf_op jit(solution)/shard_map/ppermute | solution.py:83

commit v7 on v4

--- a/solution.py
+++ b/solution.py
@@ -83,6 +83,13 @@
     return lax.ppermute(block, axis, route)
 
 
+def gathered(block, count):
+    cycles, cells, channels, bins = block.shape
+    flat = lax.all_to_all(block.reshape(-1, bins), "az", 0, 0, tiled=True)
+    parts = flat.reshape(count, cycles // count, cells, channels, bins)
+    return jnp.transpose(parts, (1, 0, 2, 3, 4)).reshape(cycles // count, count * cells, channels, bins)
+
+
 def body(
     dust_density,
     dust_velocity,
@@ -100,10 +107,10 @@
     whole = cells * az_count
     own = cycles // az_count
     turns = lax.dynamic_slice(cycle_shifts, (lax.axis_index("az") * own,), (own,))
-    ring_velocity = lax.all_to_all(dust_velocity, "az", 0, 1, tiled=True)
+    ring_velocity = gathered(dust_velocity, az_count)
     coag_local = coag(dust_density.reshape(cycles * cells, bins), kernel, fragment_bins)
     coag_local, ring_velocity = lax.optimization_barrier((coag_local, ring_velocity))
-    ring_density = lax.all_to_all(coag_local.reshape(cycles, cells, 1, bins), "az", 0, 1, tiled=True)
+    ring_density = gathered(coag_local.reshape(cycles, cells, 1, bins), az_count)
     rings = jnp.concatenate([ring_density, ring_velocity], axis=2)
     doubled = jnp.concatenate([rings, rings], axis=1)
     rings = jnp.stack(

time: 125 us -> 124 us (level)
    unnamed x14 -> x13, local copies, waits for them, and re-layouts: 3.81 us -> 1.55 us
where the time goes in v7:
time: 124 us; the launch traced here: 123 us
  waiting for transfers between devices  60.1 us (48%)
  starting transfers between devices  28.7 us (23%)
  Pallas kernels  21.4 us (17%)
  local copies, waits for them, and re-layouts  6.82 us (6%)
  between operations  3.51 us (3%)
  other arithmetic  2.08 us (2%)
    ppermute x3, waiting for transfers between devices, shifted(): return lax.ppermute(block, axis, route)  29.5 us
    all_to_all x2, waiting for transfers between devices, gathered(): flat = lax.all_to_all(block.reshape(-1, bins), 'az', 0, 0, tiled=True)  24.3 us
    pallas_call x1, Pallas kernels, coag(): pl.pallas_call(functools.partial(coag_kernel, group=group), grid=(1,), in...  21.4 us
    all_to_all x2, starting transfers between devices, gathered(): flat = lax.all_to_all(block.reshape(-1, bins), 'az', 0, 0, tiled=True)  15.2 us
    ppermute x3, starting transfers between devices, shifted(): return lax.ppermute(block, axis, route)  8.78 us
    all_to_all x1, waiting for transfers between devices, body(): state = lax.all_to_all(rings, 'az', 1, 0, tiled=True)  6.21 us
    all_to_all x1, starting transfers between devices, body(): state = lax.all_to_all(rings, 'az', 1, 0, tiled=True)  4.67 us
  transfers between devices with their start and end apart: 6, of which 5 were waited for; matrix products, arithmetic and copies ran while one was open for 2% of the time, Pallas kernels for 17%

profile of v7, /device:TPU:8, one launch (start us, length us, event | category | flops | bytes accessed | tf_op | source)
XLA Modules:
  0.0 123.2 jit_solution(17812497041147306527)
XLA Ops:
  0.6 11.3 %all-to-all-start = ((f32[32,64,128]{2,1,0:T(8,128)}), f32[32,64,128]{2,1,0:T(8,128)S(1)}, u32[]{:S(2)}, u32[]{:S(2)}) async-start(f32[32,64,128]{2,1,0:T(8,128)} %bitcast.41), calls=%async_computation | async-start | bytes 2097152 | tf_op jit(solution)/shard_map/all_to_all | solution.py:88
  12.0 21.4 %shard_map.112 = f32[1024,128]{1,0:T(8,128)} custom-call(f32[1024,128]{1,0:T(8,128)} %bitcast.49, f32[128,128]{1,0:T(8,128)} %k_ref.1, s32[128,128]{1,0:T(8,128)} %f_ref.1), custom_call_target="tpu_custom_call" | custom-call | flops 12884901888 | bytes 1048576 | tf_op jit(solution)/shard_map/pallas_call | solution.py:57
  33.3 9.0 %all-to-all-done = f32[32,64,128]{2,1,0:T(8,128)S(1)} async-done(((f32[32,64,128]{2,1,0:T(8,128)}), f32[32,64,128]{2,1,0:T(8,128)S(1)}, u32[]{:S(2)}, u32[]{:S(2)}) %all-to-all-start) | async-done | bytes 1048608 | tf_op jit(solution)/shard_map/all_to_all | solution.py:88
  42.3 0.6 copy.44
  43.0 0.6 copy.45
  43.6 3.9 %all-to-all-start.1 = ((f32[32,32,128]{2,1,0:T(8,128)}), f32[32,32,128]{2,1,0:T(8,128)S(1)}, u32[]{:S(2)}, u32[]{:S(2)}) async-start(f32[32,32,128]{2,1,0:T(8,128)} %bitcast.5), calls=%async_computation.1 | async-start | bytes 1048576 | tf_op jit(solution)/shard_map/all_to_all | solution.py:88
  47.5 0.1 dynamic_slice.9
  47.6 0.6 fusion.21
  50.8 15.3 %all-to-all-done.1 = f32[32,32,128]{2,1,0:T(8,128)S(1)} async-done(((f32[32,32,128]{2,1,0:T(8,128)}), f32[32,32,128]{2,1,0:T(8,128)S(1)}, u32[]{:S(2)}, u32[]{:S(2)}) %all-to-all-start.1) | async-done | bytes 524320 | tf_op jit(solution)/shard_map/all_to_all | solution.py:88
  66.1 0.2 maximum_maximum_fusion
  66.4 0.2 fusion.20
  66.6 0.1 constant_dynamic-slice_fusion
  66.7 0.1 pad_maximum_fusion
  66.8 2.4 %copy.48 = f32[2,512,3,128]{3,0,2,1:T(2,128)} copy(f32[2,512,3,128]{3,1,2,0:T(8,128)S(1)} %pad_maximum_fusion) | data formatting | bytes 3145728 | tf_op jit(solution)/shard_map/stack | solution.py:116
  69.2 4.7 %all-to-all-start.2 = ((f32[2,512,3,128]{3,0,2,1:T(2,128)}), f32[2,512,3,128]{3,0,2,1:T(2,128)S(1)}, u32[]{:S(2)}, u32[]{:S(2)}) async-start(f32[2,512,3,128]{3,0,2,1:T(2,128)} %copy.48), calls=%async_computation.2 | async-start | bytes 3145728 | tf_op jit(solution)/shard_map/all_to_all | solution.py:119
  73.9 2.0 %collective-permute-start.1 = (f32[128,16]{0,1:T(8,128)S(1)}, f32[128,16]{0,1:T(8,128)S(1)}, u32[]{:S(2)}, u32[]{:S(2)}) collective-permute-start(f32[128,16]{0,1:T(8,128)S(1)} %broadcast_multiply_fusion.1), channel_id=1, source_target_pairs={{0,32},{32,64},{64,96},{96,128},{128,160},{160,192},{192,224},{1,3... | collective-permute-start | bytes 24584 | tf_op jit(solution)/shard_map/ppermute | solution.py:83
  76.0 4.9 %collective-permute-start = (f32[128,32]{0,1:T(8,128)S(1)}, f32[128,32]{0,1:T(8,128)S(1)}, u32[]{:S(2)}, u32[]{:S(2)}) collective-permute-start(f32[128,32]{0,1:T(8,128)S(1)} %bitcast.47), channel_id=1, source_target_pairs={{0,32},{32,64},{64,96},{96,128},{128,160},{160,192},{192,224},{1,3... | collective-permute-start | bytes 49160 | tf_op jit(solution)/shard_map/ppermute | solution.py:83
  80.9 26.8 %collective-permute-done.1 = f32[128,16]{0,1:T(8,128)S(1)} collective-permute-done((f32[128,16]{0,1:T(8,128)S(1)}, f32[128,16]{0,1:T(8,128)S(1)}, u32[]{:S(2)}, u32[]{:S(2)}) %collective-permute-start.1) | collective-permute-done | bytes 8224 | tf_op jit(solution)/shard_map/ppermute | solution.py:83
  107.7 0.2 convolution_negate_fusion
  107.9 0.1 copy.52
  108.0 0.2 fusion
  108.3 0.2 fusion.4
  108.5 0.1 copy.51
  108.6 6.2 %all-to-all-done.2 = f32[2,512,3,128]{3,0,2,1:T(2,128)S(1)} async-done(((f32[2,512,3,128]{3,0,2,1:T(2,128)}), f32[2,512,3,128]{3,0,2,1:T(2,128)S(1)}, u32[]{:S(2)}, u32[]{:S(2)}) %all-to-all-start.2) | async-done | bytes 1572896 | tf_op jit(solution)/shard_map/all_to_all | solution.py:119
  114.8 0.1 copy.49
  114.9 0.2 copy.50
  115.2 0.8 multiply_reduce_fusion
  116.1 0.3 fusion.1
  116.4 1.9 %collective-permute-start.2 = (f32[128,128]{0,1:T(8,128)S(1)}, f32[128,128]{0,1:T(8,128)S(1)}, u32[]{:S(2)}, u32[]{:S(2)}) collective-permute-start(f32[128,128]{0,1:T(8,128)S(1)} %slice.37), channel_id=1, source_target_pairs={{32,0},{64,32},{96,64},{128,96},{160,128},{192,160},{224,192},{33,... | collective-permute-start | bytes 196616 | tf_op jit(solution)/shard_map/ppermute | solution.py:83
  118.3 1.5 %copy.54 = f32[64,16,2,128]{3,2,1,0:T(2,128)} copy(f32[64,16,2,128]{3,1,2,0:T(8,128)S(1)} %get-tuple-element.20) | data formatting | bytes 2097152
  119.8 2.7 %collective-permute-done.2 = f32[128,128]{0,1:T(8,128)S(1)} collective-permute-done((f32[128,128]{0,1:T(8,128)S(1)}, f32[128,128]{0,1:T(8,128)S(1)}, u32[]{:S(2)}, u32[]{:S(2)}) %collective-permute-start.2) | collective-permute-done | bytes 65568 | tf_op jit(solution)/shard_map/ppermute | solution.py:83
  122.6 0.6 divide_subtract_fusion
  (25 shorter events, 0.3 us)
Async XLA Ops:
  0.6 41.7 %all-to-all-start = ((f32[32,64,128]{2,1,0:T(8,128)}), f32[32,64,128]{2,1,0:T(8,128)S(1)}, u32[]{:S(2)}, u32[]{:S(2)}) async-start(f32[32,64,128]{2,1,0:T(8,128)} %bitcast.41), calls=%async_computation | async-start | bytes 2097152 | tf_op jit(solution)/shard_map/all_to_all | solution.py:88
  43.0 4.5 %copy-start.5 = (s32[64]{0:T(128)S(1)}, s32[64]{0:T(128)}, u32[]{:S(2)}) copy-start(s32[64]{0:T(128)} %param.15) | copy-start | bytes 772
  43.6 22.5 %all-to-all-start.1 = ((f32[32,32,128]{2,1,0:T(8,128)}), f32[32,32,128]{2,1,0:T(8,128)S(1)}, u32[]{:S(2)}, u32[]{:S(2)}) async-start(f32[32,32,128]{2,1,0:T(8,128)} %bitcast.5), calls=%async_computation.1 | async-start | bytes 1048576 | tf_op jit(solution)/shard_map/all_to_all | solution.py:88
  69.2 4.7 %copy-start.2 = (f32[128,64]{0,1:T(8,128)S(1)}, f32[128,64]{0,1:T(8,128)}, u32[]{:S(2)}) copy-start(f32[128,64]{0,1:T(8,128)} %param.11) | copy-start | bytes 98308
  69.2 6.7 %copy-start.1 = (f32[128,2,64]{0,2,1:T(8,128)S(1)}, f32[128,2,64]{0,2,1:T(8,128)}, u32[]{:S(2)}) copy-start(f32[128,2,64]{0,2,1:T(8,128)} %param.12) | copy-start | bytes 196612
  69.2 38.5 %copy-start.4 = (s32[64]{0:T(128)S(1)}, s32[64]{0:T(128)}, u32[]{:S(2)}) copy-start(s32[64]{0:T(128)} %param.17) | copy-start | bytes 772
  69.2 38.8 %copy-start.3 = (f32[128]{0:T(128)S(1)}, f32[128]{0:T(128)}, u32[]{:S(2)}) copy-start(f32[128]{0:T(128)} %param.14) | copy-start | bytes 1540
  69.2 45.6 %all-to-all-start.2 = ((f32[2,512,3,128]{3,0,2,1:T(2,128)}), f32[2,512,3,128]{3,0,2,1:T(2,128)S(1)}, u32[]{:S(2)}, u32[]{:S(2)}) async-start(f32[2,512,3,128]{3,0,2,1:T(2,128)} %copy.48), calls=%async_computation.2 | async-start | bytes 3145728 | tf_op jit(solution)/shard_map/all_to_all | solution.py:119
  73.9 33.8 %collective-permute-start.1 = (f32[128,16]{0,1:T(8,128)S(1)}, f32[128,16]{0,1:T(8,128)S(1)}, u32[]{:S(2)}, u32[]{:S(2)}) collective-permute-start(f32[128,16]{0,1:T(8,128)S(1)} %broadcast_multiply_fusion.1), channel_id=1, source_target_pairs={{0,32},{32,64},{64,96},{96,128},{128,160},{160,192},{192,224},{1,3... | collective-permute-start | bytes 24584 | tf_op jit(solution)/shard_map/ppermute | solution.py:83
  76.0 32.3 %collective-permute-start = (f32[128,32]{0,1:T(8,128)S(1)}, f32[128,32]{0,1:T(8,128)S(1)}, u32[]{:S(2)}, u32[]{:S(2)}) collective-permute-start(f32[128,32]{0,1:T(8,128)S(1)} %bitcast.47), channel_id=1, source_target_pairs={{0,32},{32,64},{64,96},{96,128},{128,160},{160,192},{192,224},{1,3... | collective-permute-start | bytes 49160 | tf_op jit(solution)/shard_map/ppermute | solution.py:83
  115.2 0.8 copy-start
  116.4 6.2 %collective-permute-start.2 = (f32[128,128]{0,1:T(8,128)S(1)}, f32[128,128]{0,1:T(8,128)S(1)}, u32[]{:S(2)}, u32[]{:S(2)}) collective-permute-start(f32[128,128]{0,1:T(8,128)S(1)} %slice.37), channel_id=1, source_target_pairs={{32,0},{64,32},{96,64},{128,96},{160,128},{192,160},{224,192},{33,... | collective-permute-start | bytes 196616 | tf_op jit(solution)/shard_map/ppermute | solution.py:83

commit v8 on v7

--- a/solution.py
+++ b/solution.py
@@ -135,10 +135,19 @@
     frac = 1.0 - jnp.exp(-rho_dust[:, :, None] / grain_param[None, None, :])
     velocity_out = moved_velocity + (u_dust[:, :, :, None] - moved_velocity) * frac[:, :, None, :]
     momentum = jnp.sum(coag_density[:, :, None, :] * (velocity_out - moved_velocity), axis=3) / bins
-    spread = jnp.repeat(jnp.transpose(momentum, (0, 2, 1)), 4, axis=2).reshape(cycles, 8 * cells)
-    near_kick = jnp.dot(select.T, spread, precision=lax.Precision.HIGHEST)
-    from_next = shifted(near_kick[:gas_cycles], "rad", -1)
-    kick = (near_kick[gas_cycles:] + from_next).reshape(gas_cycles, 2, 4 * cells)
+    by_axis = jnp.transpose(momentum, (0, 2, 1)).reshape(cycles, 2 * cells)
+    message = jnp.concatenate([by_axis, gas_map.astype(F32)[:, None]], axis=1)
+    arrived = shifted(message, "rad", -1)
+    own_rows = near_rows[gas_cycles:]
+
+    def kick_of(values, rows_of):
+        spread = jnp.repeat(values.reshape(cycles, 2, cells), 4, axis=2).reshape(cycles, 8 * cells)
+        hits = (rows_of[:, None] == own_rows[None, :]).astype(F32)
+        return jnp.dot(hits.T, spread, precision=lax.Precision.HIGHEST)
+
+    next_rows = arrived[:, 2 * cells].astype(jnp.int32)
+    kick = kick_of(by_axis, gas_map) + kick_of(arrived[:, : 2 * cells], next_rows)
+    kick = kick.reshape(gas_cycles, 2, 4 * cells)
     gas_out = gas_velocity - kick / gas_density[:, None, :]
     return (coag_density, velocity_out, gas_out)
 

time: 124 us -> 123 us (level)
  transfers between devices with their start and end apart: 6 -> 6, of which waited for: 5 -> 5; matrix products, arithmetic and copies ran while one was open for 2% -> 3% of each run, Pallas kernels for 17% -> 17%
where the time goes in v8:
time: 123 us
  waiting for transfers between devices  59.3 us (48%)
  starting transfers between devices  28.7 us (23%)
  Pallas kernels  21.4 us (17%)
  local copies, waits for them, and re-layouts  6.86 us (6%)
  between operations  3.54 us (3%)
  other arithmetic  2.08 us (2%)
    ppermute x3, waiting for transfers between devices, shifted(): return lax.ppermute(block, axis, route)  28.8 us
    all_to_all x2, waiting for transfers between devices, gathered(): flat = lax.all_to_all(block.reshape(-1, bins), 'az', 0, 0, tiled=True)  24.3 us
    pallas_call x1, Pallas kernels, coag(): pl.pallas_call(functools.partial(coag_kernel, group=group), grid=(1,), in...  21.4 us
    all_to_all x2, starting transfers between devices, gathered(): flat = lax.all_to_all(block.reshape(-1, bins), 'az', 0, 0, tiled=True)  15.2 us
    ppermute x3, starting transfers between devices, shifted(): return lax.ppermute(block, axis, route)  8.76 us
    all_to_all x1, waiting for transfers between devices, body(): state = lax.all_to_all(rings, 'az', 1, 0, tiled=True)  6.19 us
    all_to_all x1, starting transfers between devices, body(): state = lax.all_to_all(rings, 'az', 1, 0, tiled=True)  4.67 us
  transfers between devices with their start and end apart: 6, of which 5 were waited for; matrix products, arithmetic and copies ran while one was open for 3% of the time, Pallas kernels for 17%

profile of v8, /device:TPU:8, one launch (start us, length us, event | category | flops | bytes accessed | tf_op | source)
XLA Modules:
  0.0 122.7 jit_solution(8717375190285457319)
XLA Ops:
  0.6 11.3 %all-to-all-start = ((f32[32,64,128]{2,1,0:T(8,128)}), f32[32,64,128]{2,1,0:T(8,128)S(1)}, u32[]{:S(2)}, u32[]{:S(2)}) async-start(f32[32,64,128]{2,1,0:T(8,128)} %bitcast.49), calls=%async_computation | async-start | bytes 2097152 | tf_op jit(solution)/shard_map/all_to_all | solution.py:88
  12.0 21.4 %shard_map.112 = f32[1024,128]{1,0:T(8,128)} custom-call(f32[1024,128]{1,0:T(8,128)} %bitcast.60, f32[128,128]{1,0:T(8,128)} %k_ref.1, s32[128,128]{1,0:T(8,128)} %f_ref.1), custom_call_target="tpu_custom_call" | custom-call | flops 12884901888 | bytes 1048576 | tf_op jit(solution)/shard_map/pallas_call | solution.py:57
  33.3 9.0 %all-to-all-done = f32[32,64,128]{2,1,0:T(8,128)S(1)} async-done(((f32[32,64,128]{2,1,0:T(8,128)}), f32[32,64,128]{2,1,0:T(8,128)S(1)}, u32[]{:S(2)}, u32[]{:S(2)}) %all-to-all-start) | async-done | bytes 1048608 | tf_op jit(solution)/shard_map/all_to_all | solution.py:88
  42.3 0.6 copy.58
  43.0 0.6 copy.59
  43.6 3.9 %all-to-all-start.1 = ((f32[32,32,128]{2,1,0:T(8,128)}), f32[32,32,128]{2,1,0:T(8,128)S(1)}, u32[]{:S(2)}, u32[]{:S(2)}) async-start(f32[32,32,128]{2,1,0:T(8,128)} %bitcast.5), calls=%async_computation.1 | async-start | bytes 1048576 | tf_op jit(solution)/shard_map/all_to_all | solution.py:88
  47.6 0.6 fusion.25
  50.8 15.3 %all-to-all-done.1 = f32[32,32,128]{2,1,0:T(8,128)S(1)} async-done(((f32[32,32,128]{2,1,0:T(8,128)}), f32[32,32,128]{2,1,0:T(8,128)S(1)}, u32[]{:S(2)}, u32[]{:S(2)}) %all-to-all-start.1) | async-done | bytes 524320 | tf_op jit(solution)/shard_map/all_to_all | solution.py:88
  66.1 0.2 maximum_maximum_fusion
  66.4 0.2 fusion.24
  66.6 0.2 constant_dynamic-slice_fusion
  66.7 0.1 pad_maximum_fusion
  66.8 2.4 %copy.62 = f32[2,512,3,128]{3,0,2,1:T(2,128)} copy(f32[2,512,3,128]{3,1,2,0:T(8,128)S(1)} %pad_maximum_fusion) | data formatting | bytes 3145728 | tf_op jit(solution)/shard_map/stack | solution.py:116
  69.2 4.7 %all-to-all-start.2 = ((f32[2,512,3,128]{3,0,2,1:T(2,128)}), f32[2,512,3,128]{3,0,2,1:T(2,128)S(1)}, u32[]{:S(2)}, u32[]{:S(2)}) async-start(f32[2,512,3,128]{3,0,2,1:T(2,128)} %copy.62), calls=%async_computation.2 | async-start | bytes 3145728 | tf_op jit(solution)/shard_map/all_to_all | solution.py:119
  74.0 1.9 %collective-permute-start.1 = (f32[128,16]{0,1:T(8,128)S(1)}, f32[128,16]{0,1:T(8,128)S(1)}, u32[]{:S(2)}, u32[]{:S(2)}) collective-permute-start(f32[128,16]{0,1:T(8,128)S(1)} %broadcast_multiply_fusion.1), channel_id=1, source_target_pairs={{0,32},{32,64},{64,96},{96,128},{128,160},{160,192},{192,224},{1,3... | collective-permute-start | bytes 24584 | tf_op jit(solution)/shard_map/ppermute | solution.py:83
  76.0 4.9 %collective-permute-start = (f32[128,32]{0,1:T(8,128)S(1)}, f32[128,32]{0,1:T(8,128)S(1)}, u32[]{:S(2)}, u32[]{:S(2)}) collective-permute-start(f32[128,32]{0,1:T(8,128)S(1)} %bitcast.58), channel_id=1, source_target_pairs={{0,32},{32,64},{64,96},{96,128},{128,160},{160,192},{192,224},{1,3... | collective-permute-start | bytes 49160 | tf_op jit(solution)/shard_map/ppermute | solution.py:83
  80.9 26.8 %collective-permute-done.1 = f32[128,16]{0,1:T(8,128)S(1)} collective-permute-done((f32[128,16]{0,1:T(8,128)S(1)}, f32[128,16]{0,1:T(8,128)S(1)}, u32[]{:S(2)}, u32[]{:S(2)}) %collective-permute-start.1) | collective-permute-done | bytes 8224 | tf_op jit(solution)/shard_map/ppermute | solution.py:83
  107.7 0.2 convolution_negate_fusion
  107.9 0.1 copy.66
  108.0 0.2 fusion
  108.3 0.2 fusion.2
  108.5 0.1 copy.65
  108.6 6.2 %all-to-all-done.2 = f32[2,512,3,128]{3,0,2,1:T(2,128)S(1)} async-done(((f32[2,512,3,128]{3,0,2,1:T(2,128)}), f32[2,512,3,128]{3,0,2,1:T(2,128)S(1)}, u32[]{:S(2)}, u32[]{:S(2)}) %all-to-all-start.2) | async-done | bytes 1572896 | tf_op jit(solution)/shard_map/all_to_all | solution.py:119
  114.8 0.1 copy.63
  114.9 0.2 copy.64
  115.2 0.8 multiply_reduce_fusion
  116.1 1.9 %collective-permute-start.2 = (f32[64,33]{0,1:T(8,128)S(1)}, f32[64,33]{0,1:T(8,128)S(1)}, u32[]{:S(2)}, u32[]{:S(2)}) collective-permute-start(f32[64,33]{0,1:T(8,128)S(1)} %pad_maximum_fusion.1), channel_id=1, source_target_pairs={{32,0},{64,32},{96,64},{128,96},{160,128},{192,160},{224,192},{33,... | collective-permute-start | bytes 25352 | tf_op jit(solution)/shard_map/ppermute | solution.py:83
  118.0 0.2 fusion.12
  118.3 1.5 %copy.69 = f32[64,16,2,128]{3,2,1,0:T(2,128)} copy(f32[64,16,2,128]{3,1,2,0:T(8,128)S(1)} %get-tuple-element.23) | data formatting | bytes 2097152
  119.8 2.0 %collective-permute-done.2 = f32[64,33]{0,1:T(8,128)S(1)} collective-permute-done((f32[64,33]{0,1:T(8,128)S(1)}, f32[64,33]{0,1:T(8,128)S(1)}, u32[]{:S(2)}, u32[]{:S(2)}) %collective-permute-start.2) | collective-permute-done | bytes 8480 | tf_op jit(solution)/shard_map/ppermute | solution.py:83
  121.8 0.2 convolution_add_fusion
  122.0 0.6 divide_subtract_fusion
  (30 shorter events, 0.4 us)
Async XLA Ops:
  0.6 41.7 %all-to-all-start = ((f32[32,64,128]{2,1,0:T(8,128)}), f32[32,64,128]{2,1,0:T(8,128)S(1)}, u32[]{:S(2)}, u32[]{:S(2)}) async-start(f32[32,64,128]{2,1,0:T(8,128)} %bitcast.49), calls=%async_computation | async-start | bytes 2097152 | tf_op jit(solution)/shard_map/all_to_all | solution.py:88
  43.0 4.5 %copy-start.5 = (s32[64]{0:T(128)S(1)}, s32[64]{0:T(128)}, u32[]{:S(2)}) copy-start(s32[64]{0:T(128)} %param.15) | copy-start | bytes 772
  43.6 22.5 %all-to-all-start.1 = ((f32[32,32,128]{2,1,0:T(8,128)}), f32[32,32,128]{2,1,0:T(8,128)S(1)}, u32[]{:S(2)}, u32[]{:S(2)}) async-start(f32[32,32,128]{2,1,0:T(8,128)} %bitcast.5), calls=%async_computation.1 | async-start | bytes 1048576 | tf_op jit(solution)/shard_map/all_to_all | solution.py:88
  69.2 4.7 %copy-start.2 = (f32[128,64]{0,1:T(8,128)S(1)}, f32[128,64]{0,1:T(8,128)}, u32[]{:S(2)}) copy-start(f32[128,64]{0,1:T(8,128)} %param.11) | copy-start | bytes 98308
  69.2 6.7 %copy-start.1 = (f32[128,2,64]{0,2,1:T(8,128)S(1)}, f32[128,2,64]{0,2,1:T(8,128)}, u32[]{:S(2)}) copy-start(f32[128,2,64]{0,2,1:T(8,128)} %param.12) | copy-start | bytes 196612
  69.2 11.7 %copy-start.4 = (s32[64]{0:T(128)S(1)}, s32[64]{0:T(128)}, u32[]{:S(2)}) copy-start(s32[64]{0:T(128)} %param.17) | copy-start | bytes 772
  69.2 38.8 %copy-start.3 = (f32[128]{0:T(128)S(1)}, f32[128]{0:T(128)}, u32[]{:S(2)}) copy-start(f32[128]{0:T(128)} %param.14) | copy-start | bytes 1540
  69.2 45.6 %all-to-all-start.2 = ((f32[2,512,3,128]{3,0,2,1:T(2,128)}), f32[2,512,3,128]{3,0,2,1:T(2,128)S(1)}, u32[]{:S(2)}, u32[]{:S(2)}) async-start(f32[2,512,3,128]{3,0,2,1:T(2,128)} %copy.62), calls=%async_computation.2 | async-start | bytes 3145728 | tf_op jit(solution)/shard_map/all_to_all | solution.py:119
  74.0 33.8 %collective-permute-start.1 = (f32[128,16]{0,1:T(8,128)S(1)}, f32[128,16]{0,1:T(8,128)S(1)}, u32[]{:S(2)}, u32[]{:S(2)}) collective-permute-start(f32[128,16]{0,1:T(8,128)S(1)} %broadcast_multiply_fusion.1), channel_id=1, source_target_pairs={{0,32},{32,64},{64,96},{96,128},{128,160},{160,192},{192,224},{1,3... | collective-permute-start | bytes 24584 | tf_op jit(solution)/shard_map/ppermute | solution.py:83
  76.0 32.3 %collective-permute-start = (f32[128,32]{0,1:T(8,128)S(1)}, f32[128,32]{0,1:T(8,128)S(1)}, u32[]{:S(2)}, u32[]{:S(2)}) collective-permute-start(f32[128,32]{0,1:T(8,128)S(1)} %bitcast.58), channel_id=1, source_target_pairs={{0,32},{32,64},{64,96},{96,128},{128,160},{160,192},{192,224},{1,3... | collective-permute-start | bytes 49160 | tf_op jit(solution)/shard_map/ppermute | solution.py:83
  115.2 0.8 copy-start
  116.1 5.7 %collective-permute-start.2 = (f32[64,33]{0,1:T(8,128)S(1)}, f32[64,33]{0,1:T(8,128)S(1)}, u32[]{:S(2)}, u32[]{:S(2)}) collective-permute-start(f32[64,33]{0,1:T(8,128)S(1)} %pad_maximum_fusion.1), channel_id=1, source_target_pairs={{32,0},{64,32},{96,64},{128,96},{160,128},{192,160},{224,192},{33,... | collective-permute-start | bytes 25352 | tf_op jit(solution)/shard_map/ppermute | solution.py:83

commit v9 on v8

--- a/solution.py
+++ b/solution.py
@@ -107,10 +107,12 @@
     whole = cells * az_count
     own = cycles // az_count
     turns = lax.dynamic_slice(cycle_shifts, (lax.axis_index("az") * own,), (own,))
+    ring_density = gathered(dust_density[:, :, None, :], az_count)
+    ring_density, dust_velocity = lax.optimization_barrier((ring_density, dust_velocity))
     ring_velocity = gathered(dust_velocity, az_count)
-    coag_local = coag(dust_density.reshape(cycles * cells, bins), kernel, fragment_bins)
-    coag_local, ring_velocity = lax.optimization_barrier((coag_local, ring_velocity))
-    ring_density = gathered(coag_local.reshape(cycles, cells, 1, bins), az_count)
+    ring_coag = coag(ring_density.reshape(own * whole, bins), kernel, fragment_bins)
+    ring_coag, ring_velocity = lax.optimization_barrier((ring_coag, ring_velocity))
+    ring_density = ring_coag.reshape(own, whole, 1, bins)
     rings = jnp.concatenate([ring_density, ring_velocity], axis=2)
     doubled = jnp.concatenate([rings, rings], axis=1)
     rings = jnp.stack(

time: 123 us -> 125 us (1.016)
  blocking collectives: 0 us -> 30.4 us
  waiting for transfers between devices: 59.3 us -> 40.6 us
  starting transfers between devices: 28.7 us -> 17.3 us
    all_to_all x0 -> x1, blocking collectives: none -> 30.4 us  [gathered(): flat = lax.all_to_all(block.reshape(-1, bins), 'az', 0, 0, tiled=True)]
    all_to_all x2 -> x1, waiting for transfers between devices: 24.3 us -> 5.37 us  [gathered(): flat = lax.all_to_all(block.reshape(-1, bins), 'az', 0, 0, tiled=True)]
    all_to_all x2 -> x1, starting transfers between devices: 15.2 us -> 3.93 us  [gathered(): flat = lax.all_to_all(block.reshape(-1, bins), 'az', 0, 0, tiled=True)]
  transfers between devices with their start and end apart: 6 -> 5, of which waited for: 5 -> 4; matrix products, arithmetic and copies ran while one was open for 3% -> 3% of each run, Pallas kernels for 17% -> 17%
where the time goes in v9:
time: 125 us; the launch traced here: 124 us
  waiting for transfers between devices  40.6 us (32%)
  blocking collectives  30.4 us (24%)
  Pallas kernels  21.4 us (17%)
  starting transfers between devices  17.3 us (14%)
  local copies, waits for them, and re-layouts  8.05 us (6%)
  between operations  3.52 us (3%)
  other arithmetic  2.08 us (2%)
    all_to_all x1, blocking collectives, gathered(): flat = lax.all_to_all(block.reshape(-1, bins), 'az', 0, 0, tiled=True)  30.4 us
    ppermute x3, waiting for transfers between devices, shifted(): return lax.ppermute(block, axis, route)  28.8 us
    pallas_call x1, Pallas kernels, coag(): pl.pallas_call(functools.partial(coag_kernel, group=group), grid=(1,), in...  21.4 us
    ppermute x3, starting transfers between devices, shifted(): return lax.ppermute(block, axis, route)  8.77 us
    all_to_all x1, waiting for transfers between devices, body(): state = lax.all_to_all(rings, 'az', 1, 0, tiled=True)  6.4 us
    all_to_all x1, waiting for transfers between devices, gathered(): flat = lax.all_to_all(block.reshape(-1, bins), 'az', 0, 0, tiled=True)  5.37 us
    all_to_all x1, starting transfers between devices, body(): state = lax.all_to_all(rings, 'az', 1, 0, tiled=True)  4.56 us
    all_to_all x1, starting transfers between devices, gathered(): flat = lax.all_to_all(block.reshape(-1, bins), 'az', 0, 0, tiled=True)  3.93 us
  transfers between devices with their start and end apart: 5, of which 4 were waited for; matrix products, arithmetic and copies ran while one was open for 3% of the time, Pallas kernels for 17%

profile of v9, /device:TPU:8, one launch (start us, length us, event | category | flops | bytes accessed | tf_op | source)
XLA Modules:
  0.0 124.1 jit_solution(17979264086206708577)
XLA Ops:
  0.6 30.4 %all_to_all.36 = f32[32,32,128]{2,1,0:T(8,128)S(1)} all-to-all(f32[32,32,128]{2,1,0:T(8,128)} %bitcast.50), channel_id=1, replica_groups=mesh['rad'=8,'az'=32] {'az'}, dimensions={0} | all-to-all | bytes 1048576 | tf_op jit(solution)/shard_map/all_to_all | solution.py:88
  31.0 0.8 copy.61
  31.9 3.9 %all-to-all-start.1 = ((f32[32,64,128]{2,1,0:T(8,128)}), f32[32,64,128]{2,1,0:T(8,128)S(1)}, u32[]{:S(2)}, u32[]{:S(2)}) async-start(f32[32,64,128]{2,1,0:T(8,128)} %bitcast.5), calls=%async_computation.1 | async-start | bytes 2097152 | tf_op jit(solution)/shard_map/all_to_all | solution.py:88
  35.9 0.6 fusion.25
  39.1 21.4 %shard_map.112 = f32[1024,128]{1,0:T(8,128)} custom-call(f32[1024,128]{1,0:T(8,128)} %bitcast.51, f32[128,128]{1,0:T(8,128)} %k_ref.1, s32[128,128]{1,0:T(8,128)} %f_ref.1), custom_call_target="tpu_custom_call" | custom-call | flops 12884901888 | bytes 1048576 | tf_op jit(solution)/shard_map/pallas_call | solution.py:57
  60.4 5.4 %all-to-all-done.1 = f32[32,64,128]{2,1,0:T(8,128)S(1)} async-done(((f32[32,64,128]{2,1,0:T(8,128)}), f32[32,64,128]{2,1,0:T(8,128)S(1)}, u32[]{:S(2)}, u32[]{:S(2)}) %all-to-all-start.1) | async-done | bytes 1048608 | tf_op jit(solution)/shard_map/all_to_all | solution.py:88
  65.8 0.6 copy.62
  66.4 0.6 copy.63
  67.1 0.4 copy-done.1
  67.5 0.2 maximum_maximum_fusion
  67.7 0.2 fusion.24
  67.9 0.1 constant_dynamic-slice_fusion
  68.0 0.1 pad_maximum_fusion
  68.2 2.4 %copy.65 = f32[2,512,3,128]{3,0,2,1:T(2,128)} copy(f32[2,512,3,128]{3,1,2,0:T(8,128)S(1)} %pad_maximum_fusion) | data formatting | bytes 3145728 | tf_op jit(solution)/shard_map/stack | solution.py:118
  70.5 4.6 %all-to-all-start.2 = ((f32[2,512,3,128]{3,0,2,1:T(2,128)}), f32[2,512,3,128]{3,0,2,1:T(2,128)S(1)}, u32[]{:S(2)}, u32[]{:S(2)}) async-start(f32[2,512,3,128]{3,0,2,1:T(2,128)} %copy.65), calls=%async_computation.2 | async-start | bytes 3145728 | tf_op jit(solution)/shard_map/all_to_all | solution.py:121
  75.1 2.4 %collective-permute-start.1 = (f32[128,16]{0,1:T(8,128)S(1)}, f32[128,16]{0,1:T(8,128)S(1)}, u32[]{:S(2)}, u32[]{:S(2)}) collective-permute-start(f32[128,16]{0,1:T(8,128)S(1)} %broadcast_multiply_fusion.1), channel_id=1, source_target_pairs={{0,32},{32,64},{64,96},{96,128},{128,160},{160,192},{192,224},{1,3... | collective-permute-start | bytes 24584 | tf_op jit(solution)/shard_map/ppermute | solution.py:83
  77.6 4.5 %collective-permute-start = (f32[128,32]{0,1:T(8,128)S(1)}, f32[128,32]{0,1:T(8,128)S(1)}, u32[]{:S(2)}, u32[]{:S(2)}) collective-permute-start(f32[128,32]{0,1:T(8,128)S(1)} %bitcast.60), channel_id=1, source_target_pairs={{0,32},{32,64},{64,96},{96,128},{128,160},{160,192},{192,224},{1,3... | collective-permute-start | bytes 49160 | tf_op jit(solution)/shard_map/ppermute | solution.py:83
  82.1 26.8 %collective-permute-done.1 = f32[128,16]{0,1:T(8,128)S(1)} collective-permute-done((f32[128,16]{0,1:T(8,128)S(1)}, f32[128,16]{0,1:T(8,128)S(1)}, u32[]{:S(2)}, u32[]{:S(2)}) %collective-permute-start.1) | collective-permute-done | bytes 8224 | tf_op jit(solution)/shard_map/ppermute | solution.py:83
  109.0 0.2 convolution_negate_fusion
  109.3 0.2 fusion
  109.5 0.2 fusion.2
  109.7 0.1 copy.68
  109.8 6.4 %all-to-all-done.2 = f32[2,512,3,128]{3,0,2,1:T(2,128)S(1)} async-done(((f32[2,512,3,128]{3,0,2,1:T(2,128)}), f32[2,512,3,128]{3,0,2,1:T(2,128)S(1)}, u32[]{:S(2)}, u32[]{:S(2)}) %all-to-all-start.2) | async-done | bytes 1572896 | tf_op jit(solution)/shard_map/all_to_all | solution.py:121
  116.2 0.1 copy.66
  116.3 0.2 copy.67
  116.6 0.8 multiply_reduce_fusion
  117.5 1.9 %collective-permute-start.2 = (f32[64,33]{0,1:T(8,128)S(1)}, f32[64,33]{0,1:T(8,128)S(1)}, u32[]{:S(2)}, u32[]{:S(2)}) collective-permute-start(f32[64,33]{0,1:T(8,128)S(1)} %pad_maximum_fusion.1), channel_id=1, source_target_pairs={{32,0},{64,32},{96,64},{128,96},{160,128},{192,160},{224,192},{33,... | collective-permute-start | bytes 25352 | tf_op jit(solution)/shard_map/ppermute | solution.py:83
  119.5 0.2 fusion.12
  119.7 1.5 %copy.72 = f32[64,16,2,128]{3,2,1,0:T(2,128)} copy(f32[64,16,2,128]{3,1,2,0:T(8,128)S(1)} %get-tuple-element.27) | data formatting | bytes 2097152
  121.2 2.0 %collective-permute-done.2 = f32[64,33]{0,1:T(8,128)S(1)} collective-permute-done((f32[64,33]{0,1:T(8,128)S(1)}, f32[64,33]{0,1:T(8,128)S(1)}, u32[]{:S(2)}, u32[]{:S(2)}) %collective-permute-start.2) | collective-permute-done | bytes 8480 | tf_op jit(solution)/shard_map/ppermute | solution.py:83
  123.2 0.2 convolution_add_fusion
  123.5 0.6 divide_subtract_fusion
  (31 shorter events, 0.5 us)
Async XLA Ops:
  31.0 4.8 %copy-start.6 = (s32[64]{0:T(128)S(1)}, s32[64]{0:T(128)}, u32[]{:S(2)}) copy-start(s32[64]{0:T(128)} %param.15) | copy-start | bytes 772
  31.9 34.0 %all-to-all-start.1 = ((f32[32,64,128]{2,1,0:T(8,128)}), f32[32,64,128]{2,1,0:T(8,128)S(1)}, u32[]{:S(2)}, u32[]{:S(2)}) async-start(f32[32,64,128]{2,1,0:T(8,128)} %bitcast.5), calls=%async_computation.1 | async-start | bytes 2097152 | tf_op jit(solution)/shard_map/all_to_all | solution.py:88
  66.4 1.0 copy-start.1
  70.5 4.6 %copy-start.3 = (f32[128,64]{0,1:T(8,128)S(1)}, f32[128,64]{0,1:T(8,128)}, u32[]{:S(2)}) copy-start(f32[128,64]{0,1:T(8,128)} %param.11) | copy-start | bytes 98308
  70.5 7.0 %copy-start.2 = (f32[128,2,64]{0,2,1:T(8,128)S(1)}, f32[128,2,64]{0,2,1:T(8,128)}, u32[]{:S(2)}) copy-start(f32[128,2,64]{0,2,1:T(8,128)} %param.12) | copy-start | bytes 196612
  70.5 11.6 %copy-start.5 = (s32[64]{0:T(128)S(1)}, s32[64]{0:T(128)}, u32[]{:S(2)}) copy-start(s32[64]{0:T(128)} %param.17) | copy-start | bytes 772
  70.5 38.7 %copy-start.4 = (f32[128]{0:T(128)S(1)}, f32[128]{0:T(128)}, u32[]{:S(2)}) copy-start(f32[128]{0:T(128)} %param.14) | copy-start | bytes 1540
  70.5 45.7 %all-to-all-start.2 = ((f32[2,512,3,128]{3,0,2,1:T(2,128)}), f32[2,512,3,128]{3,0,2,1:T(2,128)S(1)}, u32[]{:S(2)}, u32[]{:S(2)}) async-start(f32[2,512,3,128]{3,0,2,1:T(2,128)} %copy.65), calls=%async_computation.2 | async-start | bytes 3145728 | tf_op jit(solution)/shard_map/all_to_all | solution.py:121
  75.1 33.8 %collective-permute-start.1 = (f32[128,16]{0,1:T(8,128)S(1)}, f32[128,16]{0,1:T(8,128)S(1)}, u32[]{:S(2)}, u32[]{:S(2)}) collective-permute-start(f32[128,16]{0,1:T(8,128)S(1)} %broadcast_multiply_fusion.1), channel_id=1, source_target_pairs={{0,32},{32,64},{64,96},{96,128},{128,160},{160,192},{192,224},{1,3... | collective-permute-start | bytes 24584 | tf_op jit(solution)/shard_map/ppermute | solution.py:83
  77.6 31.9 %collective-permute-start = (f32[128,32]{0,1:T(8,128)S(1)}, f32[128,32]{0,1:T(8,128)S(1)}, u32[]{:S(2)}, u32[]{:S(2)}) collective-permute-start(f32[128,32]{0,1:T(8,128)S(1)} %bitcast.60), channel_id=1, source_target_pairs={{0,32},{32,64},{64,96},{96,128},{128,160},{160,192},{192,224},{1,3... | collective-permute-start | bytes 49160 | tf_op jit(solution)/shard_map/ppermute | solution.py:83
  116.6 0.8 copy-start
  117.5 5.7 %collective-permute-start.2 = (f32[64,33]{0,1:T(8,128)S(1)}, f32[64,33]{0,1:T(8,128)S(1)}, u32[]{:S(2)}, u32[]{:S(2)}) collective-permute-start(f32[64,33]{0,1:T(8,128)S(1)} %pad_maximum_fusion.1), channel_id=1, source_target_pairs={{32,0},{64,32},{96,64},{128,96},{160,128},{192,160},{224,192},{33,... | collective-permute-start | bytes 25352 | tf_op jit(solution)/shard_map/ppermute | solution.py:83

commit v10 on v8

--- a/solution.py
+++ b/solution.py
@@ -107,22 +107,25 @@
     whole = cells * az_count
     own = cycles // az_count
     turns = lax.dynamic_slice(cycle_shifts, (lax.axis_index("az") * own,), (own,))
-    ring_velocity = gathered(dust_velocity, az_count)
-    coag_local = coag(dust_density.reshape(cycles * cells, bins), kernel, fragment_bins)
-    coag_local, ring_velocity = lax.optimization_barrier((coag_local, ring_velocity))
-    ring_density = gathered(coag_local.reshape(cycles, cells, 1, bins), az_count)
-    rings = jnp.concatenate([ring_density, ring_velocity], axis=2)
-    doubled = jnp.concatenate([rings, rings], axis=1)
-    rings = jnp.stack(
-        [lax.dynamic_slice_in_dim(doubled[c], whole - turns[c], whole, 0) for c in range(own)]
-    )
-    state = lax.all_to_all(rings, "az", 1, 0, tiled=True)
-    coag_density = state[:, :, 0, :]
-    moved_velocity = state[:, :, 1:, :]
+    state = jnp.concatenate([dust_density[:, :, None, :], dust_velocity], axis=2)
+    rings = gathered(state, az_count)
+
+    def rolled(ring):
+        doubled = jnp.concatenate([ring, ring], axis=1)
+        return jnp.stack(
+            [lax.dynamic_slice_in_dim(doubled[c], whole - turns[c], whole, 0) for c in range(own)]
+        )
+
+    moved_velocity = lax.all_to_all(rolled(rings[:, :, 1:, :]), "az", 1, 0, tiled=True)
+    ring_coag = coag(rolled(rings[:, :, 0, :]).reshape(own * whole, bins), kernel, fragment_bins)
     coarse_density = gas_density.reshape(gas_cycles, cells, 4).mean(-1)
     coarse_velocity = (
         gas_velocity.reshape(gas_cycles, 2, cells, 4).mean(-1).reshape(gas_cycles, 2 * cells)
     )
+    ring_coag, moved_velocity, coarse_density, coarse_velocity = lax.optimization_barrier(
+        (ring_coag, moved_velocity, coarse_density, coarse_velocity)
+    )
+    coag_density = lax.all_to_all(ring_coag.reshape(own, whole, bins), "az", 1, 0, tiled=True)
     prev_density, prev_velocity = shifted((coarse_density, coarse_velocity), "rad", 1)
     near_density = jnp.concatenate([prev_density, coarse_density], axis=0)
     near_velocity = jnp.concatenate([prev_velocity, coarse_velocity], axis=0)

time: 123 us -> 131 us (1.065)
  other arithmetic: 2.08 us -> 7.75 us
  local copies, waits for them, and re-layouts: 6.86 us -> 8.73 us
    ppermute x3, waiting for transfers between devices: 28.8 us -> 7.9 us  [shifted(): return lax.ppermute(block, axis, route)]
    all_to_all x2 -> x1, waiting for transfers between devices: 24.3 us -> 38 us  [gathered(): flat = lax.all_to_all(block.reshape(-1, bins), 'az', 0, 0, tiled=True)]
    all_to_all x1 -> x2, waiting for transfers between devices: 6.19 us -> 14 us  [the longest x1 7.61 us: body(): lax.all_to_all(rolled(rings[:, :, 1:, :]), 'az', 1, 0, tiled=True)]
    all_to_all x2 -> x1, starting transfers between devices: 15.2 us -> 11.4 us  [gathered(): flat = lax.all_to_all(block.reshape(-1, bins), 'az', 0, 0, tiled=True)]
    all_to_all x1 -> x2, starting transfers between devices: 4.67 us -> 7.99 us  [the longest x1 4.05 us: body(): lax.all_to_all(ring_coag.reshape(own, whole, bins), 'az', 1, 0, tiled=True)]
    concatenate x1 -> x3, other arithmetic: 0.2 us -> 2.76 us  [the longest x1 2.31 us: body(): jnp.concatenate([dust_density[:, :, None, :], dust_velocity], axis=2)]
    reduce_sum x1, other arithmetic: 0.8 us -> 3.1 us  [body(): jnp.sum(coag_density[:, :, None, :] * (velocity_out - moved_velocity), ax...]
    all_to_all x1 -> x2, local copies, waits for them, and re-layouts: 0.61 us -> 2.58 us  [gathered(): flat = lax.all_to_all(block.reshape(-1, bins), 'az', 0, 0, tiled=True)]
  transfers between devices with their start and end apart: 6 -> 6, of which waited for: 5 -> 5; matrix products, arithmetic and copies ran while one was open for 3% -> 2% of each run, Pallas kernels for 17% -> 16%
where the time goes in v10:
time: 131 us; the launch traced here: 130 us
  waiting for transfers between devices  59.9 us (46%)
  starting transfers between devices  28.2 us (22%)
  Pallas kernels  21.4 us (16%)
  local copies, waits for them, and re-layouts  8.73 us (7%)
  other arithmetic  7.75 us (6%)
  between operations  3.56 us (3%)
    all_to_all x1, waiting for transfers between devices, gathered(): flat = lax.all_to_all(block.reshape(-1, bins), 'az', 0, 0, tiled=True)  38 us
    pallas_call x1, Pallas kernels, coag(): pl.pallas_call(functools.partial(coag_kernel, group=group), grid=(1,), in...  21.4 us
    all_to_all x1, starting transfers between devices, gathered(): flat = lax.all_to_all(block.reshape(-1, bins), 'az', 0, 0, tiled=True)  11.4 us
    ppermute x3, starting transfers between devices, shifted(): return lax.ppermute(block, axis, route)  8.75 us
    ppermute x3, waiting for transfers between devices, shifted(): return lax.ppermute(block, axis, route)  7.9 us
    all_to_all x1, waiting for transfers between devices, body(): lax.all_to_all(rolled(rings[:, :, 1:, :]), 'az', 1, 0, tiled=True)  7.61 us
    all_to_all x1, waiting for transfers between devices, body(): lax.all_to_all(ring_coag.reshape(own, whole, bins), 'az', 1, 0, tiled=True)  6.39 us
    all_to_all x1, starting transfers between devices, body(): lax.all_to_all(ring_coag.reshape(own, whole, bins), 'az', 1, 0, tiled=True)  4.05 us
  transfers between devices with their start and end apart: 6, of which 5 were waited for; matrix products, arithmetic and copies ran while one was open for 2% of the time, Pallas kernels for 16%

profile of v10, /device:TPU:8, one launch (start us, length us, event | category | flops | bytes accessed | tf_op | source)
XLA Modules:
  0.0 130.4 jit_solution(5078504514250389236)
XLA Ops:
  0.6 2.3 %pad_maximum_fusion = f32[64,16,3,128]{3,2,1,0:T(4,128)S(1)} fusion(f32[64,16,2,128]{3,2,1,0:T(2,128)} %param.10, f32[64,16,1,128]{3,2,1,0:T(1,128)} %bitcast.48), kind=kLoop, calls=%fused_computation | loop fusion | flops 393216 | bytes 3145728 | tf_op jit(solution)/shard_map/concatenate | solution.py:110
  2.9 1.7 %all_to_all.32 = f32[32,96,128]{2,1,0:T(8,128)} reshape(f32[64,16,3,128]{3,2,1,0:T(4,128)S(1)} %pad_maximum_fusion) | data formatting | bytes 3145728 | tf_op jit(solution)/shard_map/all_to_all | solution.py:88
  4.6 11.4 %all-to-all-start = ((f32[32,96,128]{2,1,0:T(8,128)}), f32[32,96,128]{2,1,0:T(8,128)S(1)}, u32[]{:S(2)}, u32[]{:S(2)}) async-start(f32[32,96,128]{2,1,0:T(8,128)} %all_to_all.32), calls=%async_computation | async-start | bytes 3145728 | tf_op jit(solution)/shard_map/all_to_all | solution.py:88
  16.2 0.6 fusion.26
  19.5 38.0 %all-to-all-done = f32[32,96,128]{2,1,0:T(8,128)S(1)} async-done(((f32[32,96,128]{2,1,0:T(8,128)}), f32[32,96,128]{2,1,0:T(8,128)S(1)}, u32[]{:S(2)}, u32[]{:S(2)}) %all-to-all-start) | async-done | bytes 1572896 | tf_op jit(solution)/shard_map/all_to_all | solution.py:88
  57.5 0.9 copy.39
  58.4 0.9 copy.40
  59.5 0.3 fusion.1
  59.9 1.8 %copy.41 = f32[2,512,2,128]{3,2,0,1:T(2,128)} copy(f32[2,512,2,128]{3,1,2,0:T(8,128)S(1)} %pad_maximum_fusion.1) | data formatting | bytes 2097152 | tf_op jit(solution)/shard_map/stack | solution.py:115
  61.6 3.9 %all-to-all-start.1 = ((f32[2,512,2,128]{3,2,0,1:T(2,128)}), f32[2,512,2,128]{3,2,0,1:T(2,128)S(1)}, u32[]{:S(2)}, u32[]{:S(2)}) async-start(f32[2,512,2,128]{3,2,0,1:T(2,128)} %copy.41), calls=%async_computation.1 | async-start | bytes 2097152 | tf_op jit(solution)/shard_map/all_to_all | solution.py:119
  65.7 0.2 fusion.2
  65.9 0.8 pad_maximum_fusion.2
  66.8 21.4 %shard_map.112 = f32[1024,128]{1,0:T(8,128)} custom-call(f32[1024,128]{1,0:T(8,128)} %bitcast.50, f32[128,128]{1,0:T(8,128)} %k_ref.1, s32[128,128]{1,0:T(8,128)} %f_ref.1), custom_call_target="tpu_custom_call" | custom-call | flops 12884901888 | bytes 1048576 | tf_op jit(solution)/shard_map/pallas_call | solution.py:57
  88.1 7.6 %all-to-all-done.1 = f32[2,512,2,128]{3,2,0,1:T(2,128)S(1)} async-done(((f32[2,512,2,128]{3,2,0,1:T(2,128)}), f32[2,512,2,128]{3,2,0,1:T(2,128)S(1)}, u32[]{:S(2)}, u32[]{:S(2)}) %all-to-all-start.1) | async-done | bytes 1048608 | tf_op jit(solution)/shard_map/all_to_all | solution.py:119
  95.8 0.5 copy.42
  96.3 1.2 copy.43
  97.5 4.1 %all-to-all-start.2 = ((f32[2,512,128]{2,0,1:T(2,128)}), f32[2,512,128]{2,0,1:T(2,128)S(1)}, u32[]{:S(2)}, u32[]{:S(2)}) async-start(f32[2,512,128]{2,0,1:T(2,128)} %copy.43), calls=%async_computation.2 | async-start | bytes 1048576 | tf_op jit(solution)/shard_map/all_to_all | solution.py:128
  101.5 2.3 %collective-permute-start.1 = (f32[128,16]{0,1:T(8,128)S(1)}, f32[128,16]{0,1:T(8,128)S(1)}, u32[]{:S(2)}, u32[]{:S(2)}) collective-permute-start(f32[128,16]{0,1:T(8,128)S(1)} %broadcast_multiply_fusion.1), channel_id=1, source_target_pairs={{0,32},{32,64},{64,96},{96,128},{128,160},{160,192},{192,224},{1,3... | collective-permute-start | bytes 24584 | tf_op jit(solution)/shard_map/ppermute | solution.py:83
  103.9 4.5 %collective-permute-start = (f32[128,32]{0,1:T(8,128)S(1)}, f32[128,32]{0,1:T(8,128)S(1)}, u32[]{:S(2)}, u32[]{:S(2)}) collective-permute-start(f32[128,32]{0,1:T(8,128)S(1)} %bitcast.59), channel_id=1, source_target_pairs={{0,32},{32,64},{64,96},{96,128},{128,160},{160,192},{192,224},{1,3... | collective-permute-start | bytes 49160 | tf_op jit(solution)/shard_map/ppermute | solution.py:83
  108.4 4.4 %collective-permute-done.1 = f32[128,16]{0,1:T(8,128)S(1)} collective-permute-done((f32[128,16]{0,1:T(8,128)S(1)}, f32[128,16]{0,1:T(8,128)S(1)}, u32[]{:S(2)}, u32[]{:S(2)}) %collective-permute-start.1) | collective-permute-done | bytes 8224 | tf_op jit(solution)/shard_map/ppermute | solution.py:83
  112.8 0.2 convolution_negate_fusion
  113.1 0.2 fusion
  113.4 0.2 fusion.4
  113.6 0.3 copy.45
  113.9 6.4 %all-to-all-done.2 = f32[2,512,128]{2,0,1:T(2,128)S(1)} async-done(((f32[2,512,128]{2,0,1:T(2,128)}), f32[2,512,128]{2,0,1:T(2,128)S(1)}, u32[]{:S(2)}, u32[]{:S(2)}) %all-to-all-start.2) | async-done | bytes 524320 | tf_op jit(solution)/shard_map/all_to_all | solution.py:128
  120.4 3.1 %multiply_reduce_fusion = (f32[64,16,2]{2,1,0:T(8,128)S(1)}, f32[64,16,2,128]{3,2,1,0:T(2,128)}) fusion(f32[64,16,2,128]{3,2,1,0:T(2,128)S(1)} %bitcast.44, f32[64,16,128]{2,1,0:T(8,128)S(1)} %bitcast.46, f32[64,16,128]{2,1,0:T(8,128)S(1)} %fusion, f32[64,16,2]{2,1,0:T(8,128)S(1)} %copy.45), kind=kLoop, calls=%fused_computation.10 | loop fusion | flops 1570816 | bytes 3162112 | tf_op jit(solution)/shard_map/reduce_sum | solution.py:140
  123.5 0.3 copy.47
  123.8 1.9 %collective-permute-start.2 = (f32[64,33]{0,1:T(8,128)S(1)}, f32[64,33]{0,1:T(8,128)S(1)}, u32[]{:S(2)}, u32[]{:S(2)}) collective-permute-start(f32[64,33]{0,1:T(8,128)S(1)} %pad_maximum_fusion.3), channel_id=1, source_target_pairs={{32,0},{64,32},{96,64},{128,96},{160,128},{192,160},{224,192},{33,... | collective-permute-start | bytes 25352 | tf_op jit(solution)/shard_map/ppermute | solution.py:83
  125.7 0.2 fusion.14
  126.0 3.5 %collective-permute-done.2 = f32[64,33]{0,1:T(8,128)S(1)} collective-permute-done((f32[64,33]{0,1:T(8,128)S(1)}, f32[64,33]{0,1:T(8,128)S(1)}, u32[]{:S(2)}, u32[]{:S(2)}) %collective-permute-start.2) | collective-permute-done | bytes 8480 | tf_op jit(solution)/shard_map/ppermute | solution.py:83
  129.5 0.2 convolution_add_fusion
  129.7 0.6 divide_subtract_fusion
  (36 shorter events, 0.8 us)
Async XLA Ops:
  4.6 11.5 %copy-start.6 = (s32[64]{0:T(128)S(1)}, s32[64]{0:T(128)}, u32[]{:S(2)}) copy-start(s32[64]{0:T(128)} %param.15) | copy-start | bytes 772
  4.6 14.7 %copy-start.3 = (f32[128,64]{0,1:T(8,128)S(1)}, f32[128,64]{0,1:T(8,128)}, u32[]{:S(2)}) copy-start(f32[128,64]{0,1:T(8,128)} %param.11) | copy-start | bytes 98308
  4.6 14.8 %copy-start.2 = (f32[128,2,64]{0,2,1:T(8,128)S(1)}, f32[128,2,64]{0,2,1:T(8,128)}, u32[]{:S(2)}) copy-start(f32[128,2,64]{0,2,1:T(8,128)} %param.12) | copy-start | bytes 196612
  4.6 52.9 %all-to-all-start = ((f32[32,96,128]{2,1,0:T(8,128)}), f32[32,96,128]{2,1,0:T(8,128)S(1)}, u32[]{:S(2)}, u32[]{:S(2)}) async-start(f32[32,96,128]{2,1,0:T(8,128)} %all_to_all.32), calls=%async_computation | async-start | bytes 3145728 | tf_op jit(solution)/shard_map/all_to_all | solution.py:88
  61.6 34.1 %all-to-all-start.1 = ((f32[2,512,2,128]{3,2,0,1:T(2,128)}), f32[2,512,2,128]{3,2,0,1:T(2,128)S(1)}, u32[]{:S(2)}, u32[]{:S(2)}) async-start(f32[2,512,2,128]{3,2,0,1:T(2,128)} %copy.41), calls=%async_computation.1 | async-start | bytes 2097152 | tf_op jit(solution)/shard_map/all_to_all | solution.py:119
  88.1 8.1 %copy-start.1 = (f32[1024,128]{1,0:T(8,128)S(1)}, f32[1024,128]{1,0:T(8,128)}, u32[]{:S(2)}) copy-start(f32[1024,128]{1,0:T(8,128)} %shard_map.112) | copy-start | bytes 1572868
  95.7 5.8 %copy-start.5 = (s32[64]{0:T(128)S(1)}, s32[64]{0:T(128)}, u32[]{:S(2)}) copy-start(s32[64]{0:T(128)} %param.17) | copy-start | bytes 772
  95.8 17.4 %copy-start.4 = (f32[128]{0:T(128)S(1)}, f32[128]{0:T(128)}, u32[]{:S(2)}) copy-start(f32[128]{0:T(128)} %param.14) | copy-start | bytes 1540
  97.5 22.9 %all-to-all-start.2 = ((f32[2,512,128]{2,0,1:T(2,128)}), f32[2,512,128]{2,0,1:T(2,128)S(1)}, u32[]{:S(2)}, u32[]{:S(2)}) async-start(f32[2,512,128]{2,0,1:T(2,128)} %copy.43), calls=%async_computation.2 | async-start | bytes 1048576 | tf_op jit(solution)/shard_map/all_to_all | solution.py:128
  101.5 11.3 %collective-permute-start.1 = (f32[128,16]{0,1:T(8,128)S(1)}, f32[128,16]{0,1:T(8,128)S(1)}, u32[]{:S(2)}, u32[]{:S(2)}) collective-permute-start(f32[128,16]{0,1:T(8,128)S(1)} %broadcast_multiply_fusion.1), channel_id=1, source_target_pairs={{0,32},{32,64},{64,96},{96,128},{128,160},{160,192},{192,224},{1,3... | collective-permute-start | bytes 24584 | tf_op jit(solution)/shard_map/ppermute | solution.py:83
  103.9 9.5 %collective-permute-start = (f32[128,32]{0,1:T(8,128)S(1)}, f32[128,32]{0,1:T(8,128)S(1)}, u32[]{:S(2)}, u32[]{:S(2)}) collective-permute-start(f32[128,32]{0,1:T(8,128)S(1)} %bitcast.59), channel_id=1, source_target_pairs={{0,32},{32,64},{64,96},{96,128},{128,160},{160,192},{192,224},{1,3... | collective-permute-start | bytes 49160 | tf_op jit(solution)/shard_map/ppermute | solution.py:83
  120.4 3.1 %copy-start = (f32[32,2,16,128]{3,2,1,0:T(8,128)}, f32[32,2,16,128]{3,2,1,0:T(8,128)S(1)}, u32[]{:S(2)}) copy-start(f32[32,2,16,128]{3,2,1,0:T(8,128)S(1)} %copy.44) | copy-start | bytes 1572868
  123.8 5.7 %collective-permute-start.2 = (f32[64,33]{0,1:T(8,128)S(1)}, f32[64,33]{0,1:T(8,128)S(1)}, u32[]{:S(2)}, u32[]{:S(2)}) collective-permute-start(f32[64,33]{0,1:T(8,128)S(1)} %pad_maximum_fusion.3), channel_id=1, source_target_pairs={{32,0},{64,32},{96,64},{128,96},{160,128},{192,160},{224,192},{33,... | collective-permute-start | bytes 25352 | tf_op jit(solution)/shard_map/ppermute | solution.py:83

commit v11 on v8

--- a/solution.py
+++ b/solution.py
@@ -83,11 +83,14 @@
     return lax.ppermute(block, axis, route)
 
 
-def gathered(block, count):
-    cycles, cells, channels, bins = block.shape
-    flat = lax.all_to_all(block.reshape(-1, bins), "az", 0, 0, tiled=True)
-    parts = flat.reshape(count, cycles // count, cells, channels, bins)
-    return jnp.transpose(parts, (1, 0, 2, 3, 4)).reshape(cycles // count, count * cells, channels, bins)
+def sent(block):
+    return lax.all_to_all(block.reshape(-1, block.shape[-1]), "az", 0, 0, tiled=True)
+
+
+def arranged(flat, cycles, cells, count):
+    bins = flat.shape[-1]
+    parts = flat.reshape(count, cycles // count, cells, -1, bins)
+    return jnp.transpose(parts, (1, 0, 2, 3, 4)).reshape(cycles // count, count * cells, -1, bins)
 
 
 def body(
@@ -107,10 +110,13 @@
     whole = cells * az_count
     own = cycles // az_count
     turns = lax.dynamic_slice(cycle_shifts, (lax.axis_index("az") * own,), (own,))
-    ring_velocity = gathered(dust_velocity, az_count)
+    flat_velocity = sent(dust_velocity)
     coag_local = coag(dust_density.reshape(cycles * cells, bins), kernel, fragment_bins)
-    coag_local, ring_velocity = lax.optimization_barrier((coag_local, ring_velocity))
-    ring_density = gathered(coag_local.reshape(cycles, cells, 1, bins), az_count)
+    coag_local, flat_velocity = lax.optimization_barrier((coag_local, flat_velocity))
+    flat_density = sent(coag_local)
+    flat_density, flat_velocity = lax.optimization_barrier((flat_density, flat_velocity))
+    ring_velocity = arranged(flat_velocity, cycles, cells, az_count)
+    ring_density = arranged(flat_density, cycles, cells, az_count)
     rings = jnp.concatenate([ring_density, ring_velocity], axis=2)
     doubled = jnp.concatenate([rings, rings], axis=1)
     rings = jnp.stack(

time: 123 us -> 122 us (level)
  transfers between devices with their start and end apart: 6 -> 6, of which waited for: 5 -> 5; matrix products, arithmetic and copies ran while one was open for 3% -> 3% of each run, Pallas kernels for 17% -> 18%
where the time goes in v11:
time: 122 us
  waiting for transfers between devices  59.3 us (49%)
  starting transfers between devices  28.6 us (23%)
  Pallas kernels  21.4 us (18%)
  local copies, waits for them, and re-layouts  5.72 us (5%)
  between operations  3.54 us (3%)
  other arithmetic  2.08 us (2%)
    ppermute x3, waiting for transfers between devices, shifted(): return lax.ppermute(block, axis, route)  28.8 us
    all_to_all x2, waiting for transfers between devices, sent(): lax.all_to_all(block.reshape(-1, block.shape[-1]), 'az', 0, 0, tiled=True)  24.3 us
    pallas_call x1, Pallas kernels, coag(): pl.pallas_call(functools.partial(coag_kernel, group=group), grid=(1,), in...  21.4 us
    all_to_all x2, starting transfers between devices, sent(): lax.all_to_all(block.reshape(-1, block.shape[-1]), 'az', 0, 0, tiled=True)  15.2 us
    ppermute x3, starting transfers between devices, shifted(): return lax.ppermute(block, axis, route)  8.77 us
    all_to_all x1, waiting for transfers between devices, body(): state = lax.all_to_all(rings, 'az', 1, 0, tiled=True)  6.21 us
    all_to_all x1, starting transfers between devices, body(): state = lax.all_to_all(rings, 'az', 1, 0, tiled=True)  4.65 us
  transfers between devices with their start and end apart: 6, of which 5 were waited for; matrix products, arithmetic and copies ran while one was open for 3% of the time, Pallas kernels for 18%

profile of v11, /device:TPU:8, one launch (start us, length us, event | category | flops | bytes accessed | tf_op | source)
XLA Modules:
  0.0 121.5 jit_solution(16454102953061699743)
XLA Ops:
  0.6 11.3 %all-to-all-start = ((f32[32,64,128]{2,1,0:T(8,128)}), f32[32,64,128]{2,1,0:T(8,128)S(1)}, u32[]{:S(2)}, u32[]{:S(2)}) async-start(f32[32,64,128]{2,1,0:T(8,128)} %bitcast.51), calls=%async_computation | async-start | bytes 2097152 | tf_op jit(solution)/shard_map/all_to_all | solution.py:87
  12.0 21.4 %shard_map.112 = f32[1024,128]{1,0:T(8,128)} custom-call(f32[1024,128]{1,0:T(8,128)} %bitcast.63, f32[128,128]{1,0:T(8,128)} %k_ref.1, s32[128,128]{1,0:T(8,128)} %f_ref.1), custom_call_target="tpu_custom_call" | custom-call | flops 12884901888 | bytes 1048576 | tf_op jit(solution)/shard_map/pallas_call | solution.py:57
  33.3 9.0 %all-to-all-done = f32[32,64,128]{2,1,0:T(8,128)S(1)} async-done(((f32[32,64,128]{2,1,0:T(8,128)}), f32[32,64,128]{2,1,0:T(8,128)S(1)}, u32[]{:S(2)}, u32[]{:S(2)}) %all-to-all-start) | async-done | bytes 1048608 | tf_op jit(solution)/shard_map/all_to_all | solution.py:87
  42.3 3.9 %all-to-all-start.1 = ((f32[32,32,128]{2,1,0:T(8,128)}), f32[32,32,128]{2,1,0:T(8,128)S(1)}, u32[]{:S(2)}, u32[]{:S(2)}) async-start(f32[32,32,128]{2,1,0:T(8,128)} %bitcast.52), calls=%async_computation.1 | async-start | bytes 1048576 | tf_op jit(solution)/shard_map/all_to_all | solution.py:87
  46.3 0.1 dynamic_slice.9
  46.3 0.6 fusion.25
  49.5 15.3 %all-to-all-done.1 = f32[32,32,128]{2,1,0:T(8,128)S(1)} async-done(((f32[32,32,128]{2,1,0:T(8,128)}), f32[32,32,128]{2,1,0:T(8,128)S(1)}, u32[]{:S(2)}, u32[]{:S(2)}) %all-to-all-start.1) | async-done | bytes 524320 | tf_op jit(solution)/shard_map/all_to_all | solution.py:87
  64.9 0.1 copy.49
  65.0 0.2 maximum_maximum_fusion
  65.2 0.2 fusion.24
  65.4 0.2 constant_dynamic-slice_fusion
  65.6 0.1 pad_maximum_fusion
  65.7 2.4 %copy.51 = f32[2,512,3,128]{3,0,2,1:T(2,128)} copy(f32[2,512,3,128]{3,1,2,0:T(8,128)S(1)} %pad_maximum_fusion) | data formatting | bytes 3145728 | tf_op jit(solution)/shard_map/stack | solution.py:122
  68.1 4.7 %all-to-all-start.2 = ((f32[2,512,3,128]{3,0,2,1:T(2,128)}), f32[2,512,3,128]{3,0,2,1:T(2,128)S(1)}, u32[]{:S(2)}, u32[]{:S(2)}) async-start(f32[2,512,3,128]{3,0,2,1:T(2,128)} %copy.51), calls=%async_computation.2 | async-start | bytes 3145728 | tf_op jit(solution)/shard_map/all_to_all | solution.py:125
  72.8 2.0 %collective-permute-start.1 = (f32[128,16]{0,1:T(8,128)S(1)}, f32[128,16]{0,1:T(8,128)S(1)}, u32[]{:S(2)}, u32[]{:S(2)}) collective-permute-start(f32[128,16]{0,1:T(8,128)S(1)} %broadcast_multiply_fusion.1), channel_id=1, source_target_pairs={{0,32},{32,64},{64,96},{96,128},{128,160},{160,192},{192,224},{1,3... | collective-permute-start | bytes 24584 | tf_op jit(solution)/shard_map/ppermute | solution.py:83
  74.8 4.9 %collective-permute-start = (f32[128,32]{0,1:T(8,128)S(1)}, f32[128,32]{0,1:T(8,128)S(1)}, u32[]{:S(2)}, u32[]{:S(2)}) collective-permute-start(f32[128,32]{0,1:T(8,128)S(1)} %bitcast.61), channel_id=1, source_target_pairs={{0,32},{32,64},{64,96},{96,128},{128,160},{160,192},{192,224},{1,3... | collective-permute-start | bytes 49160 | tf_op jit(solution)/shard_map/ppermute | solution.py:83
  79.8 26.8 %collective-permute-done.1 = f32[128,16]{0,1:T(8,128)S(1)} collective-permute-done((f32[128,16]{0,1:T(8,128)S(1)}, f32[128,16]{0,1:T(8,128)S(1)}, u32[]{:S(2)}, u32[]{:S(2)}) %collective-permute-start.1) | collective-permute-done | bytes 8224 | tf_op jit(solution)/shard_map/ppermute | solution.py:83
  106.6 0.2 convolution_negate_fusion
  106.7 0.1 copy.55
  106.9 0.2 fusion
  107.1 0.2 fusion.2
  107.3 0.1 copy.54
  107.4 6.2 %all-to-all-done.2 = f32[2,512,3,128]{3,0,2,1:T(2,128)S(1)} async-done(((f32[2,512,3,128]{3,0,2,1:T(2,128)}), f32[2,512,3,128]{3,0,2,1:T(2,128)S(1)}, u32[]{:S(2)}, u32[]{:S(2)}) %all-to-all-start.2) | async-done | bytes 1572896 | tf_op jit(solution)/shard_map/all_to_all | solution.py:125
  113.6 0.1 copy.52
  113.7 0.2 copy.53
  114.0 0.8 multiply_reduce_fusion
  114.9 1.9 %collective-permute-start.2 = (f32[64,33]{0,1:T(8,128)S(1)}, f32[64,33]{0,1:T(8,128)S(1)}, u32[]{:S(2)}, u32[]{:S(2)}) collective-permute-start(f32[64,33]{0,1:T(8,128)S(1)} %pad_maximum_fusion.1), channel_id=1, source_target_pairs={{32,0},{64,32},{96,64},{128,96},{160,128},{192,160},{224,192},{33,... | collective-permute-start | bytes 25352 | tf_op jit(solution)/shard_map/ppermute | solution.py:83
  116.9 0.2 fusion.12
  117.1 1.5 %copy.58 = f32[64,16,2,128]{3,2,1,0:T(2,128)} copy(f32[64,16,2,128]{3,1,2,0:T(8,128)S(1)} %get-tuple-element.24) | data formatting | bytes 2097152
  118.6 2.0 %collective-permute-done.2 = f32[64,33]{0,1:T(8,128)S(1)} collective-permute-done((f32[64,33]{0,1:T(8,128)S(1)}, f32[64,33]{0,1:T(8,128)S(1)}, u32[]{:S(2)}, u32[]{:S(2)}) %collective-permute-start.2) | collective-permute-done | bytes 8480 | tf_op jit(solution)/shard_map/ppermute | solution.py:83
  120.6 0.2 convolution_add_fusion
  120.9 0.6 divide_subtract_fusion
  (29 shorter events, 0.3 us)
Async XLA Ops:
  0.6 41.7 %all-to-all-start = ((f32[32,64,128]{2,1,0:T(8,128)}), f32[32,64,128]{2,1,0:T(8,128)S(1)}, u32[]{:S(2)}, u32[]{:S(2)}) async-start(f32[32,64,128]{2,1,0:T(8,128)} %bitcast.51), calls=%async_computation | async-start | bytes 2097152 | tf_op jit(solution)/shard_map/all_to_all | solution.py:87
  12.0 34.3 %copy-start.5 = (s32[64]{0:T(128)S(1)}, s32[64]{0:T(128)}, u32[]{:S(2)}) copy-start(s32[64]{0:T(128)} %param.15) | copy-start | bytes 772
  42.3 22.5 %all-to-all-start.1 = ((f32[32,32,128]{2,1,0:T(8,128)}), f32[32,32,128]{2,1,0:T(8,128)S(1)}, u32[]{:S(2)}, u32[]{:S(2)}) async-start(f32[32,32,128]{2,1,0:T(8,128)} %bitcast.52), calls=%async_computation.1 | async-start | bytes 1048576 | tf_op jit(solution)/shard_map/all_to_all | solution.py:87
  68.1 4.7 %copy-start.2 = (f32[128,64]{0,1:T(8,128)S(1)}, f32[128,64]{0,1:T(8,128)}, u32[]{:S(2)}) copy-start(f32[128,64]{0,1:T(8,128)} %param.11) | copy-start | bytes 98308
  68.1 6.7 %copy-start.1 = (f32[128,2,64]{0,2,1:T(8,128)S(1)}, f32[128,2,64]{0,2,1:T(8,128)}, u32[]{:S(2)}) copy-start(f32[128,2,64]{0,2,1:T(8,128)} %param.12) | copy-start | bytes 196612
  68.1 11.7 %copy-start.4 = (s32[64]{0:T(128)S(1)}, s32[64]{0:T(128)}, u32[]{:S(2)}) copy-start(s32[64]{0:T(128)} %param.17) | copy-start | bytes 772
  68.1 38.8 %copy-start.3 = (f32[128]{0:T(128)S(1)}, f32[128]{0:T(128)}, u32[]{:S(2)}) copy-start(f32[128]{0:T(128)} %param.14) | copy-start | bytes 1540
  68.1 45.6 %all-to-all-start.2 = ((f32[2,512,3,128]{3,0,2,1:T(2,128)}), f32[2,512,3,128]{3,0,2,1:T(2,128)S(1)}, u32[]{:S(2)}, u32[]{:S(2)}) async-start(f32[2,512,3,128]{3,0,2,1:T(2,128)} %copy.51), calls=%async_computation.2 | async-start | bytes 3145728 | tf_op jit(solution)/shard_map/all_to_all | solution.py:125
  72.8 33.8 %collective-permute-start.1 = (f32[128,16]{0,1:T(8,128)S(1)}, f32[128,16]{0,1:T(8,128)S(1)}, u32[]{:S(2)}, u32[]{:S(2)}) collective-permute-start(f32[128,16]{0,1:T(8,128)S(1)} %broadcast_multiply_fusion.1), channel_id=1, source_target_pairs={{0,32},{32,64},{64,96},{96,128},{128,160},{160,192},{192,224},{1,3... | collective-permute-start | bytes 24584 | tf_op jit(solution)/shard_map/ppermute | solution.py:83
  74.8 32.3 %collective-permute-start = (f32[128,32]{0,1:T(8,128)S(1)}, f32[128,32]{0,1:T(8,128)S(1)}, u32[]{:S(2)}, u32[]{:S(2)}) collective-permute-start(f32[128,32]{0,1:T(8,128)S(1)} %bitcast.61), channel_id=1, source_target_pairs={{0,32},{32,64},{64,96},{96,128},{128,160},{160,192},{192,224},{1,3... | collective-permute-start | bytes 49160 | tf_op jit(solution)/shard_map/ppermute | solution.py:83
  114.0 0.8 copy-start
  114.9 5.7 %collective-permute-start.2 = (f32[64,33]{0,1:T(8,128)S(1)}, f32[64,33]{0,1:T(8,128)S(1)}, u32[]{:S(2)}, u32[]{:S(2)}) collective-permute-start(f32[64,33]{0,1:T(8,128)S(1)} %pad_maximum_fusion.1), channel_id=1, source_target_pairs={{32,0},{64,32},{96,64},{128,96},{160,128},{192,160},{224,192},{33,... | collective-permute-start | bytes 25352 | tf_op jit(solution)/shard_map/ppermute | solution.py:83

commit v12 on v11

--- a/solution.py
+++ b/solution.py
@@ -120,9 +120,12 @@
     rings = jnp.concatenate([ring_density, ring_velocity], axis=2)
     doubled = jnp.concatenate([rings, rings], axis=1)
     rings = jnp.stack(
-        [lax.dynamic_slice_in_dim(doubled[c], whole - turns[c], whole, 0) for c in range(own)]
+        [lax.dynamic_slice_in_dim(doubled[c], whole - turns[c], whole, 0) for c in range(own)],
+        axis=1,
     )
-    state = lax.all_to_all(rings, "az", 1, 0, tiled=True)
+    state = lax.all_to_all(rings.reshape(-1, bins), "az", 0, 0, tiled=True)
+    state = state.reshape(az_count, cells, own, -1, bins)
+    state = jnp.transpose(state, (0, 2, 1, 3, 4)).reshape(cycles, cells, -1, bins)
     coag_density = state[:, :, 0, :]
     moved_velocity = state[:, :, 1:, :]
     coarse_density = gas_density.reshape(gas_cycles, cells, 4).mean(-1)

time: 122 us -> 124 us (1.016)
  local copies, waits for them, and re-layouts: 5.72 us -> 7.62 us
    all_to_all x2, local copies, waits for them, and re-layouts: 0.31 us -> 2.59 us  [body(): state = lax.all_to_all(rings.reshape(-1, bins), 'az', 0, 0, tiled=True)]
  transfers between devices with their start and end apart: 6 -> 6, of which waited for: 5 -> 5; matrix products, arithmetic and copies ran while one was open for 3% -> 3% of each run, Pallas kernels for 18% -> 17%
where the time goes in v12:
time: 124 us; the launch traced here: 123 us
  waiting for transfers between devices  59.3 us (48%)
  starting transfers between devices  28.6 us (23%)
  Pallas kernels  21.4 us (17%)
  local copies, waits for them, and re-layouts  7.62 us (6%)
  between operations  3.54 us (3%)
  other arithmetic  2.08 us (2%)
    ppermute x3, waiting for transfers between devices, shifted(): return lax.ppermute(block, axis, route)  28.8 us
    all_to_all x2, waiting for transfers between devices, sent(): lax.all_to_all(block.reshape(-1, block.shape[-1]), 'az', 0, 0, tiled=True)  24.3 us
    pallas_call x1, Pallas kernels, coag(): pl.pallas_call(functools.partial(coag_kernel, group=group), grid=(1,), in...  21.4 us
    all_to_all x2, starting transfers between devices, sent(): lax.all_to_all(block.reshape(-1, block.shape[-1]), 'az', 0, 0, tiled=True)  15.2 us
    ppermute x3, starting transfers between devices, shifted(): return lax.ppermute(block, axis, route)  8.76 us
    all_to_all x1, waiting for transfers between devices, body(): state = lax.all_to_all(rings.reshape(-1, bins), 'az', 0, 0, tiled=True)  6.2 us
    all_to_all x1, starting transfers between devices, body(): state = lax.all_to_all(rings.reshape(-1, bins), 'az', 0, 0, tiled=True)  4.66 us
    all_to_all x2, local copies, waits for them, and re-layouts, body(): state = lax.all_to_all(rings.reshape(-1, bins), 'az', 0, 0, tiled=True)  2.59 us
  transfers between devices with their start and end apart: 6, of which 5 were waited for; matrix products, arithmetic and copies ran while one was open for 3% of the time, Pallas kernels for 17%

profile of v12, /device:TPU:8, one launch (start us, length us, event | category | flops | bytes accessed | tf_op | source)
XLA Modules:
  0.0 123.4 jit_solution(14496378255446296294)
XLA Ops:
  0.6 11.3 %all-to-all-start = ((f32[32,64,128]{2,1,0:T(8,128)}), f32[32,64,128]{2,1,0:T(8,128)S(1)}, u32[]{:S(2)}, u32[]{:S(2)}) async-start(f32[32,64,128]{2,1,0:T(8,128)} %bitcast.55), calls=%async_computation | async-start | bytes 2097152 | tf_op jit(solution)/shard_map/all_to_all | solution.py:87
  12.0 21.4 %shard_map.112 = f32[1024,128]{1,0:T(8,128)} custom-call(f32[1024,128]{1,0:T(8,128)} %bitcast.67, f32[128,128]{1,0:T(8,128)} %k_ref.1, s32[128,128]{1,0:T(8,128)} %f_ref.1), custom_call_target="tpu_custom_call" | custom-call | flops 12884901888 | bytes 1048576 | tf_op jit(solution)/shard_map/pallas_call | solution.py:57
  33.3 9.0 %all-to-all-done = f32[32,64,128]{2,1,0:T(8,128)S(1)} async-done(((f32[32,64,128]{2,1,0:T(8,128)}), f32[32,64,128]{2,1,0:T(8,128)S(1)}, u32[]{:S(2)}, u32[]{:S(2)}) %all-to-all-start) | async-done | bytes 1048608 | tf_op jit(solution)/shard_map/all_to_all | solution.py:87
  42.3 3.9 %all-to-all-start.1 = ((f32[32,32,128]{2,1,0:T(8,128)}), f32[32,32,128]{2,1,0:T(8,128)S(1)}, u32[]{:S(2)}, u32[]{:S(2)}) async-start(f32[32,32,128]{2,1,0:T(8,128)} %bitcast.56), calls=%async_computation.1 | async-start | bytes 1048576 | tf_op jit(solution)/shard_map/all_to_all | solution.py:87
  46.3 0.6 fusion.25
  49.5 15.3 %all-to-all-done.1 = f32[32,32,128]{2,1,0:T(8,128)S(1)} async-done(((f32[32,32,128]{2,1,0:T(8,128)}), f32[32,32,128]{2,1,0:T(8,128)S(1)}, u32[]{:S(2)}, u32[]{:S(2)}) %all-to-all-start.1) | async-done | bytes 524320 | tf_op jit(solution)/shard_map/all_to_all | solution.py:87
  64.9 0.1 copy.41
  65.0 0.2 maximum_maximum_fusion
  65.2 0.2 fusion.24
  65.4 0.2 dynamic-slice_bitcast_fusion
  65.6 0.1 pad_maximum_fusion
  65.7 1.1 copy.43
  66.8 1.7 %all_to_all.28 = f32[32,96,128]{2,1,0:T(8,128)} reshape(f32[512,2,3,128]{3,2,1,0:T(4,128)S(1)} %copy.43) | data formatting | bytes 3145728 | tf_op jit(solution)/shard_map/all_to_all | solution.py:126
  68.5 4.7 %all-to-all-start.2 = ((f32[32,96,128]{2,1,0:T(8,128)}), f32[32,96,128]{2,1,0:T(8,128)S(1)}, u32[]{:S(2)}, u32[]{:S(2)}) async-start(f32[32,96,128]{2,1,0:T(8,128)} %all_to_all.28), calls=%async_computation.2 | async-start | bytes 3145728 | tf_op jit(solution)/shard_map/all_to_all | solution.py:126
  73.2 2.0 %collective-permute-start.1 = (f32[128,16]{0,1:T(8,128)S(1)}, f32[128,16]{0,1:T(8,128)S(1)}, u32[]{:S(2)}, u32[]{:S(2)}) collective-permute-start(f32[128,16]{0,1:T(8,128)S(1)} %broadcast_multiply_fusion.1), channel_id=1, source_target_pairs={{0,32},{32,64},{64,96},{96,128},{128,160},{160,192},{192,224},{1,3... | collective-permute-start | bytes 24584 | tf_op jit(solution)/shard_map/ppermute | solution.py:83
  75.2 4.9 %collective-permute-start = (f32[128,32]{0,1:T(8,128)S(1)}, f32[128,32]{0,1:T(8,128)S(1)}, u32[]{:S(2)}, u32[]{:S(2)}) collective-permute-start(f32[128,32]{0,1:T(8,128)S(1)} %bitcast.65), channel_id=1, source_target_pairs={{0,32},{32,64},{64,96},{96,128},{128,160},{160,192},{192,224},{1,3... | collective-permute-start | bytes 49160 | tf_op jit(solution)/shard_map/ppermute | solution.py:83
  80.2 26.8 %collective-permute-done.1 = f32[128,16]{0,1:T(8,128)S(1)} collective-permute-done((f32[128,16]{0,1:T(8,128)S(1)}, f32[128,16]{0,1:T(8,128)S(1)}, u32[]{:S(2)}, u32[]{:S(2)}) %collective-permute-start.1) | collective-permute-done | bytes 8224 | tf_op jit(solution)/shard_map/ppermute | solution.py:83
  107.0 0.2 convolution_negate_fusion
  107.1 0.1 copy.47
  107.3 0.2 fusion
  107.5 0.2 fusion.2
  107.7 0.1 copy.46
  107.8 6.2 %all-to-all-done.2 = f32[32,96,128]{2,1,0:T(8,128)S(1)} async-done(((f32[32,96,128]{2,1,0:T(8,128)}), f32[32,96,128]{2,1,0:T(8,128)S(1)}, u32[]{:S(2)}, u32[]{:S(2)}) %all-to-all-start.2) | async-done | bytes 1572896 | tf_op jit(solution)/shard_map/all_to_all | solution.py:126
  114.0 0.9 copy.44
  114.9 0.9 copy.45
  115.9 0.8 multiply_reduce_fusion
  116.8 1.9 %collective-permute-start.2 = (f32[64,33]{0,1:T(8,128)S(1)}, f32[64,33]{0,1:T(8,128)S(1)}, u32[]{:S(2)}, u32[]{:S(2)}) collective-permute-start(f32[64,33]{0,1:T(8,128)S(1)} %pad_maximum_fusion.1), channel_id=1, source_target_pairs={{32,0},{64,32},{96,64},{128,96},{160,128},{192,160},{224,192},{33,... | collective-permute-start | bytes 25352 | tf_op jit(solution)/shard_map/ppermute | solution.py:83
  118.8 0.2 fusion.12
  119.0 1.5 %copy.50 = f32[64,16,2,128]{3,2,1,0:T(2,128)} copy(f32[64,16,2,128]{3,1,2,0:T(8,128)S(1)} %get-tuple-element.21) | data formatting | bytes 2097152
  120.5 2.0 %collective-permute-done.2 = f32[64,33]{0,1:T(8,128)S(1)} collective-permute-done((f32[64,33]{0,1:T(8,128)S(1)}, f32[64,33]{0,1:T(8,128)S(1)}, u32[]{:S(2)}, u32[]{:S(2)}) %collective-permute-start.2) | collective-permute-done | bytes 8480 | tf_op jit(solution)/shard_map/ppermute | solution.py:83
  122.5 0.2 convolution_add_fusion
  122.8 0.6 divide_subtract_fusion
  (30 shorter events, 0.4 us)
Async XLA Ops:
  0.6 41.7 %all-to-all-start = ((f32[32,64,128]{2,1,0:T(8,128)}), f32[32,64,128]{2,1,0:T(8,128)S(1)}, u32[]{:S(2)}, u32[]{:S(2)}) async-start(f32[32,64,128]{2,1,0:T(8,128)} %bitcast.55), calls=%async_computation | async-start | bytes 2097152 | tf_op jit(solution)/shard_map/all_to_all | solution.py:87
  12.0 34.3 %copy-start.5 = (s32[64]{0:T(128)S(1)}, s32[64]{0:T(128)}, u32[]{:S(2)}) copy-start(s32[64]{0:T(128)} %param.15) | copy-start | bytes 772
  42.3 22.5 %all-to-all-start.1 = ((f32[32,32,128]{2,1,0:T(8,128)}), f32[32,32,128]{2,1,0:T(8,128)S(1)}, u32[]{:S(2)}, u32[]{:S(2)}) async-start(f32[32,32,128]{2,1,0:T(8,128)} %bitcast.56), calls=%async_computation.1 | async-start | bytes 1048576 | tf_op jit(solution)/shard_map/all_to_all | solution.py:87
  68.5 4.7 %copy-start.2 = (f32[128,64]{0,1:T(8,128)S(1)}, f32[128,64]{0,1:T(8,128)}, u32[]{:S(2)}) copy-start(f32[128,64]{0,1:T(8,128)} %param.11) | copy-start | bytes 98308
  68.5 6.7 %copy-start.1 = (f32[128,2,64]{0,2,1:T(8,128)S(1)}, f32[128,2,64]{0,2,1:T(8,128)}, u32[]{:S(2)}) copy-start(f32[128,2,64]{0,2,1:T(8,128)} %param.12) | copy-start | bytes 196612
  68.5 11.7 %copy-start.4 = (s32[64]{0:T(128)S(1)}, s32[64]{0:T(128)}, u32[]{:S(2)}) copy-start(s32[64]{0:T(128)} %param.17) | copy-start | bytes 772
  68.5 38.8 %copy-start.3 = (f32[128]{0:T(128)S(1)}, f32[128]{0:T(128)}, u32[]{:S(2)}) copy-start(f32[128]{0:T(128)} %param.14) | copy-start | bytes 1540
  68.5 45.6 %all-to-all-start.2 = ((f32[32,96,128]{2,1,0:T(8,128)}), f32[32,96,128]{2,1,0:T(8,128)S(1)}, u32[]{:S(2)}, u32[]{:S(2)}) async-start(f32[32,96,128]{2,1,0:T(8,128)} %all_to_all.28), calls=%async_computation.2 | async-start | bytes 3145728 | tf_op jit(solution)/shard_map/all_to_all | solution.py:126
  73.2 33.8 %collective-permute-start.1 = (f32[128,16]{0,1:T(8,128)S(1)}, f32[128,16]{0,1:T(8,128)S(1)}, u32[]{:S(2)}, u32[]{:S(2)}) collective-permute-start(f32[128,16]{0,1:T(8,128)S(1)} %broadcast_multiply_fusion.1), channel_id=1, source_target_pairs={{0,32},{32,64},{64,96},{96,128},{128,160},{160,192},{192,224},{1,3... | collective-permute-start | bytes 24584 | tf_op jit(solution)/shard_map/ppermute | solution.py:83
  75.2 32.3 %collective-permute-start = (f32[128,32]{0,1:T(8,128)S(1)}, f32[128,32]{0,1:T(8,128)S(1)}, u32[]{:S(2)}, u32[]{:S(2)}) collective-permute-start(f32[128,32]{0,1:T(8,128)S(1)} %bitcast.65), channel_id=1, source_target_pairs={{0,32},{32,64},{64,96},{96,128},{128,160},{160,192},{192,224},{1,3... | collective-permute-start | bytes 49160 | tf_op jit(solution)/shard_map/ppermute | solution.py:83
  115.9 0.8 copy-start
  116.8 5.7 %collective-permute-start.2 = (f32[64,33]{0,1:T(8,128)S(1)}, f32[64,33]{0,1:T(8,128)S(1)}, u32[]{:S(2)}, u32[]{:S(2)}) collective-permute-start(f32[64,33]{0,1:T(8,128)S(1)} %pad_maximum_fusion.1), channel_id=1, source_target_pairs={{32,0},{64,32},{96,64},{128,96},{160,128},{192,160},{224,192},{33,... | collective-permute-start | bytes 25352 | tf_op jit(solution)/shard_map/ppermute | solution.py:83

commit v13 on v11

--- a/solution.py
+++ b/solution.py
@@ -122,7 +122,8 @@
     rings = jnp.stack(
         [lax.dynamic_slice_in_dim(doubled[c], whole - turns[c], whole, 0) for c in range(own)]
     )
-    state = lax.all_to_all(rings, "az", 1, 0, tiled=True)
+    blocks = rings.reshape(own, az_count, cells, -1, bins)
+    state = lax.all_to_all(blocks, "az", 1, 0, tiled=False).reshape(cycles, cells, -1, bins)
     coag_density = state[:, :, 0, :]
     moved_velocity = state[:, :, 1:, :]
     coarse_density = gas_density.reshape(gas_cycles, cells, 4).mean(-1)

time: 122 us -> 124 us (1.016)
  other arithmetic: 2.08 us -> 4.53 us
  local copies, waits for them, and re-layouts: 5.72 us -> 3.43 us
  waiting for transfers between devices: 59.3 us -> 60.6 us
    reduce_sum x1, other arithmetic: 0.8 us -> 3.17 us  [body(): jnp.sum(coag_density[:, :, None, :] * (velocity_out - moved_velocity), ax...]
    ppermute x3, waiting for transfers between devices: 28.8 us -> 30.3 us  [shifted(): return lax.ppermute(block, axis, route)]
    unnamed x13 -> x12, local copies, waits for them, and re-layouts: 1.55 us -> 0.04 us
  transfers between devices with their start and end apart: 6 -> 6, of which waited for: 5 -> 5; matrix products, arithmetic and copies ran while one was open for 3% -> 2% of each run, Pallas kernels for 18% -> 17%
where the time goes in v13:
time: 124 us; the launch traced here: 123 us
  waiting for transfers between devices  60.6 us (49%)
  starting transfers between devices  28.7 us (23%)
  Pallas kernels  21.4 us (17%)
  other arithmetic  4.53 us (4%)
  between operations  3.53 us (3%)
  local copies, waits for them, and re-layouts  3.43 us (3%)
    ppermute x3, waiting for transfers between devices, shifted(): return lax.ppermute(block, axis, route)  30.3 us
    all_to_all x2, waiting for transfers between devices, sent(): lax.all_to_all(block.reshape(-1, block.shape[-1]), 'az', 0, 0, tiled=True)  24.3 us
    pallas_call x1, Pallas kernels, coag(): pl.pallas_call(functools.partial(coag_kernel, group=group), grid=(1,), in...  21.4 us
    all_to_all x2, starting transfers between devices, sent(): lax.all_to_all(block.reshape(-1, block.shape[-1]), 'az', 0, 0, tiled=True)  15.2 us
    ppermute x3, starting transfers between devices, shifted(): return lax.ppermute(block, axis, route)  8.74 us
    all_to_all x1, waiting for transfers between devices, body(): lax.all_to_all(blocks, 'az', 1, 0, tiled=False)  5.97 us
    all_to_all x1, starting transfers between devices, body(): lax.all_to_all(blocks, 'az', 1, 0, tiled=False)  4.7 us
    reduce_sum x1, other arithmetic, body(): jnp.sum(coag_density[:, :, None, :] * (velocity_out - moved_velocity), ax...  3.17 us
  transfers between devices with their start and end apart: 6, of which 5 were waited for; matrix products, arithmetic and copies ran while one was open for 2% of the time, Pallas kernels for 17%

profile of v13, /device:TPU:8, one launch (start us, length us, event | category | flops | bytes accessed | tf_op | source)
XLA Modules:
  0.0 123.0 jit_solution(1499027039043391125)
XLA Ops:
  0.6 11.3 %all-to-all-start = ((f32[32,64,128]{2,1,0:T(8,128)}), f32[32,64,128]{2,1,0:T(8,128)S(1)}, u32[]{:S(2)}, u32[]{:S(2)}) async-start(f32[32,64,128]{2,1,0:T(8,128)} %bitcast.57), calls=%async_computation | async-start | bytes 2097152 | tf_op jit(solution)/shard_map/all_to_all | solution.py:87
  12.0 21.4 %shard_map.112 = f32[1024,128]{1,0:T(8,128)} custom-call(f32[1024,128]{1,0:T(8,128)} %bitcast.69, f32[128,128]{1,0:T(8,128)} %k_ref.1, s32[128,128]{1,0:T(8,128)} %f_ref.1), custom_call_target="tpu_custom_call" | custom-call | flops 12884901888 | bytes 1048576 | tf_op jit(solution)/shard_map/pallas_call | solution.py:57
  33.3 9.0 %all-to-all-done = f32[32,64,128]{2,1,0:T(8,128)S(1)} async-done(((f32[32,64,128]{2,1,0:T(8,128)}), f32[32,64,128]{2,1,0:T(8,128)S(1)}, u32[]{:S(2)}, u32[]{:S(2)}) %all-to-all-start) | async-done | bytes 1048608 | tf_op jit(solution)/shard_map/all_to_all | solution.py:87
  42.3 3.9 %all-to-all-start.1 = ((f32[32,32,128]{2,1,0:T(8,128)}), f32[32,32,128]{2,1,0:T(8,128)S(1)}, u32[]{:S(2)}, u32[]{:S(2)}) async-start(f32[32,32,128]{2,1,0:T(8,128)} %bitcast.58), calls=%async_computation.1 | async-start | bytes 1048576 | tf_op jit(solution)/shard_map/all_to_all | solution.py:87
  46.3 0.1 dynamic_slice.9
  46.3 0.6 fusion.25
  49.5 15.3 %all-to-all-done.1 = f32[32,32,128]{2,1,0:T(8,128)S(1)} async-done(((f32[32,32,128]{2,1,0:T(8,128)}), f32[32,32,128]{2,1,0:T(8,128)S(1)}, u32[]{:S(2)}, u32[]{:S(2)}) %all-to-all-start.1) | async-done | bytes 524320 | tf_op jit(solution)/shard_map/all_to_all | solution.py:87
  64.9 0.1 copy.36
  65.0 0.2 maximum_maximum_fusion
  65.2 0.2 fusion.24
  65.4 0.1 constant_dynamic-slice_fusion
  65.6 0.2 pad_maximum_fusion
  65.7 1.4 %copy.38 = f32[1,2,32,16,3,128]{5,3,4,1,0,2:T(8,128)} copy(f32[1,2,32,16,3,128]{5,3,2,4,1,0:T(8,128)S(1)} %pad_maximum_fusion) | data formatting | bytes 3145728 | tf_op jit(solution)/shard_map/stack | solution.py:122
  67.1 4.7 %all-to-all-start.2 = ((f32[1,2,32,16,3,128]{5,3,4,1,0,2:T(8,128)}), f32[1,2,32,16,3,128]{5,3,4,1,0,2:T(8,128)S(1)}, u32[]{:S(2)}, u32[]{:S(2)}) async-start(f32[1,2,32,16,3,128]{5,3,4,1,0,2:T(8,128)} %copy.38), calls=%async_computation.2 | async-start | bytes 3145728 | tf_op jit(solution)/shard_map/all_to_all | solution.py:126
  71.9 1.9 %collective-permute-start.1 = (f32[128,16]{0,1:T(8,128)S(1)}, f32[128,16]{0,1:T(8,128)S(1)}, u32[]{:S(2)}, u32[]{:S(2)}) collective-permute-start(f32[128,16]{0,1:T(8,128)S(1)} %broadcast_multiply_fusion.1), channel_id=1, source_target_pairs={{0,32},{32,64},{64,96},{96,128},{128,160},{160,192},{192,224},{1,3... | collective-permute-start | bytes 24584 | tf_op jit(solution)/shard_map/ppermute | solution.py:83
  73.9 4.9 %collective-permute-start = (f32[128,32]{0,1:T(8,128)S(1)}, f32[128,32]{0,1:T(8,128)S(1)}, u32[]{:S(2)}, u32[]{:S(2)}) collective-permute-start(f32[128,32]{0,1:T(8,128)S(1)} %bitcast.67), channel_id=1, source_target_pairs={{0,32},{32,64},{64,96},{96,128},{128,160},{160,192},{192,224},{1,3... | collective-permute-start | bytes 49160 | tf_op jit(solution)/shard_map/ppermute | solution.py:83
  78.9 26.8 %collective-permute-done.1 = f32[128,16]{0,1:T(8,128)S(1)} collective-permute-done((f32[128,16]{0,1:T(8,128)S(1)}, f32[128,16]{0,1:T(8,128)S(1)}, u32[]{:S(2)}, u32[]{:S(2)}) %collective-permute-start.1) | collective-permute-done | bytes 8224 | tf_op jit(solution)/shard_map/ppermute | solution.py:83
  105.7 0.2 convolution_negate_fusion
  105.8 0.1 copy.42
  105.9 0.0 copy-done.3
  106.0 0.2 fusion
  106.2 0.2 fusion.2
  106.4 0.3 copy.41
  106.8 6.0 %all-to-all-done.2 = f32[1,2,32,16,3,128]{5,3,4,1,0,2:T(8,128)S(1)} async-done(((f32[1,2,32,16,3,128]{5,3,4,1,0,2:T(8,128)}), f32[1,2,32,16,3,128]{5,3,4,1,0,2:T(8,128)S(1)}, u32[]{:S(2)}, u32[]{:S(2)}) %all-to-all-start.2) | async-done | bytes 1572896 | tf_op jit(solution)/shard_map/all_to_all | solution.py:126
  112.8 0.1 slice.39
  112.9 3.2 %multiply_reduce_fusion = (f32[64,16,2]{2,1,0:T(8,128)S(1)}, f32[64,16,2,128]{3,2,1,0:T(2,128)}) fusion(f32[64,16,2,128]{3,1,2,0:T(8,128)S(1)} %slice.39, f32[64,16,128]{2,1,0:T(8,128)S(1)} %slice_bitcast_fusion, f32[64,16,128]{2,1,0:T(8,128)S(1)} %fusion, f32[64,16,2]{2,1,0:T(8,128)S(1)} %copy.41), kind=kLoop, calls=%fused_computation.4 | loop fusion | flops 1570816 | bytes 3162112 | tf_op jit(solution)/shard_map/reduce_sum | solution.py:144
  116.1 0.3 copy.43
  116.4 1.9 %collective-permute-start.2 = (f32[64,33]{0,1:T(8,128)S(1)}, f32[64,33]{0,1:T(8,128)S(1)}, u32[]{:S(2)}, u32[]{:S(2)}) collective-permute-start(f32[64,33]{0,1:T(8,128)S(1)} %pad_maximum_fusion.1), channel_id=1, source_target_pairs={{32,0},{64,32},{96,64},{128,96},{160,128},{192,160},{224,192},{33,... | collective-permute-start | bytes 25352 | tf_op jit(solution)/shard_map/ppermute | solution.py:83
  118.3 0.2 fusion.12
  118.6 3.5 %collective-permute-done.2 = f32[64,33]{0,1:T(8,128)S(1)} collective-permute-done((f32[64,33]{0,1:T(8,128)S(1)}, f32[64,33]{0,1:T(8,128)S(1)}, u32[]{:S(2)}, u32[]{:S(2)}) %collective-permute-start.2) | collective-permute-done | bytes 8480 | tf_op jit(solution)/shard_map/ppermute | solution.py:83
  122.1 0.2 convolution_add_fusion
  122.3 0.6 divide_subtract_fusion
  (27 shorter events, 0.3 us)
Async XLA Ops:
  0.6 41.7 %all-to-all-start = ((f32[32,64,128]{2,1,0:T(8,128)}), f32[32,64,128]{2,1,0:T(8,128)S(1)}, u32[]{:S(2)}, u32[]{:S(2)}) async-start(f32[32,64,128]{2,1,0:T(8,128)} %bitcast.57), calls=%async_computation | async-start | bytes 2097152 | tf_op jit(solution)/shard_map/all_to_all | solution.py:87
  12.0 34.3 %copy-start.5 = (s32[64]{0:T(128)S(1)}, s32[64]{0:T(128)}, u32[]{:S(2)}) copy-start(s32[64]{0:T(128)} %param.15) | copy-start | bytes 772
  42.3 22.5 %all-to-all-start.1 = ((f32[32,32,128]{2,1,0:T(8,128)}), f32[32,32,128]{2,1,0:T(8,128)S(1)}, u32[]{:S(2)}, u32[]{:S(2)}) async-start(f32[32,32,128]{2,1,0:T(8,128)} %bitcast.58), calls=%async_computation.1 | async-start | bytes 1048576 | tf_op jit(solution)/shard_map/all_to_all | solution.py:87
  67.1 4.7 %copy-start.2 = (f32[128,64]{0,1:T(8,128)S(1)}, f32[128,64]{0,1:T(8,128)}, u32[]{:S(2)}) copy-start(f32[128,64]{0,1:T(8,128)} %param.11) | copy-start | bytes 98308
  67.1 6.7 %copy-start.1 = (f32[128,2,64]{0,2,1:T(8,128)S(1)}, f32[128,2,64]{0,2,1:T(8,128)}, u32[]{:S(2)}) copy-start(f32[128,2,64]{0,2,1:T(8,128)} %param.12) | copy-start | bytes 196612
  67.1 11.7 %copy-start.4 = (s32[64]{0:T(128)S(1)}, s32[64]{0:T(128)}, u32[]{:S(2)}) copy-start(s32[64]{0:T(128)} %param.17) | copy-start | bytes 772
  67.1 38.8 %copy-start.3 = (f32[128]{0:T(128)S(1)}, f32[128]{0:T(128)}, u32[]{:S(2)}) copy-start(f32[128]{0:T(128)} %param.14) | copy-start | bytes 1540
  67.1 45.6 %all-to-all-start.2 = ((f32[1,2,32,16,3,128]{5,3,4,1,0,2:T(8,128)}), f32[1,2,32,16,3,128]{5,3,4,1,0,2:T(8,128)S(1)}, u32[]{:S(2)}, u32[]{:S(2)}) async-start(f32[1,2,32,16,3,128]{5,3,4,1,0,2:T(8,128)} %copy.38), calls=%async_computation.2 | async-start | bytes 3145728 | tf_op jit(solution)/shard_map/all_to_all | solution.py:126
  71.9 33.8 %collective-permute-start.1 = (f32[128,16]{0,1:T(8,128)S(1)}, f32[128,16]{0,1:T(8,128)S(1)}, u32[]{:S(2)}, u32[]{:S(2)}) collective-permute-start(f32[128,16]{0,1:T(8,128)S(1)} %broadcast_multiply_fusion.1), channel_id=1, source_target_pairs={{0,32},{32,64},{64,96},{96,128},{128,160},{160,192},{192,224},{1,3... | collective-permute-start | bytes 24584 | tf_op jit(solution)/shard_map/ppermute | solution.py:83
  73.9 32.3 %collective-permute-start = (f32[128,32]{0,1:T(8,128)S(1)}, f32[128,32]{0,1:T(8,128)S(1)}, u32[]{:S(2)}, u32[]{:S(2)}) collective-permute-start(f32[128,32]{0,1:T(8,128)S(1)} %bitcast.67), channel_id=1, source_target_pairs={{0,32},{32,64},{64,96},{96,128},{128,160},{160,192},{192,224},{1,3... | collective-permute-start | bytes 49160 | tf_op jit(solution)/shard_map/ppermute | solution.py:83
  112.8 3.3 %copy-start = (f32[64,16,128]{2,1,0:T(8,128)}, f32[64,16,128]{2,1,0:T(8,128)S(1)}, u32[]{:S(2)}) copy-start(f32[64,16,128]{2,1,0:T(8,128)S(1)} %slice_bitcast_fusion) | copy-start | bytes 1572868
  116.4 5.7 %collective-permute-start.2 = (f32[64,33]{0,1:T(8,128)S(1)}, f32[64,33]{0,1:T(8,128)S(1)}, u32[]{:S(2)}, u32[]{:S(2)}) collective-permute-start(f32[64,33]{0,1:T(8,128)S(1)} %pad_maximum_fusion.1), channel_id=1, source_target_pairs={{32,0},{64,32},{96,64},{128,96},{160,128},{192,160},{224,192},{33,... | collective-permute-start | bytes 25352 | tf_op jit(solution)/shard_map/ppermute | solution.py:83

commit v14 on v13

--- a/solution.py
+++ b/solution.py
@@ -144,6 +144,10 @@
     momentum = jnp.sum(coag_density[:, :, None, :] * (velocity_out - moved_velocity), axis=3) / bins
     by_axis = jnp.transpose(momentum, (0, 2, 1)).reshape(cycles, 2 * cells)
     message = jnp.concatenate([by_axis, gas_map.astype(F32)[:, None]], axis=1)
+    message, moved_velocity, u_dust, frac = lax.optimization_barrier(
+        (message, moved_velocity, u_dust, frac)
+    )
+    velocity_out = moved_velocity + (u_dust[:, :, :, None] - moved_velocity) * frac[:, :, None, :]
     arrived = shifted(message, "rad", -1)
     own_rows = near_rows[gas_cycles:]
 

time: 124 us -> 123 us (level)
  waiting for transfers between devices: 60.6 us -> 58.2 us
  other arithmetic: 4.53 us -> 6.59 us
    reduce_sum x1 -> x0, other arithmetic: 3.17 us -> none  [body(): jnp.sum(coag_density[:, :, None, :] * (velocity_out - moved_velocity), ax...]
    unnamed x0 -> x1, other arithmetic: none -> 2.81 us
    ppermute x3, waiting for transfers between devices: 30.3 us -> 27.9 us  [shifted(): return lax.ppermute(block, axis, route)]
    add x0 -> x1, other arithmetic: none -> 2.42 us  [body(): moved_velocity + (u_dust[:, :, :, None] - moved_velocity) * frac[:, :, No...]
  transfers between devices with their start and end apart: 6 -> 6, of which waited for: 5 -> 5; matrix products, arithmetic and copies ran while one was open for 2% -> 4% of each run, Pallas kernels for 17% -> 17%
where the time goes in v14:
time: 123 us
  waiting for transfers between devices  58.2 us (47%)
  starting transfers between devices  28.6 us (23%)
  Pallas kernels  21.4 us (17%)
  other arithmetic  6.59 us (5%)
  local copies, waits for them, and re-layouts  3.77 us (3%)
  between operations  3.55 us (3%)
    ppermute x3, waiting for transfers between devices, shifted(): return lax.ppermute(block, axis, route)  27.9 us
    all_to_all x2, waiting for transfers between devices, sent(): lax.all_to_all(block.reshape(-1, block.shape[-1]), 'az', 0, 0, tiled=True)  24.3 us
    pallas_call x1, Pallas kernels, coag(): pl.pallas_call(functools.partial(coag_kernel, group=group), grid=(1,), in...  21.4 us
    all_to_all x2, starting transfers between devices, sent(): lax.all_to_all(block.reshape(-1, block.shape[-1]), 'az', 0, 0, tiled=True)  15.2 us
    ppermute x3, starting transfers between devices, shifted(): return lax.ppermute(block, axis, route)  8.77 us
    all_to_all x1, waiting for transfers between devices, body(): lax.all_to_all(blocks, 'az', 1, 0, tiled=False)  5.97 us
    all_to_all x1, starting transfers between devices, body(): lax.all_to_all(blocks, 'az', 1, 0, tiled=False)  4.66 us
    unnamed x1, other arithmetic  2.81 us
  transfers between devices with their start and end apart: 6, of which 5 were waited for; matrix products, arithmetic and copies ran while one was open for 4% of the time, Pallas kernels for 17%

profile of v14, /device:TPU:8, one launch (start us, length us, event | category | flops | bytes accessed | tf_op | source)
XLA Modules:
  0.0 123.0 jit_solution(7501126840875949500)
XLA Ops:
  0.6 11.3 %all-to-all-start = ((f32[32,64,128]{2,1,0:T(8,128)}), f32[32,64,128]{2,1,0:T(8,128)S(1)}, u32[]{:S(2)}, u32[]{:S(2)}) async-start(f32[32,64,128]{2,1,0:T(8,128)} %bitcast.57), calls=%async_computation | async-start | bytes 2097152 | tf_op jit(solution)/shard_map/all_to_all | solution.py:87
  12.0 21.4 %shard_map.112 = f32[1024,128]{1,0:T(8,128)} custom-call(f32[1024,128]{1,0:T(8,128)} %bitcast.70, f32[128,128]{1,0:T(8,128)} %k_ref.1, s32[128,128]{1,0:T(8,128)} %f_ref.1), custom_call_target="tpu_custom_call" | custom-call | flops 12884901888 | bytes 1048576 | tf_op jit(solution)/shard_map/pallas_call | solution.py:57
  33.3 9.0 %all-to-all-done = f32[32,64,128]{2,1,0:T(8,128)S(1)} async-done(((f32[32,64,128]{2,1,0:T(8,128)}), f32[32,64,128]{2,1,0:T(8,128)S(1)}, u32[]{:S(2)}, u32[]{:S(2)}) %all-to-all-start) | async-done | bytes 1048608 | tf_op jit(solution)/shard_map/all_to_all | solution.py:87
  42.3 3.9 %all-to-all-start.1 = ((f32[32,32,128]{2,1,0:T(8,128)}), f32[32,32,128]{2,1,0:T(8,128)S(1)}, u32[]{:S(2)}, u32[]{:S(2)}) async-start(f32[32,32,128]{2,1,0:T(8,128)} %bitcast.58), calls=%async_computation.1 | async-start | bytes 1048576 | tf_op jit(solution)/shard_map/all_to_all | solution.py:87
  46.3 0.6 fusion.28
  49.5 15.3 %all-to-all-done.1 = f32[32,32,128]{2,1,0:T(8,128)S(1)} async-done(((f32[32,32,128]{2,1,0:T(8,128)}), f32[32,32,128]{2,1,0:T(8,128)S(1)}, u32[]{:S(2)}, u32[]{:S(2)}) %all-to-all-start.1) | async-done | bytes 524320 | tf_op jit(solution)/shard_map/all_to_all | solution.py:87
  64.9 0.1 copy.40
  65.0 0.2 maximum_maximum_fusion
  65.2 0.2 fusion.26
  65.4 0.2 constant_dynamic-slice_fusion
  65.6 0.2 pad_maximum_fusion
  65.8 1.4 %copy.42 = f32[1,2,32,16,3,128]{5,3,4,1,0,2:T(8,128)} copy(f32[1,2,32,16,3,128]{5,3,2,4,1,0:T(8,128)S(1)} %pad_maximum_fusion) | data formatting | bytes 3145728 | tf_op jit(solution)/shard_map/stack | solution.py:122
  67.2 4.7 %all-to-all-start.2 = ((f32[1,2,32,16,3,128]{5,3,4,1,0,2:T(8,128)}), f32[1,2,32,16,3,128]{5,3,4,1,0,2:T(8,128)S(1)}, u32[]{:S(2)}, u32[]{:S(2)}) async-start(f32[1,2,32,16,3,128]{5,3,4,1,0,2:T(8,128)} %copy.42), calls=%async_computation.2 | async-start | bytes 3145728 | tf_op jit(solution)/shard_map/all_to_all | solution.py:126
  71.9 1.9 %collective-permute-start.1 = (f32[128,16]{0,1:T(8,128)S(1)}, f32[128,16]{0,1:T(8,128)S(1)}, u32[]{:S(2)}, u32[]{:S(2)}) collective-permute-start(f32[128,16]{0,1:T(8,128)S(1)} %broadcast_multiply_fusion.1), channel_id=1, source_target_pairs={{0,32},{32,64},{64,96},{96,128},{128,160},{160,192},{192,224},{1,3... | collective-permute-start | bytes 24584 | tf_op jit(solution)/shard_map/ppermute | solution.py:83
  73.9 4.9 %collective-permute-start = (f32[128,32]{0,1:T(8,128)S(1)}, f32[128,32]{0,1:T(8,128)S(1)}, u32[]{:S(2)}, u32[]{:S(2)}) collective-permute-start(f32[128,32]{0,1:T(8,128)S(1)} %bitcast.68), channel_id=1, source_target_pairs={{0,32},{32,64},{64,96},{96,128},{128,160},{160,192},{192,224},{1,3... | collective-permute-start | bytes 49160 | tf_op jit(solution)/shard_map/ppermute | solution.py:83
  78.9 26.8 %collective-permute-done.1 = f32[128,16]{0,1:T(8,128)S(1)} collective-permute-done((f32[128,16]{0,1:T(8,128)S(1)}, f32[128,16]{0,1:T(8,128)S(1)}, u32[]{:S(2)}, u32[]{:S(2)}) %collective-permute-start.1) | collective-permute-done | bytes 8224 | tf_op jit(solution)/shard_map/ppermute | solution.py:83
  105.6 0.2 convolution_negate_fusion
  105.8 0.1 copy.46
  106.0 0.2 fusion.2
  106.2 0.2 fusion.4
  106.4 0.3 copy.45
  106.8 6.0 %all-to-all-done.2 = f32[1,2,32,16,3,128]{5,3,4,1,0,2:T(8,128)S(1)} async-done(((f32[1,2,32,16,3,128]{5,3,4,1,0,2:T(8,128)}), f32[1,2,32,16,3,128]{5,3,4,1,0,2:T(8,128)S(1)}, u32[]{:S(2)}, u32[]{:S(2)}) %all-to-all-start.2) | async-done | bytes 1572896 | tf_op jit(solution)/shard_map/all_to_all | solution.py:126
  112.8 0.1 slice.39
  112.9 2.8 %fusion.27 = (f32[64,16,2,128]{3,2,1,0:T(2,128)S(1)}, f32[64,16,2]{2,1,0:T(8,128)S(1)}) fusion(f32[64,16,2,128]{3,1,2,0:T(8,128)S(1)} %slice.39, f32[64,16,128]{2,1,0:T(8,128)S(1)} %fusion.2, f32[64,16,2]{2,1,0:T(8,128)S(1)} %copy.45, f32[64,16,128]{2,1,0:T(8,128)S(1)} %slice_bitcast_fusion), kind=kLoop, calls=%fused_computation.45 | loop fusion | flops 1570816 | bytes 3162112
  115.8 0.3 copy.47
  116.0 0.3 copy.48
  116.4 1.9 %collective-permute-start.2 = (f32[64,33]{0,1:T(8,128)S(1)}, f32[64,33]{0,1:T(8,128)S(1)}, u32[]{:S(2)}, u32[]{:S(2)}) collective-permute-start(f32[64,33]{0,1:T(8,128)S(1)} %pad_maximum_fusion.1), channel_id=1, source_target_pairs={{32,0},{64,32},{96,64},{128,96},{160,128},{192,160},{224,192},{33,... | collective-permute-start | bytes 25352 | tf_op jit(solution)/shard_map/ppermute | solution.py:83
  118.3 2.4 %multiply_add_fusion = f32[64,16,2,128]{3,2,1,0:T(2,128)} fusion(f32[64,16,2,128]{3,2,1,0:T(2,128)S(1)} %get-tuple-element.15, f32[64,16,128]{2,1,0:T(8,128)S(1)} %fusion.2, f32[64,16,2]{2,1,0:T(8,128)S(1)} %copy.48), kind=kLoop, calls=%fused_computation.7 | loop fusion | flops 786432 | bytes 2629632 | tf_op jit(solution)/shard_map/add | solution.py:150
  120.7 0.2 fusion.14
  121.0 1.1 collective-permute-done.2
  122.1 0.2 convolution_add_fusion
  122.3 0.6 divide_subtract_fusion
  (29 shorter events, 0.4 us)
Async XLA Ops:
  0.6 41.7 %all-to-all-start = ((f32[32,64,128]{2,1,0:T(8,128)}), f32[32,64,128]{2,1,0:T(8,128)S(1)}, u32[]{:S(2)}, u32[]{:S(2)}) async-start(f32[32,64,128]{2,1,0:T(8,128)} %bitcast.57), calls=%async_computation | async-start | bytes 2097152 | tf_op jit(solution)/shard_map/all_to_all | solution.py:87
  12.0 34.3 %copy-start.5 = (s32[64]{0:T(128)S(1)}, s32[64]{0:T(128)}, u32[]{:S(2)}) copy-start(s32[64]{0:T(128)} %param.15) | copy-start | bytes 772
  42.3 22.5 %all-to-all-start.1 = ((f32[32,32,128]{2,1,0:T(8,128)}), f32[32,32,128]{2,1,0:T(8,128)S(1)}, u32[]{:S(2)}, u32[]{:S(2)}) async-start(f32[32,32,128]{2,1,0:T(8,128)} %bitcast.58), calls=%async_computation.1 | async-start | bytes 1048576 | tf_op jit(solution)/shard_map/all_to_all | solution.py:87
  67.1 4.7 %copy-start.2 = (f32[128,64]{0,1:T(8,128)S(1)}, f32[128,64]{0,1:T(8,128)}, u32[]{:S(2)}) copy-start(f32[128,64]{0,1:T(8,128)} %param.11) | copy-start | bytes 98308
  67.1 6.7 %copy-start.1 = (f32[128,2,64]{0,2,1:T(8,128)S(1)}, f32[128,2,64]{0,2,1:T(8,128)}, u32[]{:S(2)}) copy-start(f32[128,2,64]{0,2,1:T(8,128)} %param.12) | copy-start | bytes 196612
  67.1 11.7 %copy-start.4 = (s32[64]{0:T(128)S(1)}, s32[64]{0:T(128)}, u32[]{:S(2)}) copy-start(s32[64]{0:T(128)} %param.17) | copy-start | bytes 772
  67.2 38.8 %copy-start.3 = (f32[128]{0:T(128)S(1)}, f32[128]{0:T(128)}, u32[]{:S(2)}) copy-start(f32[128]{0:T(128)} %param.14) | copy-start | bytes 1540
  67.2 45.6 %all-to-all-start.2 = ((f32[1,2,32,16,3,128]{5,3,4,1,0,2:T(8,128)}), f32[1,2,32,16,3,128]{5,3,4,1,0,2:T(8,128)S(1)}, u32[]{:S(2)}, u32[]{:S(2)}) async-start(f32[1,2,32,16,3,128]{5,3,4,1,0,2:T(8,128)} %copy.42), calls=%async_computation.2 | async-start | bytes 3145728 | tf_op jit(solution)/shard_map/all_to_all | solution.py:126
  71.9 33.8 %collective-permute-start.1 = (f32[128,16]{0,1:T(8,128)S(1)}, f32[128,16]{0,1:T(8,128)S(1)}, u32[]{:S(2)}, u32[]{:S(2)}) collective-permute-start(f32[128,16]{0,1:T(8,128)S(1)} %broadcast_multiply_fusion.1), channel_id=1, source_target_pairs={{0,32},{32,64},{64,96},{96,128},{128,160},{160,192},{192,224},{1,3... | collective-permute-start | bytes 24584 | tf_op jit(solution)/shard_map/ppermute | solution.py:83
  73.9 32.3 %collective-permute-start = (f32[128,32]{0,1:T(8,128)S(1)}, f32[128,32]{0,1:T(8,128)S(1)}, u32[]{:S(2)}, u32[]{:S(2)}) collective-permute-start(f32[128,32]{0,1:T(8,128)S(1)} %bitcast.68), channel_id=1, source_target_pairs={{0,32},{32,64},{64,96},{96,128},{128,160},{160,192},{192,224},{1,3... | collective-permute-start | bytes 49160 | tf_op jit(solution)/shard_map/ppermute | solution.py:83
  112.8 3.0 %copy-start = (f32[64,16,128]{2,1,0:T(8,128)}, f32[64,16,128]{2,1,0:T(8,128)S(1)}, u32[]{:S(2)}) copy-start(f32[64,16,128]{2,1,0:T(8,128)S(1)} %slice_bitcast_fusion) | copy-start | bytes 1572868
  116.4 5.7 %collective-permute-start.2 = (f32[64,33]{0,1:T(8,128)S(1)}, f32[64,33]{0,1:T(8,128)S(1)}, u32[]{:S(2)}, u32[]{:S(2)}) collective-permute-start(f32[64,33]{0,1:T(8,128)S(1)} %pad_maximum_fusion.1), channel_id=1, source_target_pairs={{32,0},{64,32},{96,64},{128,96},{160,128},{192,160},{224,192},{33,... | collective-permute-start | bytes 25352 | tf_op jit(solution)/shard_map/ppermute | solution.py:83

commit v15 on v13

--- a/solution.py
+++ b/solution.py
@@ -144,6 +144,9 @@
     momentum = jnp.sum(coag_density[:, :, None, :] * (velocity_out - moved_velocity), axis=3) / bins
     by_axis = jnp.transpose(momentum, (0, 2, 1)).reshape(cycles, 2 * cells)
     message = jnp.concatenate([by_axis, gas_map.astype(F32)[:, None]], axis=1)
+    message, state, u_dust, frac = lax.optimization_barrier((message, state, u_dust, frac))
+    moved_velocity = state[:, :, 1:, :]
+    velocity_out = moved_velocity + (u_dust[:, :, :, None] - moved_velocity) * frac[:, :, None, :]
     arrived = shifted(message, "rad", -1)
     own_rows = near_rows[gas_cycles:]
 

time: 124 us -> 127 us (1.024)
  other arithmetic: 4.53 us -> 8.15 us
  waiting for transfers between devices: 60.6 us -> 57.1 us
  local copies, waits for them, and re-layouts: 3.43 us -> 5.95 us
    add x0 -> x1, other arithmetic: none -> 4.02 us  [body(): moved_velocity + (u_dust[:, :, :, None] - moved_velocity) * frac[:, :, No...]
    ppermute x3, waiting for transfers between devices: 30.3 us -> 26.8 us  [shifted(): return lax.ppermute(block, axis, route)]
    optimization_barrier x0 -> x2, local copies, waits for them, and re-layouts: none -> 2.52 us  [body(): lax.optimization_barrier((message, state, u_dust, frac))]
  transfers between devices with their start and end apart: 6 -> 6, of which waited for: 5 -> 4; matrix products, arithmetic and copies ran while one was open for 2% -> 5% of each run, Pallas kernels for 17% -> 17%
where the time goes in v15:
time: 127 us; the launch traced here: 126 us
  waiting for transfers between devices  57.1 us (45%)
  starting transfers between devices  28.7 us (23%)
  Pallas kernels  21.4 us (17%)
  other arithmetic  8.15 us (6%)
  local copies, waits for them, and re-layouts  5.95 us (5%)
  between operations  3.57 us (3%)
    ppermute x3, waiting for transfers between devices, shifted(): return lax.ppermute(block, axis, route)  26.8 us
    all_to_all x2, waiting for transfers between devices, sent(): lax.all_to_all(block.reshape(-1, block.shape[-1]), 'az', 0, 0, tiled=True)  24.3 us
    pallas_call x1, Pallas kernels, coag(): pl.pallas_call(functools.partial(coag_kernel, group=group), grid=(1,), in...  21.4 us
    all_to_all x2, starting transfers between devices, sent(): lax.all_to_all(block.reshape(-1, block.shape[-1]), 'az', 0, 0, tiled=True)  15.2 us
    ppermute x3, starting transfers between devices, shifted(): return lax.ppermute(block, axis, route)  8.78 us
    all_to_all x1, waiting for transfers between devices, body(): lax.all_to_all(blocks, 'az', 1, 0, tiled=False)  5.98 us
    all_to_all x1, starting transfers between devices, body(): lax.all_to_all(blocks, 'az', 1, 0, tiled=False)  4.66 us
    add x1, other arithmetic, body(): moved_velocity + (u_dust[:, :, :, None] - moved_velocity) * frac[:, :, No...  4.02 us
  transfers between devices with their start and end apart: 6, of which 4 were waited for; matrix products, arithmetic and copies ran while one was open for 5% of the time, Pallas kernels for 17%

profile of v15, /device:TPU:8, one launch (start us, length us, event | category | flops | bytes accessed | tf_op | source)
XLA Modules:
  0.0 125.7 jit_solution(14829675869417233471)
XLA Ops:
  0.6 11.3 %all-to-all-start = ((f32[32,64,128]{2,1,0:T(8,128)}), f32[32,64,128]{2,1,0:T(8,128)S(1)}, u32[]{:S(2)}, u32[]{:S(2)}) async-start(f32[32,64,128]{2,1,0:T(8,128)} %bitcast.58), calls=%async_computation | async-start | bytes 2097152 | tf_op jit(solution)/shard_map/all_to_all | solution.py:87
  12.0 21.4 %shard_map.112 = f32[1024,128]{1,0:T(8,128)} custom-call(f32[1024,128]{1,0:T(8,128)} %bitcast.71, f32[128,128]{1,0:T(8,128)} %k_ref.1, s32[128,128]{1,0:T(8,128)} %f_ref.1), custom_call_target="tpu_custom_call" | custom-call | flops 12884901888 | bytes 1048576 | tf_op jit(solution)/shard_map/pallas_call | solution.py:57
  33.3 9.0 %all-to-all-done = f32[32,64,128]{2,1,0:T(8,128)S(1)} async-done(((f32[32,64,128]{2,1,0:T(8,128)}), f32[32,64,128]{2,1,0:T(8,128)S(1)}, u32[]{:S(2)}, u32[]{:S(2)}) %all-to-all-start) | async-done | bytes 1048608 | tf_op jit(solution)/shard_map/all_to_all | solution.py:87
  42.3 3.9 %all-to-all-start.1 = ((f32[32,32,128]{2,1,0:T(8,128)}), f32[32,32,128]{2,1,0:T(8,128)S(1)}, u32[]{:S(2)}, u32[]{:S(2)}) async-start(f32[32,32,128]{2,1,0:T(8,128)} %bitcast.59), calls=%async_computation.1 | async-start | bytes 1048576 | tf_op jit(solution)/shard_map/all_to_all | solution.py:87
  46.3 0.6 fusion.27
  49.5 15.3 %all-to-all-done.1 = f32[32,32,128]{2,1,0:T(8,128)S(1)} async-done(((f32[32,32,128]{2,1,0:T(8,128)}), f32[32,32,128]{2,1,0:T(8,128)S(1)}, u32[]{:S(2)}, u32[]{:S(2)}) %all-to-all-start.1) | async-done | bytes 524320 | tf_op jit(solution)/shard_map/all_to_all | solution.py:87
  64.9 0.1 copy.42
  65.0 0.2 maximum_maximum_fusion
  65.2 0.2 fusion.26
  65.4 0.1 constant_dynamic-slice_fusion
  65.6 0.2 pad_maximum_fusion
  65.8 1.4 %copy.44 = f32[1,2,32,16,3,128]{5,3,4,1,0,2:T(8,128)} copy(f32[1,2,32,16,3,128]{5,3,2,4,1,0:T(8,128)S(1)} %pad_maximum_fusion) | data formatting | bytes 3145728 | tf_op jit(solution)/shard_map/stack | solution.py:122
  67.1 4.7 %all-to-all-start.2 = ((f32[1,2,32,16,3,128]{5,3,4,1,0,2:T(8,128)}), f32[1,2,32,16,3,128]{5,3,4,1,0,2:T(8,128)S(1)}, u32[]{:S(2)}, u32[]{:S(2)}) async-start(f32[1,2,32,16,3,128]{5,3,4,1,0,2:T(8,128)} %copy.44), calls=%async_computation.2 | async-start | bytes 3145728 | tf_op jit(solution)/shard_map/all_to_all | solution.py:126
  71.9 2.0 %collective-permute-start.1 = (f32[128,16]{0,1:T(8,128)S(1)}, f32[128,16]{0,1:T(8,128)S(1)}, u32[]{:S(2)}, u32[]{:S(2)}) collective-permute-start(f32[128,16]{0,1:T(8,128)S(1)} %broadcast_multiply_fusion.1), channel_id=1, source_target_pairs={{0,32},{32,64},{64,96},{96,128},{128,160},{160,192},{192,224},{1,3... | collective-permute-start | bytes 24584 | tf_op jit(solution)/shard_map/ppermute | solution.py:83
  73.9 4.9 %collective-permute-start = (f32[128,32]{0,1:T(8,128)S(1)}, f32[128,32]{0,1:T(8,128)S(1)}, u32[]{:S(2)}, u32[]{:S(2)}) collective-permute-start(f32[128,32]{0,1:T(8,128)S(1)} %bitcast.69), channel_id=1, source_target_pairs={{0,32},{32,64},{64,96},{96,128},{128,160},{160,192},{192,224},{1,3... | collective-permute-start | bytes 49160 | tf_op jit(solution)/shard_map/ppermute | solution.py:83
  78.9 26.8 %collective-permute-done.1 = f32[128,16]{0,1:T(8,128)S(1)} collective-permute-done((f32[128,16]{0,1:T(8,128)S(1)}, f32[128,16]{0,1:T(8,128)S(1)}, u32[]{:S(2)}, u32[]{:S(2)}) %collective-permute-start.1) | collective-permute-done | bytes 8224 | tf_op jit(solution)/shard_map/ppermute | solution.py:83
  105.6 0.2 convolution_negate_fusion
  105.8 0.1 copy.48
  105.9 0.2 fusion.2
  106.2 0.2 fusion.4
  106.4 0.3 copy.47
  106.7 6.0 %all-to-all-done.2 = f32[1,2,32,16,3,128]{5,3,4,1,0,2:T(8,128)S(1)} async-done(((f32[1,2,32,16,3,128]{5,3,4,1,0,2:T(8,128)}), f32[1,2,32,16,3,128]{5,3,4,1,0,2:T(8,128)S(1)}, u32[]{:S(2)}, u32[]{:S(2)}) %all-to-all-start.2) | async-done | bytes 1572896 | tf_op jit(solution)/shard_map/all_to_all | solution.py:126
  112.8 0.1 slice.43
  112.9 2.8 %fusion.1 = f32[64,16,2]{2,1,0:T(8,128)S(1)} fusion(f32[64,16,2,128]{3,1,2,0:T(8,128)S(1)} %slice.43, f32[64,16,128]{2,1,0:T(8,128)S(1)} %fusion.2, f32[64,16,2]{2,1,0:T(8,128)S(1)} %copy.47, f32[64,16,128]{2,1,0:T(8,128)S(1)} %slice_bitcast_fusion), kind=kLoop, calls=%fused_computation.6 | loop fusion | flops 1570816 | bytes 2113536 | tf_op jit(solution)/shard_map/reduce_sum | solution.py:144
  115.7 0.3 copy.49
  116.0 2.2 %copy.50 = f32[64,16,3,128]{3,2,1,0:T(4,128)} copy(f32[64,16,3,128]{3,1,2,0:T(8,128)S(1)} %bitcast.51) | data formatting | bytes 3145728 | tf_op jit(solution)/shard_map/optimization_barrier | solution.py:147
  118.2 0.3 copy.51
  118.5 1.9 %collective-permute-start.2 = (f32[64,33]{0,1:T(8,128)S(1)}, f32[64,33]{0,1:T(8,128)S(1)}, u32[]{:S(2)}, u32[]{:S(2)}) collective-permute-start(f32[64,33]{0,1:T(8,128)S(1)} %pad_maximum_fusion.1), channel_id=1, source_target_pairs={{32,0},{64,32},{96,64},{128,96},{160,128},{192,160},{224,192},{33,... | collective-permute-start | bytes 25352 | tf_op jit(solution)/shard_map/ppermute | solution.py:83
  120.5 4.0 %multiply_add_fusion = f32[64,16,2,128]{3,2,1,0:T(2,128)} fusion(f32[64,16,3,128]{3,2,1,0:T(4,128)} %copy.50, f32[64,16,128]{2,1,0:T(8,128)S(1)} %fusion.2, f32[64,16,2]{2,1,0:T(8,128)S(1)} %copy.51), kind=kLoop, calls=%fused_computation.7 | loop fusion | flops 786432 | bytes 2629632 | tf_op jit(solution)/shard_map/add | solution.py:149
  124.5 0.2 fusion.14
  124.8 0.2 convolution_add_fusion
  125.0 0.6 divide_subtract_fusion
  (30 shorter events, 0.4 us)
Async XLA Ops:
  0.6 41.7 %all-to-all-start = ((f32[32,64,128]{2,1,0:T(8,128)}), f32[32,64,128]{2,1,0:T(8,128)S(1)}, u32[]{:S(2)}, u32[]{:S(2)}) async-start(f32[32,64,128]{2,1,0:T(8,128)} %bitcast.58), calls=%async_computation | async-start | bytes 2097152 | tf_op jit(solution)/shard_map/all_to_all | solution.py:87
  12.0 34.3 %copy-start.5 = (s32[64]{0:T(128)S(1)}, s32[64]{0:T(128)}, u32[]{:S(2)}) copy-start(s32[64]{0:T(128)} %param.15) | copy-start | bytes 772
  42.3 22.5 %all-to-all-start.1 = ((f32[32,32,128]{2,1,0:T(8,128)}), f32[32,32,128]{2,1,0:T(8,128)S(1)}, u32[]{:S(2)}, u32[]{:S(2)}) async-start(f32[32,32,128]{2,1,0:T(8,128)} %bitcast.59), calls=%async_computation.1 | async-start | bytes 1048576 | tf_op jit(solution)/shard_map/all_to_all | solution.py:87
  67.1 4.7 %copy-start.2 = (f32[128,64]{0,1:T(8,128)S(1)}, f32[128,64]{0,1:T(8,128)}, u32[]{:S(2)}) copy-start(f32[128,64]{0,1:T(8,128)} %param.11) | copy-start | bytes 98308
  67.1 6.7 %copy-start.1 = (f32[128,2,64]{0,2,1:T(8,128)S(1)}, f32[128,2,64]{0,2,1:T(8,128)}, u32[]{:S(2)}) copy-start(f32[128,2,64]{0,2,1:T(8,128)} %param.12) | copy-start | bytes 196612
  67.1 11.7 %copy-start.4 = (s32[64]{0:T(128)S(1)}, s32[64]{0:T(128)}, u32[]{:S(2)}) copy-start(s32[64]{0:T(128)} %param.17) | copy-start | bytes 772
  67.1 38.8 %copy-start.3 = (f32[128]{0:T(128)S(1)}, f32[128]{0:T(128)}, u32[]{:S(2)}) copy-start(f32[128]{0:T(128)} %param.14) | copy-start | bytes 1540
  67.1 45.6 %all-to-all-start.2 = ((f32[1,2,32,16,3,128]{5,3,4,1,0,2:T(8,128)}), f32[1,2,32,16,3,128]{5,3,4,1,0,2:T(8,128)S(1)}, u32[]{:S(2)}, u32[]{:S(2)}) async-start(f32[1,2,32,16,3,128]{5,3,4,1,0,2:T(8,128)} %copy.44), calls=%async_computation.2 | async-start | bytes 3145728 | tf_op jit(solution)/shard_map/all_to_all | solution.py:126
  71.9 33.8 %collective-permute-start.1 = (f32[128,16]{0,1:T(8,128)S(1)}, f32[128,16]{0,1:T(8,128)S(1)}, u32[]{:S(2)}, u32[]{:S(2)}) collective-permute-start(f32[128,16]{0,1:T(8,128)S(1)} %broadcast_multiply_fusion.1), channel_id=1, source_target_pairs={{0,32},{32,64},{64,96},{96,128},{128,160},{160,192},{192,224},{1,3... | collective-permute-start | bytes 24584 | tf_op jit(solution)/shard_map/ppermute | solution.py:83
  73.9 32.3 %collective-permute-start = (f32[128,32]{0,1:T(8,128)S(1)}, f32[128,32]{0,1:T(8,128)S(1)}, u32[]{:S(2)}, u32[]{:S(2)}) collective-permute-start(f32[128,32]{0,1:T(8,128)S(1)} %bitcast.69), channel_id=1, source_target_pairs={{0,32},{32,64},{64,96},{96,128},{128,160},{160,192},{192,224},{1,3... | collective-permute-start | bytes 49160 | tf_op jit(solution)/shard_map/ppermute | solution.py:83
  112.8 2.9 %copy-start = (f32[64,16,128]{2,1,0:T(8,128)}, f32[64,16,128]{2,1,0:T(8,128)S(1)}, u32[]{:S(2)}) copy-start(f32[64,16,128]{2,1,0:T(8,128)S(1)} %slice_bitcast_fusion) | copy-start | bytes 1572868
  118.5 6.2 %collective-permute-start.2 = (f32[64,33]{0,1:T(8,128)S(1)}, f32[64,33]{0,1:T(8,128)S(1)}, u32[]{:S(2)}, u32[]{:S(2)}) collective-permute-start(f32[64,33]{0,1:T(8,128)S(1)} %pad_maximum_fusion.1), channel_id=1, source_target_pairs={{32,0},{64,32},{96,64},{128,96},{160,128},{192,160},{224,192},{33,... | collective-permute-start | bytes 25352 | tf_op jit(solution)/shard_map/ppermute | solution.py:83
